TPU v7x, 1024 devices: a whole 4x8x16 slice. The times are simulated.
1024 devices in a mesh: seq: 128 (over y, z), head: 8 (over x, core).
Axes of the slice: x: 4, y: 8, z: 16, core: 2. Of those that a mesh axis runs over, the one named last changes fastest.
Arguments:
- queries: bfloat16 [32768, 3072], P('seq', 'head'), may hold values from -8 to 8
- key_states: bfloat16 [32768, 3072], P('seq', 'head'), may hold values from -8 to 8
- value_states: bfloat16 [32768, 3072], P('seq', 'head'), may hold values from -12 to 12
- level_offsets: int32 [3, 24], P(None, 'head'), may hold values from 0 to 31
- out_weight: bfloat16 [3072, 5120], P(None, 'head'), may hold values from -0.109375 to 0.109375
Outputs:
- layer_output: bfloat16 [32768, 5120], P('seq', 'head')
All inputs are finite; a program needn't handle non-finite values.
Results may differ from a plain program's by a relative error of at most 0.0057.
Values may be sent and summed in bfloat16 or wider, within the bound.
No kernel may reach another device: no remote copies, remote signals or barrier semaphores. Data moves between devices by JAX's collectives and lax.ppermute only.
A program may use at most 32 MiB of HBM per device.

v0:
```python
import jax
import jax.numpy as jnp
from jax import lax
from jax.sharding import PartitionSpec as P

RATE_MID = 8
RATE_TOP = 32
SEG_ROWS = 1024


NEG_FILL = -1e30


def from_behind(array, axis, by):
    peers = lax.axis_size(axis)
    pairs = [(i, i + by) for i in range(peers) if 0 <= i + by < peers]
    return lax.ppermute(array, axis, pairs)


def pick_rows(states, chooser, spacing):
    row_count, head_count, head_width = states.shape
    grouped = states.reshape(row_count // spacing, spacing, head_count, head_width)
    return jnp.einsum("nrhd,rh->nhd", grouped, chooser, preferred_element_type=jnp.float32).astype(
        jnp.bfloat16
    )


def attend(query_rows, key_rows, value_rows, allowed, scale_factor):
    scores = (
        jnp.einsum("qhd,khd->hqk", query_rows, key_rows, preferred_element_type=jnp.float32)
        * scale_factor
    )
    scores = jnp.where(allowed[None], scores, NEG_FILL)
    highest = jnp.max(scores, axis=2, keepdims=True)
    weights = jnp.exp(scores - highest)
    totals = jnp.sum(weights, axis=2, keepdims=True)
    shares = (weights / totals).astype(jnp.bfloat16)
    result = jnp.einsum("hqk,khd->qhd", shares, value_rows, preferred_element_type=jnp.float32)
    return (result, (highest + jnp.log(totals))[:, :, 0].T)


def lower_segment(pair_rows, span_devices):
    holding = pair_rows
    for bit_no in range(span_devices.bit_length() - 1):
        arrived = from_behind(holding, "seq", 2**bit_no)
        holding = jnp.concatenate([arrived, holding], axis=0)
    return holding


def segment_mask(sparse_count, span_devices, position):
    shape_pair = (sparse_count, span_devices * sparse_count)
    query_index = lax.broadcasted_iota(jnp.int32, shape_pair, 0)
    key_index = lax.broadcasted_iota(jnp.int32, shape_pair, 1)
    lowest = (span_devices - 1 - position) * sparse_count
    return (key_index >= lowest) & (key_index <= (span_devices - 1) * sparse_count + query_index)


def spread_back(level_out, level_lse, chooser):
    picked = chooser.astype(jnp.float32)
    sparse_count, head_count, head_width = level_out.shape
    row_count = sparse_count * chooser.shape[0]
    full_out = (level_out[:, None, :, :] * picked[None, :, :, None]).reshape(
        row_count, head_count, head_width
    )
    full_lse = jnp.where(chooser[None], level_lse[:, None, :], NEG_FILL).reshape(
        row_count, head_count
    )
    return (full_out, full_lse)


def level_setup(query_all, key_all, value_all, offset_row, spacing):
    head_count = query_all.shape[1]
    chooser = (
        lax.broadcasted_iota(jnp.int32, (spacing, head_count), 0) == (offset_row % spacing)[None, :]
    )
    chooser_bf = chooser.astype(jnp.bfloat16)
    query_rows = pick_rows(query_all, chooser_bf, spacing)
    pair_rows = jnp.stack(
        [pick_rows(key_all, chooser_bf, spacing), pick_rows(value_all, chooser_bf, spacing)], axis=1
    )
    return (chooser, query_rows, pair_rows)


def local(queries, key_states, value_states, level_offsets, out_weight):
    row_count = queries.shape[0]
    head_count = level_offsets.shape[1]
    head_width = queries.shape[1] // head_count
    scale_factor = head_width ** (-0.5)
    seq_count = lax.axis_size("seq")
    seq_index = lax.axis_index("seq")
    query_all = queries.reshape(row_count, head_count, head_width)
    key_all = key_states.reshape(row_count, head_count, head_width)
    value_all = value_states.reshape(row_count, head_count, head_width)
    full_outs = []
    full_lses = []
    for level_no, spacing in enumerate((1, RATE_MID)):
        span_devices = min(SEG_ROWS * spacing // row_count, seq_count)
        sparse_count = row_count // spacing
        chooser, query_rows, pair_rows = level_setup(
            query_all, key_all, value_all, level_offsets[level_no], spacing
        )
        buffer = lower_segment(pair_rows, span_devices)
        allowed = segment_mask(sparse_count, span_devices, seq_index % span_devices)
        level_out, level_lse = attend(query_rows, buffer[:, 0], buffer[:, 1], allowed, scale_factor)
        full_out, full_lse = spread_back(level_out, level_lse, chooser)
        full_outs.append(full_out)
        full_lses.append(full_lse)
    spacing = RATE_TOP
    span_devices = min(SEG_ROWS * spacing // row_count, seq_count)
    sparse_count = row_count // spacing
    chooser, query_rows, pair_rows = level_setup(
        query_all, key_all, value_all, level_offsets[2], spacing
    )
    shard_rows = lax.all_gather(pair_rows, "seq", axis=0, tiled=True)
    running_max = jnp.full((head_count, sparse_count), NEG_FILL, jnp.float32)
    piece_rows = shard_rows.shape[0]
    shape_pair = (sparse_count, piece_rows)
    key_global = lax.broadcasted_iota(jnp.int32, shape_pair, 1)
    query_global = seq_index * sparse_count + lax.broadcasted_iota(jnp.int32, shape_pair, 0)
    same_segment = key_global // (span_devices * sparse_count) == seq_index // span_devices
    allowed = same_segment & (key_global <= query_global)
    scores = (
        jnp.einsum("qhd,khd->hqk", query_rows, shard_rows[:, 0], preferred_element_type=jnp.float32)
        * scale_factor
    )
    scores = jnp.where(allowed[None], scores, NEG_FILL)
    new_max = jnp.maximum(running_max, jnp.max(scores, axis=2))
    weights = jnp.where(allowed[None], jnp.exp(scores - new_max[:, :, None]), 0.0)
    running_sum = jnp.sum(weights, axis=2)
    added = jnp.einsum(
        "hqk,khd->hqd",
        weights.astype(jnp.bfloat16),
        shard_rows[:, 1],
        preferred_element_type=jnp.float32,
    )
    running_out = added
    running_max, running_sum, running_out = (new_max, running_sum, running_out)
    level_out = (running_out / running_sum[:, :, None]).transpose(1, 0, 2)
    level_lse = (running_max + jnp.log(running_sum)).T
    full_out, full_lse = spread_back(level_out, level_lse, chooser)
    full_outs.append(full_out)
    full_lses.append(full_lse)
    lse_stack = jnp.stack(full_lses)
    level_top = jnp.max(lse_stack, axis=0)
    level_weights = jnp.exp(lse_stack - level_top[None])
    mixed_heads = (
        jnp.sum(level_weights[..., None] * jnp.stack(full_outs), axis=0)
        / jnp.sum(level_weights, axis=0)[..., None]
    )
    heads_out = mixed_heads.astype(jnp.bfloat16).reshape(row_count, head_count * head_width)
    projected = jnp.dot(
        lax.all_gather(heads_out, "head", axis=1, tiled=True),
        out_weight,
        preferred_element_type=jnp.float32,
    )
    return projected.astype(jnp.bfloat16)


def solution(mesh):
    return jax.shard_map(
        local,
        mesh=mesh,
        in_specs=(
            P("seq", "head"),
            P("seq", "head"),
            P("seq", "head"),
            P(None, "head"),
            P(None, "head"),
        ),
        out_specs=P("seq", "head"),
        check_vma=False,
    )
```

profile of v0, /device:TPU:1, one launch (start us, length us, event | category | flops | bytes accessed | tf_op | source)
XLA Modules:
  0.0 265.3 jit_solution(3901600487925894381)
XLA Ops:
  6.5 1.1 reshape_reshape.26
  7.6 0.8 fusion.49
  8.4 1.0 reshape_reshape.25
  9.4 0.1 fusion.11
  9.6 0.1 fusion.13
  9.7 0.6 pad_maximum_fusion.2
  10.5 1.1 fusion.17
  11.6 0.2 fusion.19
  11.8 4.8 %collective-permute-start.2 = (bf16[32,2,3,128]{3,0,2,1:T(8,128)(2,1)S(1)}, bf16[32,2,3,128]{3,0,2,1:T(8,128)(2,1)S(1)}, u32[]{:S(2)}, u32[]{:S(2)}) collective-permute-start(bf16[32,2,3,128]{3,0,2,1:T(8,128)(2,1)S(1)} %pad_maximum_fusion.1), channel_id=1, source_target_pairs={{0,8},{8,16},{16,24},{24,32},{32,40},{40,48},{48,56},{56,64},{64,7... | collective-permute-start | bytes 147464 | tf_op jit(solution)/shard_map/ppermute | solution.py:17
  16.7 0.1 copy.12
  16.8 0.1 copy.11
  17.0 0.2 copy.14
  17.1 0.2 copy.13
  17.4 4.0 %collective-permute-start = (bf16[256,2,3,128]{3,0,2,1:T(8,128)(2,1)S(1)}, bf16[256,2,3,128]{3,0,2,1:T(8,128)(2,1)S(1)}, u32[]{:S(2)}, u32[]{:S(2)}) collective-permute-start(bf16[256,2,3,128]{3,0,2,1:T(8,128)(2,1)S(1)} %pad_maximum_fusion), channel_id=1, source_target_pairs={{0,8},{8,16},{16,24},{24,32},{32,40},{40,48},{48,56},{56,64},{64,7... | collective-permute-start | bytes 1179656 | tf_op jit(solution)/shard_map/ppermute | solution.py:17
  21.5 0.2 fusion.21
  21.7 0.1 fusion.15
  21.9 0.2 fusion.8
  22.1 7.0 %collective-permute-start.3 = (bf16[64,2,3,128]{3,0,2,1:T(8,128)(2,1)S(1)}, bf16[64,2,3,128]{3,0,2,1:T(8,128)(2,1)S(1)}, u32[]{:S(2)}, u32[]{:S(2)}) collective-permute-start(bf16[64,2,3,128]{3,0,2,1:T(8,128)(2,1)S(1)} %maximum_maximum_fusion.4), channel_id=1, source_target_pairs={{0,16},{8,24},{16,32},{24,40},{32,48},{40,56},{48,64},{56,72},{64,... | collective-permute-start | bytes 294920 | tf_op jit(solution)/shard_map/ppermute | solution.py:17
  29.1 0.1 fusion.25
  29.2 2.2 collective-permute-done.3
  31.4 12.4 %collective-permute-start.4 = (bf16[128,2,3,128]{3,0,2,1:T(8,128)(2,1)S(1)}, bf16[128,2,3,128]{3,0,2,1:T(8,128)(2,1)S(1)}, u32[]{:S(2)}, u32[]{:S(2)}) collective-permute-start(bf16[128,2,3,128]{3,0,2,1:T(8,128)(2,1)S(1)} %maximum_maximum_fusion.3), channel_id=1, source_target_pairs={{0,32},{8,40},{16,48},{24,56},{32,64},{40,72},{48,80},{56,88},{64,... | collective-permute-start | bytes 589832 | tf_op jit(solution)/shard_map/ppermute | solution.py:17
  43.8 3.2 %collective-permute-done.4 = bf16[128,2,3,128]{3,0,2,1:T(8,128)(2,1)S(1)} collective-permute-done((bf16[128,2,3,128]{3,0,2,1:T(8,128)(2,1)S(1)}, bf16[128,2,3,128]{3,0,2,1:T(8,128)(2,1)S(1)}, u32[]{:S(2)}, u32[]{:S(2)}) %collective-permute-start.4) | collective-permute-done | bytes 196640 | tf_op jit(solution)/shard_map/ppermute | solution.py:17
  47.1 29.2 %collective-permute-start.5 = (bf16[256,2,3,128]{3,0,2,1:T(8,128)(2,1)S(1)}, bf16[256,2,3,128]{3,0,2,1:T(8,128)(2,1)S(1)}, u32[]{:S(2)}, u32[]{:S(2)}) collective-permute-start(bf16[256,2,3,128]{3,0,2,1:T(8,128)(2,1)S(1)} %maximum_maximum_fusion.2), channel_id=1, source_target_pairs={{0,64},{8,72},{16,80},{24,88},{32,96},{40,104},{48,112},{56,120},{... | collective-permute-start | bytes 1179656 | tf_op jit(solution)/shard_map/ppermute | solution.py:17
  76.3 0.8 copy.15
  77.2 0.1 mul.109
  77.4 1.3 collective-permute-start.1
  78.8 25.8 %collective-permute-done.5 = bf16[256,2,3,128]{3,0,2,1:T(8,128)(2,1)S(1)} collective-permute-done((bf16[256,2,3,128]{3,0,2,1:T(8,128)(2,1)S(1)}, bf16[256,2,3,128]{3,0,2,1:T(8,128)(2,1)S(1)}, u32[]{:S(2)}, u32[]{:S(2)}) %collective-permute-start.5) | collective-permute-done | bytes 393248 | tf_op jit(solution)/shard_map/ppermute | solution.py:17
  104.7 7.7 %collective-permute-start.6 = (bf16[512,2,3,128]{3,0,2,1:T(8,128)(2,1)S(1)}, bf16[512,2,3,128]{3,0,2,1:T(8,128)(2,1)S(1)}, u32[]{:S(2)}, u32[]{:S(2)}) collective-permute-start(bf16[512,2,3,128]{3,0,2,1:T(8,128)(2,1)S(1)} %constant_dynamic-update-slice_fusion), channel_id=1, source_target_pairs={{0,128},{8,136},{16,144},{24,152},{32,160},{40,168},{48,176},{56,1... | collective-permute-start | bytes 2359304 | tf_op jit(solution)/shard_map/ppermute | solution.py:17
  112.4 10.3 %collective-permute-done.1 = bf16[512,2,3,128]{3,0,2,1:T(8,128)(2,1)S(1)} collective-permute-done((bf16[512,2,3,128]{3,0,2,1:T(8,128)(2,1)S(1)}, bf16[512,2,3,128]{3,0,2,1:T(8,128)(2,1)S(1)}, u32[]{:S(2)}, u32[]{:S(2)}) %collective-permute-start.1) | collective-permute-done | bytes 786464 | tf_op jit(solution)/shard_map/ppermute | solution.py:17
  122.7 0.1 maximum_maximum_fusion
  122.9 0.7 fusion.1
  123.6 0.7 fusion
  124.3 1.2 fusion.3
  125.5 13.8 %collective-permute-done.6 = bf16[512,2,3,128]{3,0,2,1:T(8,128)(2,1)S(1)} collective-permute-done((bf16[512,2,3,128]{3,0,2,1:T(8,128)(2,1)S(1)}, bf16[512,2,3,128]{3,0,2,1:T(8,128)(2,1)S(1)}, u32[]{:S(2)}, u32[]{:S(2)}) %collective-permute-start.6) | collective-permute-done | bytes 786464 | tf_op jit(solution)/shard_map/ppermute | solution.py:17
  139.5 0.5 fusion.63
  140.0 0.2 fusion.10
  140.3 0.1 select_n.119
  140.5 0.3 convolution_bitcast_fusion
  140.8 0.2 copy.19
  141.1 67.5 %all-gather.3.cloned.1.call-done = bf16[1024,2,3,128]{3,0,2,1:T(8,128)(2,1)} async-done(((bf16[8,2,3,128]{3,0,2,1:T(8,128)(2,1)}), bf16[1024,2,3,128]{3,0,2,1:T(8,128)(2,1)}) %all-gather.3.cloned.1.call-update) | async-done | bytes 1572880 | tf_op jit(solution)/shard_map/all_gather | solution.py:114
  208.5 1.5 fusion.62
  210.1 0.2 fusion.27
  210.5 1.4 fusion.7
  212.0 0.2 copy.20
  212.2 0.1 fusion.5
  212.3 0.7 divide_convert_fusion.4
  213.0 40.7 %all-gather.5.cloned.1.call-done = bf16[256,3072]{0,1:T(8,128)(2,1)} async-done(((bf16[256,384]{0,1:T(8,128)(2,1)}), bf16[256,3072]{0,1:T(8,128)(2,1)}) %all-gather.5.cloned.1.call-update) | async-done | bytes 1572880 | tf_op jit(solution)/shard_map/all_gather | solution.py:152
  253.8 4.7 %convolution_convert_fusion = bf16[256,640]{1,0:T(8,128)(2,1)} fusion(bf16[256,3072]{0,1:T(8,128)(2,1)} %all-gather.5.cloned.1.call-done, bf16[3072,640]{1,0:T(8,128)(2,1)} %param.9), kind=kOutput, calls=%fused_computation.7 | convolution fusion | flops 1006796800 | bytes 5832704 | tf_op jit(solution)/shard_map/dot_general | solution.py:151
  (62 shorter events, 1.5 us)
Async XLA Ops:
  6.5 10.1 %copy-start = (bf16[256,384]{1,0:T(8,128)(2,1)S(1)}, bf16[256,384]{1,0:T(8,128)(2,1)}, u32[]{:S(2)}) copy-start(bf16[256,384]{1,0:T(8,128)(2,1)} %param.7) | copy-start | bytes 589828
  6.5 5.1 %copy-start.1 = (bf16[256,384]{1,0:T(8,128)(2,1)S(1)}, bf16[256,384]{1,0:T(8,128)(2,1)}, u32[]{:S(2)}) copy-start(bf16[256,384]{1,0:T(8,128)(2,1)} %param.6) | copy-start | bytes 589828
  6.5 202.0 %all-gather.3.cloned.1.call-start = ((), (), s32[]{:S(2)}) async-start(), calls=%async_computation | async-start | bytes 1585152 | tf_op jit(solution)/shard_map/all_gather | solution.py:114
  10.3 11.1 %copy-start.2 = (bf16[256,384]{1,0:T(8,128)(2,1)S(1)}, bf16[256,384]{1,0:T(8,128)(2,1)}, u32[]{:S(2)}) copy-start(bf16[256,384]{1,0:T(8,128)(2,1)} %param.5) | copy-start | bytes 589828
  10.4 243.4 %all-gather.5.cloned.1.call-start = ((), (), s32[]{:S(2)}) async-start(), calls=%async_computation.1 | async-start | bytes 1769472 | tf_op jit(solution)/shard_map/all_gather | solution.py:152
  11.8 10.3 %collective-permute-start.2 = (bf16[32,2,3,128]{3,0,2,1:T(8,128)(2,1)S(1)}, bf16[32,2,3,128]{3,0,2,1:T(8,128)(2,1)S(1)}, u32[]{:S(2)}, u32[]{:S(2)}) collective-permute-start(bf16[32,2,3,128]{3,0,2,1:T(8,128)(2,1)S(1)} %pad_maximum_fusion.1), channel_id=1, source_target_pairs={{0,8},{8,16},{16,24},{24,32},{32,40},{40,48},{48,56},{56,64},{64,7... | collective-permute-start | bytes 147464 | tf_op jit(solution)/shard_map/ppermute | solution.py:17
  17.4 60.0 %collective-permute-start = (bf16[256,2,3,128]{3,0,2,1:T(8,128)(2,1)S(1)}, bf16[256,2,3,128]{3,0,2,1:T(8,128)(2,1)S(1)}, u32[]{:S(2)}, u32[]{:S(2)}) collective-permute-start(bf16[256,2,3,128]{3,0,2,1:T(8,128)(2,1)S(1)} %pad_maximum_fusion), channel_id=1, source_target_pairs={{0,8},{8,16},{16,24},{24,32},{32,40},{40,48},{48,56},{56,64},{64,7... | collective-permute-start | bytes 1179656 | tf_op jit(solution)/shard_map/ppermute | solution.py:17
  22.1 9.3 %collective-permute-start.3 = (bf16[64,2,3,128]{3,0,2,1:T(8,128)(2,1)S(1)}, bf16[64,2,3,128]{3,0,2,1:T(8,128)(2,1)S(1)}, u32[]{:S(2)}, u32[]{:S(2)}) collective-permute-start(bf16[64,2,3,128]{3,0,2,1:T(8,128)(2,1)S(1)} %maximum_maximum_fusion.4), channel_id=1, source_target_pairs={{0,16},{8,24},{16,32},{24,40},{32,48},{40,56},{48,64},{56,72},{64,... | collective-permute-start | bytes 294920 | tf_op jit(solution)/shard_map/ppermute | solution.py:17
  31.4 15.7 %collective-permute-start.4 = (bf16[128,2,3,128]{3,0,2,1:T(8,128)(2,1)S(1)}, bf16[128,2,3,128]{3,0,2,1:T(8,128)(2,1)S(1)}, u32[]{:S(2)}, u32[]{:S(2)}) collective-permute-start(bf16[128,2,3,128]{3,0,2,1:T(8,128)(2,1)S(1)} %maximum_maximum_fusion.3), channel_id=1, source_target_pairs={{0,32},{8,40},{16,48},{24,56},{32,64},{40,72},{48,80},{56,88},{64,... | collective-permute-start | bytes 589832 | tf_op jit(solution)/shard_map/ppermute | solution.py:17
  47.1 57.5 %collective-permute-start.5 = (bf16[256,2,3,128]{3,0,2,1:T(8,128)(2,1)S(1)}, bf16[256,2,3,128]{3,0,2,1:T(8,128)(2,1)S(1)}, u32[]{:S(2)}, u32[]{:S(2)}) collective-permute-start(bf16[256,2,3,128]{3,0,2,1:T(8,128)(2,1)S(1)} %maximum_maximum_fusion.2), channel_id=1, source_target_pairs={{0,64},{8,72},{16,80},{24,88},{32,96},{40,104},{48,112},{56,120},{... | collective-permute-start | bytes 1179656 | tf_op jit(solution)/shard_map/ppermute | solution.py:17
  77.4 45.3 %collective-permute-start.1 = (bf16[512,2,3,128]{3,0,2,1:T(8,128)(2,1)S(1)}, bf16[512,2,3,128]{3,0,2,1:T(8,128)(2,1)S(1)}, u32[]{:S(2)}, u32[]{:S(2)}) collective-permute-start(bf16[512,2,3,128]{3,0,2,1:T(8,128)(2,1)S(1)} %maximum_maximum_fusion.1), channel_id=1, source_target_pairs={{0,16},{8,24},{16,32},{24,40},{32,48},{40,56},{48,64},{56,72},{64,... | collective-permute-start | bytes 2359304 | tf_op jit(solution)/shard_map/ppermute | solution.py:17
  104.7 18.1 %copy-start.3 = (bf16[256,384]{0,1:T(8,128)(2,1)S(1)}, bf16[256,384]{0,1:T(8,128)(2,1)}, u32[]{:S(2)}) copy-start(bf16[256,384]{0,1:T(8,128)(2,1)} %copy.15) | copy-start | bytes 589828
  104.7 34.6 %collective-permute-start.6 = (bf16[512,2,3,128]{3,0,2,1:T(8,128)(2,1)S(1)}, bf16[512,2,3,128]{3,0,2,1:T(8,128)(2,1)S(1)}, u32[]{:S(2)}, u32[]{:S(2)}) collective-permute-start(bf16[512,2,3,128]{3,0,2,1:T(8,128)(2,1)S(1)} %constant_dynamic-update-slice_fusion), channel_id=1, source_target_pairs={{0,128},{8,136},{16,144},{24,152},{32,160},{40,168},{48,176},{56,1... | collective-permute-start | bytes 2359304 | tf_op jit(solution)/shard_map/ppermute | solution.py:17
Sparse Core Ops, SparseCore 0:
  11.4 197.0 all-gather.2
  213.2 40.5 all-gather.4
where the time goes:
time: 266 us; the launch traced here: 265 us
  waiting for transfers between devices  164 us (62%)
  starting transfers between devices  66.5 us (25%)
  between operations  13.9 us (5%)
  matrix products  12.2 us (5%)
  local copies, waits for them, and re-layouts  4.73 us (2%)
  other arithmetic  4.45 us (2%)
    all_gather x1, waiting for transfers between devices, local(): shard_rows = lax.all_gather(pair_rows, 'seq', axis=0, tiled=True)  67.5 us
    ppermute x7, starting transfers between devices, from_behind(): return lax.ppermute(array, axis, pairs)  66.5 us
    ppermute x7, waiting for transfers between devices, from_behind(): return lax.ppermute(array, axis, pairs)  55.3 us
    all_gather x1, waiting for transfers between devices, local(): lax.all_gather(heads_out, 'head', axis=1, tiled=True)  40.7 us
  transfers between devices with their start and end apart: 9, of which 7 were waited for; matrix products, arithmetic and copies ran while one was open for 3% of the time, Pallas kernels for 0%

commit v1 on v0

v1 whole, which is shorter than its diff:
```python
import jax
import jax.numpy as jnp
from jax import lax
from jax.sharding import PartitionSpec as P

RATE_MID = 8
RATE_TOP = 32
SEG_ROWS = 1024
ROW = 16


NEG_FILL = -1e30


def send(array, pairs):
    return lax.ppermute(array, "seq", pairs)


def pick_rows(states, chooser, spacing):
    row_count, head_count, head_width = states.shape
    grouped = states.reshape(row_count // spacing, spacing, head_count, head_width)
    return jnp.einsum("nrhd,rh->nhd", grouped, chooser, preferred_element_type=jnp.float32).astype(
        jnp.bfloat16
    )


def attend(query_rows, key_rows, value_rows, allowed, scale_factor):
    scores = (
        jnp.einsum("qhd,khd->hqk", query_rows, key_rows, preferred_element_type=jnp.float32)
        * scale_factor
    )
    if allowed is not None:
        scores = jnp.where(allowed[None], scores, NEG_FILL)
    highest = jnp.max(scores, axis=2, keepdims=True)
    weights = jnp.exp(scores - highest)
    totals = jnp.sum(weights, axis=2, keepdims=True)
    shares = (weights / totals).astype(jnp.bfloat16)
    result = jnp.einsum("hqk,khd->qhd", shares, value_rows, preferred_element_type=jnp.float32)
    return (result, (highest + jnp.log(totals))[:, :, 0].T)


def merge(outs, lses):
    lse_stack = jnp.stack(lses)
    top = jnp.max(lse_stack, axis=0)
    weights = jnp.exp(lse_stack - top[None])
    total = jnp.sum(weights, axis=0)
    out = jnp.sum(weights[..., None] * jnp.stack(outs), axis=0) / total[..., None]
    return out, top + jnp.log(total)


def spread_back(level_out, level_lse, chooser):
    picked = chooser.astype(jnp.float32)
    sparse_count, head_count, head_width = level_out.shape
    row_count = sparse_count * chooser.shape[0]
    full_out = (level_out[:, None, :, :] * picked[None, :, :, None]).reshape(
        row_count, head_count, head_width
    )
    full_lse = jnp.where(chooser[None], level_lse[:, None, :], NEG_FILL).reshape(
        row_count, head_count
    )
    return (full_out, full_lse)


def level_setup(query_all, key_all, value_all, offset_row, spacing):
    head_count = query_all.shape[1]
    chooser = (
        lax.broadcasted_iota(jnp.int32, (spacing, head_count), 0) == (offset_row % spacing)[None, :]
    )
    chooser_bf = chooser.astype(jnp.bfloat16)
    query_rows = pick_rows(query_all, chooser_bf, spacing)
    pair_rows = jnp.stack(
        [pick_rows(key_all, chooser_bf, spacing), pick_rows(value_all, chooser_bf, spacing)], axis=1
    )
    return (chooser, query_rows, pair_rows)


def pack(out, lse):
    return jnp.concatenate([out, lse[..., None]], axis=-1)


def unpack(packed):
    return packed[..., :-1], packed[..., -1]


def ring_gather(block, seq_count):
    forward = [(s, (s // ROW) * ROW + (s % ROW + 1) % ROW) for s in range(seq_count)]
    backward = [(s, (s // ROW) * ROW + (s % ROW - 1) % ROW) for s in range(seq_count)]
    ahead = [None] * ROW
    ahead[0] = block
    moving = block
    for step in range(1, ROW // 2 + 1):
        moving = send(moving, forward)
        ahead[step] = moving
    moving = block
    for step in range(1, ROW // 2):
        moving = send(moving, backward)
        ahead[ROW - step] = moving
    return jnp.stack(ahead)


def local(queries, key_states, value_states, level_offsets, out_weight):
    row_count = queries.shape[0]
    head_count = level_offsets.shape[1]
    head_width = queries.shape[1] // head_count
    scale_factor = head_width ** (-0.5)
    seq_count = lax.axis_size("seq")
    seq_index = lax.axis_index("seq")
    row_y = seq_index // ROW
    row_z = seq_index % ROW
    rows_total = seq_count // ROW
    query_all = queries.reshape(row_count, head_count, head_width)
    key_all = key_states.reshape(row_count, head_count, head_width)
    value_all = value_states.reshape(row_count, head_count, head_width)
    full_outs = []
    full_lses = []

    span0 = SEG_ROWS // row_count
    chooser0, query0, pair0 = level_setup(query_all, key_all, value_all, level_offsets[0], 1)
    arrived = []
    for shift in range(span0 - 1, 0, -1):
        pairs = [(s, s + shift) for s in range(seq_count) if s % span0 + shift < span0]
        arrived.append(send(pair0, pairs))
    buffer0 = jnp.concatenate(arrived + [pair0], axis=0)
    shape0 = (row_count, span0 * row_count)
    key_index = lax.broadcasted_iota(jnp.int32, shape0, 1)
    query_index = lax.broadcasted_iota(jnp.int32, shape0, 0)
    lowest = (span0 - 1 - seq_index % span0) * row_count
    allowed0 = (key_index >= lowest) & (key_index <= (span0 - 1) * row_count + query_index)
    out0, lse0 = attend(query0, buffer0[:, 0], buffer0[:, 1], allowed0, scale_factor)
    full_out, full_lse = spread_back(out0, lse0, chooser0)
    full_outs.append(full_out)
    full_lses.append(full_lse)

    chooser1, query1, pair1 = level_setup(query_all, key_all, value_all, level_offsets[1], RATE_MID)
    chooser2, query2, pair2 = level_setup(query_all, key_all, value_all, level_offsets[2], RATE_TOP)
    count1 = pair1.shape[0]
    count2 = pair2.shape[0]
    ring = ring_gather(jnp.concatenate([pair1, pair2], axis=0), seq_count)
    row1 = ring[:, :count1]
    row2 = ring[:, count1:]

    def own_row(query_rows, row_blocks, count):
        keys = row_blocks.reshape(ROW * count, 2, head_count, head_width)
        shape = (count, ROW * count)
        key_index = lax.broadcasted_iota(jnp.int32, shape, 1)
        query_index = lax.broadcasted_iota(jnp.int32, shape, 0)
        offset = key_index // count
        allowed = jnp.where(
            offset == 0, key_index % count <= query_index, offset <= row_z
        )
        return attend(query_rows, keys[:, 0], keys[:, 1], allowed, scale_factor)

    def whole_row(query_rows, row_blocks, count):
        keys = row_blocks.reshape(ROW * count, 2, head_count, head_width)
        return attend(query_rows, keys[:, 0], keys[:, 1], None, scale_factor)

    up = [(s, s - ROW) for s in range(seq_count) if (s // ROW) % 2 == 1]
    down = [(s, s + ROW) for s in range(seq_count) if (s // ROW) % 2 == 0]
    visiting1 = send(query1, up)
    own_out1, own_lse1 = own_row(query1, row1, count1)
    cross1 = send(pack(*whole_row(visiting1, row1, count1)), down)
    cross_out1, cross_lse1 = unpack(cross1)
    cross_lse1 = jnp.where(row_y % 2 == 1, cross_lse1, NEG_FILL)
    out1, lse1 = merge([own_out1, cross_out1], [own_lse1, cross_lse1])
    full_out, full_lse = spread_back(out1, lse1, chooser1)
    full_outs.append(full_out)
    full_lses.append(full_lse)

    own_out2, own_lse2 = own_row(query2, row2, count2)
    visiting = []
    for gap in range(1, rows_total):
        pairs = [(s, s - gap * ROW) for s in range(seq_count) if s // ROW >= gap]
        visiting.append(send(query2, pairs))
    visiting2 = jnp.concatenate(visiting, axis=0)
    cross_out, cross_lse = whole_row(visiting2, row2, count2)
    outs2 = [own_out2]
    lses2 = [own_lse2]
    for gap in range(1, rows_total):
        pairs = [(s, s + gap * ROW) for s in range(seq_count) if s // ROW + gap < rows_total]
        part = slice((gap - 1) * count2, gap * count2)
        back_out, back_lse = unpack(send(pack(cross_out[part], cross_lse[part]), pairs))
        outs2.append(back_out)
        lses2.append(jnp.where(row_y >= gap, back_lse, NEG_FILL))
    out2, lse2 = merge(outs2, lses2)
    full_out, full_lse = spread_back(out2, lse2, chooser2)
    full_outs.append(full_out)
    full_lses.append(full_lse)

    lse_stack = jnp.stack(full_lses)
    level_top = jnp.max(lse_stack, axis=0)
    level_weights = jnp.exp(lse_stack - level_top[None])
    mixed_heads = (
        jnp.sum(level_weights[..., None] * jnp.stack(full_outs), axis=0)
        / jnp.sum(level_weights, axis=0)[..., None]
    )
    heads_out = mixed_heads.astype(jnp.bfloat16).reshape(row_count, head_count * head_width)
    projected = jnp.dot(
        lax.all_gather(heads_out, "head", axis=1, tiled=True),
        out_weight,
        preferred_element_type=jnp.float32,
    )
    return projected.astype(jnp.bfloat16)


def solution(mesh):
    return jax.shard_map(
        local,
        mesh=mesh,
        in_specs=(
            P("seq", "head"),
            P("seq", "head"),
            P("seq", "head"),
            P(None, "head"),
            P(None, "head"),
        ),
        out_specs=P("seq", "head"),
        check_vma=False,
    )
```

time: 266 us -> 207 us (0.78)
  waiting for transfers between devices: 164 us -> 69.7 us
  starting transfers between devices: 66.5 us -> 98.3 us
    all_gather x1 -> x0, waiting for transfers between devices: 67.5 us -> none  [local(): shard_rows = lax.all_gather(pair_rows, 'seq', axis=0, tiled=True)]
    ppermute x7 -> x34, starting transfers between devices: 66.5 us -> 98.3 us  [send(): return lax.ppermute(array, 'seq', pairs)]
    ppermute x7 -> x34, waiting for transfers between devices: 55.3 us -> 32.6 us  [send(): return lax.ppermute(array, 'seq', pairs)]
    all_gather x1, waiting for transfers between devices: 40.7 us -> 37.1 us  [local(): lax.all_gather(heads_out, 'head', axis=1, tiled=True)]
    dot_general x2 -> x0, matrix products: 2.93 us -> none  [the longest x1 1.52 us: local(): jnp.einsum('qhd,khd->hqk', query_rows, shard_rows[:, 0], preferred_elemen...]
  transfers between devices with their start and end apart: 9 -> 35, of which waited for: 7 -> 11; matrix products, arithmetic and copies ran while one was open for 3% -> 5% of each run, Pallas kernels for 0% -> 0%
where the time goes in v1:
time: 207 us; the launch traced here: 206 us
  starting transfers between devices  98.3 us (47%)
  waiting for transfers between devices  69.7 us (34%)
  between operations  14.5 us (7%)
  matrix products  12.5 us (6%)
  local copies, waits for them, and re-layouts  6.06 us (3%)
  other arithmetic  5.16 us (2%)
    ppermute x34, starting transfers between devices, send(): return lax.ppermute(array, 'seq', pairs)  98.3 us
    all_gather x1, waiting for transfers between devices, local(): lax.all_gather(heads_out, 'head', axis=1, tiled=True)  37.1 us
    ppermute x34, waiting for transfers between devices, send(): return lax.ppermute(array, 'seq', pairs)  32.6 us
    dot_general x1, matrix products, local(): jnp.dot(lax.all_gather(heads_out, 'head', axis=1, tiled=True), out_weight...  4.73 us
  transfers between devices with their start and end apart: 35, of which 11 were waited for; matrix products, arithmetic and copies ran while one was open for 5% of the time, Pallas kernels for 0%

profile of v1, /device:TPU:1, one launch (start us, length us, event | category | flops | bytes accessed | tf_op | source)
XLA Modules:
  0.0 206.3 jit_solution(8243566828998579735)
XLA Ops:
  6.5 1.0 reshape_reshape.25
  9.4 1.1 fusion.16
  10.6 1.1 fusion.18
  12.1 4.8 %collective-permute-start.3 = (bf16[40,2,3,128]{3,0,2,1:T(8,128)(2,1)S(1)}, bf16[40,2,3,128]{3,0,2,1:T(8,128)(2,1)S(1)}, u32[]{:S(2)}, u32[]{:S(2)}) collective-permute-start(bf16[40,2,3,128]{3,0,2,1:T(8,128)(2,1)S(1)} %maximum_maximum_fusion.1), channel_id=1, source_target_pairs={{0,8},{8,16},{16,24},{24,32},{32,40},{40,48},{48,56},{56,64},{64,7... | collective-permute-start | bytes 184328 | tf_op jit(solution)/shard_map/ppermute | solution.py:16
  16.9 15.9 %collective-permute-start.11 = (bf16[40,2,3,128]{3,0,2,1:T(8,128)(2,1)S(1)}, bf16[40,2,3,128]{3,0,2,1:T(8,128)(2,1)S(1)}, u32[]{:S(2)}, u32[]{:S(2)}) collective-permute-start(bf16[40,2,3,128]{3,0,2,1:T(8,128)(2,1)S(1)} %maximum_maximum_fusion.1), channel_id=1, source_target_pairs={{0,120},{8,0},{16,8},{24,16},{32,24},{40,32},{48,40},{56,48},{64,5... | collective-permute-start | bytes 184328 | tf_op jit(solution)/shard_map/ppermute | solution.py:16
  33.9 1.3 collective-permute-start.20
  35.2 1.3 collective-permute-start.21
  36.5 1.3 collective-permute-start.22
  37.9 1.1 fusion.20
  40.5 1.3 collective-permute-start.23
  41.8 1.3 collective-permute-start.24
  43.1 1.1 collective-permute-done.22
  44.2 1.3 collective-permute-start.25
  45.5 4.9 %collective-permute-done.23 = bf16[8,3,128]{2,0,1:T(8,128)(2,1)S(1)} collective-permute-done((bf16[8,3,128]{2,0,1:T(8,128)(2,1)S(1)}, bf16[8,3,128]{2,0,1:T(8,128)(2,1)S(1)}, u32[]{:S(2)}, u32[]{:S(2)}) %collective-permute-start.23) | collective-permute-done | bytes 6176 | tf_op jit(solution)/shard_map/ppermute | solution.py:16
  50.4 1.3 collective-permute-start.26
  52.0 1.3 collective-permute-start.2
  53.5 1.3 collective-permute-start.1
  54.8 1.2 collective-permute-done.26
  56.0 1.3 collective-permute-start
  57.3 1.9 collective-permute-start.4
  59.3 4.6 %collective-permute-start.12 = (bf16[40,2,3,128]{3,0,2,1:T(8,128)(2,1)S(1)}, bf16[40,2,3,128]{3,0,2,1:T(8,128)(2,1)S(1)}, u32[]{:S(2)}, u32[]{:S(2)}) collective-permute-start(bf16[40,2,3,128]{3,0,2,1:T(8,128)(2,1)S(1)} %collective-permute-done.11), channel_id=1, source_target_pairs={{0,120},{8,0},{16,8},{24,16},{32,24},{40,32},{48,40},{56,48},{64,5... | collective-permute-start | bytes 184328 | tf_op jit(solution)/shard_map/ppermute | solution.py:16
  63.9 14.2 %collective-permute-done.4 = bf16[40,2,3,128]{3,0,2,1:T(8,128)(2,1)S(1)} collective-permute-done((bf16[40,2,3,128]{3,0,2,1:T(8,128)(2,1)S(1)}, bf16[40,2,3,128]{3,0,2,1:T(8,128)(2,1)S(1)}, u32[]{:S(2)}, u32[]{:S(2)}) %collective-permute-start.4) | collective-permute-done | bytes 61472 | tf_op jit(solution)/shard_map/ppermute | solution.py:16
  78.0 3.8 %collective-permute-start.5 = (bf16[40,2,3,128]{3,0,2,1:T(8,128)(2,1)S(1)}, bf16[40,2,3,128]{3,0,2,1:T(8,128)(2,1)S(1)}, u32[]{:S(2)}, u32[]{:S(2)}) collective-permute-start(bf16[40,2,3,128]{3,0,2,1:T(8,128)(2,1)S(1)} %collective-permute-done.4), channel_id=1, source_target_pairs={{0,8},{8,16},{16,24},{24,32},{32,40},{40,48},{48,56},{56,64},{64,7... | collective-permute-start | bytes 184328 | tf_op jit(solution)/shard_map/ppermute | solution.py:16
  81.9 2.7 %collective-permute-start.13 = (bf16[40,2,3,128]{3,0,2,1:T(8,128)(2,1)S(1)}, bf16[40,2,3,128]{3,0,2,1:T(8,128)(2,1)S(1)}, u32[]{:S(2)}, u32[]{:S(2)}) collective-permute-start(bf16[40,2,3,128]{3,0,2,1:T(8,128)(2,1)S(1)} %collective-permute-done.12), channel_id=1, source_target_pairs={{0,120},{8,0},{16,8},{24,16},{32,24},{40,32},{48,40},{56,48},{64,5... | collective-permute-start | bytes 184328 | tf_op jit(solution)/shard_map/ppermute | solution.py:16
  84.6 2.6 %collective-permute-start.6 = (bf16[40,2,3,128]{3,0,2,1:T(8,128)(2,1)S(1)}, bf16[40,2,3,128]{3,0,2,1:T(8,128)(2,1)S(1)}, u32[]{:S(2)}, u32[]{:S(2)}) collective-permute-start(bf16[40,2,3,128]{3,0,2,1:T(8,128)(2,1)S(1)} %collective-permute-done.5), channel_id=1, source_target_pairs={{0,8},{8,16},{16,24},{24,32},{32,40},{40,48},{48,56},{56,64},{64,7... | collective-permute-start | bytes 184328 | tf_op jit(solution)/shard_map/ppermute | solution.py:16
  87.2 10.1 %collective-permute-start.14 = (bf16[40,2,3,128]{3,0,2,1:T(8,128)(2,1)S(1)}, bf16[40,2,3,128]{3,0,2,1:T(8,128)(2,1)S(1)}, u32[]{:S(2)}, u32[]{:S(2)}) collective-permute-start(bf16[40,2,3,128]{3,0,2,1:T(8,128)(2,1)S(1)} %collective-permute-done.13), channel_id=1, source_target_pairs={{0,120},{8,0},{16,8},{24,16},{32,24},{40,32},{48,40},{56,48},{64,5... | collective-permute-start | bytes 184328 | tf_op jit(solution)/shard_map/ppermute | solution.py:16
  97.4 1.9 collective-permute-start.7
  99.3 4.6 %collective-permute-start.15 = (bf16[40,2,3,128]{3,0,2,1:T(8,128)(2,1)S(1)}, bf16[40,2,3,128]{3,0,2,1:T(8,128)(2,1)S(1)}, u32[]{:S(2)}, u32[]{:S(2)}) collective-permute-start(bf16[40,2,3,128]{3,0,2,1:T(8,128)(2,1)S(1)} %collective-permute-done.14), channel_id=1, source_target_pairs={{0,120},{8,0},{16,8},{24,16},{32,24},{40,32},{48,40},{56,48},{64,5... | collective-permute-start | bytes 184328 | tf_op jit(solution)/shard_map/ppermute | solution.py:16
  103.9 1.9 collective-permute-start.8
  105.9 1.3 collective-permute-start.18
  107.2 2.9 %collective-permute-done.8 = bf16[40,2,3,128]{3,0,2,1:T(8,128)(2,1)S(1)} collective-permute-done((bf16[40,2,3,128]{3,0,2,1:T(8,128)(2,1)S(1)}, bf16[40,2,3,128]{3,0,2,1:T(8,128)(2,1)S(1)}, u32[]{:S(2)}, u32[]{:S(2)}) %collective-permute-start.8) | collective-permute-done | bytes 61472 | tf_op jit(solution)/shard_map/ppermute | solution.py:16
  110.1 1.9 collective-permute-start.16
  112.0 3.0 %collective-permute-done.16 = bf16[40,2,3,128]{3,0,2,1:T(8,128)(2,1)S(1)} collective-permute-done((bf16[40,2,3,128]{3,0,2,1:T(8,128)(2,1)S(1)}, bf16[40,2,3,128]{3,0,2,1:T(8,128)(2,1)S(1)}, u32[]{:S(2)}, u32[]{:S(2)}) %collective-permute-start.16) | collective-permute-done | bytes 61472 | tf_op jit(solution)/shard_map/ppermute | solution.py:16
  115.0 1.9 collective-permute-start.9
  117.0 4.6 %collective-permute-start.17 = (bf16[40,2,3,128]{3,0,2,1:T(8,128)(2,1)S(1)}, bf16[40,2,3,128]{3,0,2,1:T(8,128)(2,1)S(1)}, u32[]{:S(2)}, u32[]{:S(2)}) collective-permute-start(bf16[40,2,3,128]{3,0,2,1:T(8,128)(2,1)S(1)} %collective-permute-done.16), channel_id=1, source_target_pairs={{0,120},{8,0},{16,8},{24,16},{32,24},{40,32},{48,40},{56,48},{64,5... | collective-permute-start | bytes 184328 | tf_op jit(solution)/shard_map/ppermute | solution.py:16
  123.1 1.2 fusion.3
  124.3 1.9 collective-permute-start.10
  126.3 4.3 %collective-permute-done.10 = bf16[40,2,3,128]{3,0,2,1:T(8,128)(2,1)S(1)} collective-permute-done((bf16[40,2,3,128]{3,0,2,1:T(8,128)(2,1)S(1)}, bf16[40,2,3,128]{3,0,2,1:T(8,128)(2,1)S(1)}, u32[]{:S(2)}, u32[]{:S(2)}) %collective-permute-start.10) | collective-permute-done | bytes 61472 | tf_op jit(solution)/shard_map/ppermute | solution.py:16
  134.0 3.0 %collective-permute-start.27 = (f32[8,3,129]{2,0,1:T(8,128)S(1)}, f32[8,3,129]{2,0,1:T(8,128)S(1)}, u32[]{:S(2)}, u32[]{:S(2)}) collective-permute-start(f32[8,3,129]{2,0,1:T(8,128)S(1)} %pad_maximum_fusion.2), channel_id=1, source_target_pairs={{0,128},{8,136},{16,144},{24,152},{32,160},{40,168},{48,176},{56,1... | collective-permute-start | bytes 37160 | tf_op jit(solution)/shard_map/ppermute | solution.py:16
  137.1 4.3 %collective-permute-start.28 = (f32[8,3,129]{2,0,1:T(8,128)S(1)}, f32[8,3,129]{2,0,1:T(8,128)S(1)}, u32[]{:S(2)}, u32[]{:S(2)}) collective-permute-start(f32[8,3,129]{2,0,1:T(8,128)S(1)} %pad_maximum_fusion.3), channel_id=1, source_target_pairs={{0,256},{8,264},{16,272},{24,280},{32,288},{40,296},{48,304},{56,3... | collective-permute-start | bytes 37160 | tf_op jit(solution)/shard_map/ppermute | solution.py:16
  141.5 2.8 %collective-permute-start.29 = (f32[8,3,129]{2,0,1:T(8,128)S(1)}, f32[8,3,129]{2,0,1:T(8,128)S(1)}, u32[]{:S(2)}, u32[]{:S(2)}) collective-permute-start(f32[8,3,129]{2,0,1:T(8,128)S(1)} %pad_maximum_fusion.4), channel_id=1, source_target_pairs={{0,384},{8,392},{16,400},{24,408},{32,416},{40,424},{48,432},{56,4... | collective-permute-start | bytes 37160 | tf_op jit(solution)/shard_map/ppermute | solution.py:16
  144.4 3.8 %collective-permute-start.30 = (f32[8,3,129]{2,0,1:T(8,128)S(1)}, f32[8,3,129]{2,0,1:T(8,128)S(1)}, u32[]{:S(2)}, u32[]{:S(2)}) collective-permute-start(f32[8,3,129]{2,0,1:T(8,128)S(1)} %pad_maximum_fusion.5), channel_id=1, source_target_pairs={{0,512},{8,520},{16,528},{24,536},{32,544},{40,552},{48,560},{56,5... | collective-permute-start | bytes 37160 | tf_op jit(solution)/shard_map/ppermute | solution.py:16
  148.3 1.3 collective-permute-start.31
  149.9 1.3 collective-permute-start.32
  151.3 1.3 collective-permute-start.33
  152.7 1.3 collective-permute-start.19
  157.6 37.1 %all-gather.2.cloned.1.call-done = bf16[256,3072]{0,1:T(8,128)(2,1)} async-done(((bf16[256,384]{0,1:T(8,128)(2,1)}), bf16[256,3072]{0,1:T(8,128)(2,1)}) %all-gather.2.cloned.1.call-update) | async-done | bytes 1572880 | tf_op jit(solution)/shard_map/all_gather | solution.py:198
  194.7 4.7 %convolution_convert_fusion = bf16[256,640]{1,0:T(8,128)(2,1)} fusion(bf16[256,3072]{0,1:T(8,128)(2,1)} %all-gather.2.cloned.1.call-done, bf16[3072,640]{1,0:T(8,128)(2,1)} %param.9), kind=kOutput, calls=%fused_computation.7 | convolution fusion | flops 1006796800 | bytes 5832704 | tf_op jit(solution)/shard_map/dot_general | solution.py:197
  (181 shorter events, 14.5 us)
Async XLA Ops:
  6.5 32.5 %copy-start = (bf16[256,384]{1,0:T(8,128)(2,1)S(1)}, bf16[256,384]{1,0:T(8,128)(2,1)}, u32[]{:S(2)}) copy-start(bf16[256,384]{1,0:T(8,128)(2,1)} %param.7) | copy-start | bytes 589828
  6.5 32.7 %copy-start.1 = (bf16[256,384]{1,0:T(8,128)(2,1)S(1)}, bf16[256,384]{1,0:T(8,128)(2,1)}, u32[]{:S(2)}) copy-start(bf16[256,384]{1,0:T(8,128)(2,1)} %param.6) | copy-start | bytes 589828
  6.5 33.6 %copy-start.2 = (bf16[256,384]{1,0:T(8,128)(2,1)S(1)}, bf16[256,384]{1,0:T(8,128)(2,1)}, u32[]{:S(2)}) copy-start(bf16[256,384]{1,0:T(8,128)(2,1)} %param.5) | copy-start | bytes 589828
  6.5 188.2 %all-gather.2.cloned.1.call-start = ((), (), s32[]{:S(2)}) async-start(), calls=%async_computation | async-start | bytes 1769472 | tf_op jit(solution)/shard_map/all_gather | solution.py:198
  12.1 45.2 %collective-permute-start.3 = (bf16[40,2,3,128]{3,0,2,1:T(8,128)(2,1)S(1)}, bf16[40,2,3,128]{3,0,2,1:T(8,128)(2,1)S(1)}, u32[]{:S(2)}, u32[]{:S(2)}) collective-permute-start(bf16[40,2,3,128]{3,0,2,1:T(8,128)(2,1)S(1)} %maximum_maximum_fusion.1), channel_id=1, source_target_pairs={{0,8},{8,16},{16,24},{24,32},{32,40},{40,48},{48,56},{56,64},{64,7... | collective-permute-start | bytes 184328 | tf_op jit(solution)/shard_map/ppermute | solution.py:16
  16.9 42.4 %collective-permute-start.11 = (bf16[40,2,3,128]{3,0,2,1:T(8,128)(2,1)S(1)}, bf16[40,2,3,128]{3,0,2,1:T(8,128)(2,1)S(1)}, u32[]{:S(2)}, u32[]{:S(2)}) collective-permute-start(bf16[40,2,3,128]{3,0,2,1:T(8,128)(2,1)S(1)} %maximum_maximum_fusion.1), channel_id=1, source_target_pairs={{0,120},{8,0},{16,8},{24,16},{32,24},{40,32},{48,40},{56,48},{64,5... | collective-permute-start | bytes 184328 | tf_op jit(solution)/shard_map/ppermute | solution.py:16
  33.9 6.6 %collective-permute-start.20 = (bf16[8,3,128]{2,0,1:T(8,128)(2,1)S(1)}, bf16[8,3,128]{2,0,1:T(8,128)(2,1)S(1)}, u32[]{:S(2)}, u32[]{:S(2)}) collective-permute-start(bf16[8,3,128]{2,0,1:T(8,128)(2,1)S(1)} %convert_bitcast_fusion.3), channel_id=1, source_target_pairs={{128,0},{136,8},{144,16},{152,24},{160,32},{168,40},{176,48},{184,... | collective-permute-start | bytes 18440 | tf_op jit(solution)/shard_map/ppermute | solution.py:16
  35.2 6.6 %collective-permute-start.21 = (bf16[8,3,128]{2,0,1:T(8,128)(2,1)S(1)}, bf16[8,3,128]{2,0,1:T(8,128)(2,1)S(1)}, u32[]{:S(2)}, u32[]{:S(2)}) collective-permute-start(bf16[8,3,128]{2,0,1:T(8,128)(2,1)S(1)} %convert_bitcast_fusion.3), channel_id=1, source_target_pairs={{256,0},{264,8},{272,16},{280,24},{288,32},{296,40},{304,48},{312,... | collective-permute-start | bytes 18440 | tf_op jit(solution)/shard_map/ppermute | solution.py:16
  36.5 7.7 %collective-permute-start.22 = (bf16[8,3,128]{2,0,1:T(8,128)(2,1)S(1)}, bf16[8,3,128]{2,0,1:T(8,128)(2,1)S(1)}, u32[]{:S(2)}, u32[]{:S(2)}) collective-permute-start(bf16[8,3,128]{2,0,1:T(8,128)(2,1)S(1)} %convert_bitcast_fusion.3), channel_id=1, source_target_pairs={{384,0},{392,8},{400,16},{408,24},{416,32},{424,40},{432,48},{440,... | collective-permute-start | bytes 18440 | tf_op jit(solution)/shard_map/ppermute | solution.py:16
  40.5 9.9 %collective-permute-start.23 = (bf16[8,3,128]{2,0,1:T(8,128)(2,1)S(1)}, bf16[8,3,128]{2,0,1:T(8,128)(2,1)S(1)}, u32[]{:S(2)}, u32[]{:S(2)}) collective-permute-start(bf16[8,3,128]{2,0,1:T(8,128)(2,1)S(1)} %convert_bitcast_fusion.3), channel_id=1, source_target_pairs={{512,0},{520,8},{528,16},{536,24},{544,32},{552,40},{560,48},{568,... | collective-permute-start | bytes 18440 | tf_op jit(solution)/shard_map/ppermute | solution.py:16
  41.8 10.2 %collective-permute-start.24 = (bf16[8,3,128]{2,0,1:T(8,128)(2,1)S(1)}, bf16[8,3,128]{2,0,1:T(8,128)(2,1)S(1)}, u32[]{:S(2)}, u32[]{:S(2)}) collective-permute-start(bf16[8,3,128]{2,0,1:T(8,128)(2,1)S(1)} %convert_bitcast_fusion.3), channel_id=1, source_target_pairs={{640,0},{648,8},{656,16},{664,24},{672,32},{680,40},{688,48},{696,... | collective-permute-start | bytes 18440 | tf_op jit(solution)/shard_map/ppermute | solution.py:16
  44.2 9.3 %collective-permute-start.25 = (bf16[8,3,128]{2,0,1:T(8,128)(2,1)S(1)}, bf16[8,3,128]{2,0,1:T(8,128)(2,1)S(1)}, u32[]{:S(2)}, u32[]{:S(2)}) collective-permute-start(bf16[8,3,128]{2,0,1:T(8,128)(2,1)S(1)} %convert_bitcast_fusion.3), channel_id=1, source_target_pairs={{768,0},{776,8},{784,16},{792,24},{800,32},{808,40},{816,48},{824,... | collective-permute-start | bytes 18440 | tf_op jit(solution)/shard_map/ppermute | solution.py:16
  50.4 5.6 %collective-permute-start.26 = (bf16[8,3,128]{2,0,1:T(8,128)(2,1)S(1)}, bf16[8,3,128]{2,0,1:T(8,128)(2,1)S(1)}, u32[]{:S(2)}, u32[]{:S(2)}) collective-permute-start(bf16[8,3,128]{2,0,1:T(8,128)(2,1)S(1)} %convert_bitcast_fusion.3), channel_id=1, source_target_pairs={{896,0},{904,8},{912,16},{920,24},{928,32},{936,40},{944,48},{952,... | collective-permute-start | bytes 18440 | tf_op jit(solution)/shard_map/ppermute | solution.py:16
  52.0 64.9 %collective-permute-start.2 = (bf16[256,2,3,128]{3,0,2,1:T(8,128)(2,1)S(1)}, bf16[256,2,3,128]{3,0,2,1:T(8,128)(2,1)S(1)}, u32[]{:S(2)}, u32[]{:S(2)}) collective-permute-start(bf16[256,2,3,128]{3,0,2,1:T(8,128)(2,1)S(1)} %pad_maximum_fusion), channel_id=1, source_target_pairs={{0,8},{8,16},{16,24},{32,40},{40,48},{48,56},{64,72},{72,80},{80,8... | collective-permute-start | bytes 1179656 | tf_op jit(solution)/shard_map/ppermute | solution.py:16
  53.5 68.0 %collective-permute-start.1 = (bf16[256,2,3,128]{3,0,2,1:T(8,128)(2,1)S(1)}, bf16[256,2,3,128]{3,0,2,1:T(8,128)(2,1)S(1)}, u32[]{:S(2)}, u32[]{:S(2)}) collective-permute-start(bf16[256,2,3,128]{3,0,2,1:T(8,128)(2,1)S(1)} %pad_maximum_fusion), channel_id=1, source_target_pairs={{0,16},{8,24},{32,48},{40,56},{64,80},{72,88},{96,112},{104,120},{... | collective-permute-start | bytes 1179656 | tf_op jit(solution)/shard_map/ppermute | solution.py:16
  56.0 65.6 %collective-permute-start = (bf16[256,2,3,128]{3,0,2,1:T(8,128)(2,1)S(1)}, bf16[256,2,3,128]{3,0,2,1:T(8,128)(2,1)S(1)}, u32[]{:S(2)}, u32[]{:S(2)}) collective-permute-start(bf16[256,2,3,128]{3,0,2,1:T(8,128)(2,1)S(1)} %pad_maximum_fusion), channel_id=1, source_target_pairs={{0,24},{32,56},{64,88},{96,120},{128,152},{160,184},{192,216},{224... | collective-permute-start | bytes 1179656 | tf_op jit(solution)/shard_map/ppermute | solution.py:16
  57.3 20.7 %collective-permute-start.4 = (bf16[40,2,3,128]{3,0,2,1:T(8,128)(2,1)S(1)}, bf16[40,2,3,128]{3,0,2,1:T(8,128)(2,1)S(1)}, u32[]{:S(2)}, u32[]{:S(2)}) collective-permute-start(bf16[40,2,3,128]{3,0,2,1:T(8,128)(2,1)S(1)} %collective-permute-done.3), channel_id=1, source_target_pairs={{0,8},{8,16},{16,24},{24,32},{32,40},{40,48},{48,56},{56,64},{64,7... | collective-permute-start | bytes 184328 | tf_op jit(solution)/shard_map/ppermute | solution.py:16
  59.3 22.6 %collective-permute-start.12 = (bf16[40,2,3,128]{3,0,2,1:T(8,128)(2,1)S(1)}, bf16[40,2,3,128]{3,0,2,1:T(8,128)(2,1)S(1)}, u32[]{:S(2)}, u32[]{:S(2)}) collective-permute-start(bf16[40,2,3,128]{3,0,2,1:T(8,128)(2,1)S(1)} %collective-permute-done.11), channel_id=1, source_target_pairs={{0,120},{8,0},{16,8},{24,16},{32,24},{40,32},{48,40},{56,48},{64,5... | collective-permute-start | bytes 184328 | tf_op jit(solution)/shard_map/ppermute | solution.py:16
  78.0 6.5 %collective-permute-start.5 = (bf16[40,2,3,128]{3,0,2,1:T(8,128)(2,1)S(1)}, bf16[40,2,3,128]{3,0,2,1:T(8,128)(2,1)S(1)}, u32[]{:S(2)}, u32[]{:S(2)}) collective-permute-start(bf16[40,2,3,128]{3,0,2,1:T(8,128)(2,1)S(1)} %collective-permute-done.4), channel_id=1, source_target_pairs={{0,8},{8,16},{16,24},{24,32},{32,40},{40,48},{48,56},{56,64},{64,7... | collective-permute-start | bytes 184328 | tf_op jit(solution)/shard_map/ppermute | solution.py:16
  81.9 5.3 %collective-permute-start.13 = (bf16[40,2,3,128]{3,0,2,1:T(8,128)(2,1)S(1)}, bf16[40,2,3,128]{3,0,2,1:T(8,128)(2,1)S(1)}, u32[]{:S(2)}, u32[]{:S(2)}) collective-permute-start(bf16[40,2,3,128]{3,0,2,1:T(8,128)(2,1)S(1)} %collective-permute-done.12), channel_id=1, source_target_pairs={{0,120},{8,0},{16,8},{24,16},{32,24},{40,32},{48,40},{56,48},{64,5... | collective-permute-start | bytes 184328 | tf_op jit(solution)/shard_map/ppermute | solution.py:16
  84.6 12.8 %collective-permute-start.6 = (bf16[40,2,3,128]{3,0,2,1:T(8,128)(2,1)S(1)}, bf16[40,2,3,128]{3,0,2,1:T(8,128)(2,1)S(1)}, u32[]{:S(2)}, u32[]{:S(2)}) collective-permute-start(bf16[40,2,3,128]{3,0,2,1:T(8,128)(2,1)S(1)} %collective-permute-done.5), channel_id=1, source_target_pairs={{0,8},{8,16},{16,24},{24,32},{32,40},{40,48},{48,56},{56,64},{64,7... | collective-permute-start | bytes 184328 | tf_op jit(solution)/shard_map/ppermute | solution.py:16
  87.2 12.1 %collective-permute-start.14 = (bf16[40,2,3,128]{3,0,2,1:T(8,128)(2,1)S(1)}, bf16[40,2,3,128]{3,0,2,1:T(8,128)(2,1)S(1)}, u32[]{:S(2)}, u32[]{:S(2)}) collective-permute-start(bf16[40,2,3,128]{3,0,2,1:T(8,128)(2,1)S(1)} %collective-permute-done.13), channel_id=1, source_target_pairs={{0,120},{8,0},{16,8},{24,16},{32,24},{40,32},{48,40},{56,48},{64,5... | collective-permute-start | bytes 184328 | tf_op jit(solution)/shard_map/ppermute | solution.py:16
  97.4 6.5 %collective-permute-start.7 = (bf16[40,2,3,128]{3,0,2,1:T(8,128)(2,1)S(1)}, bf16[40,2,3,128]{3,0,2,1:T(8,128)(2,1)S(1)}, u32[]{:S(2)}, u32[]{:S(2)}) collective-permute-start(bf16[40,2,3,128]{3,0,2,1:T(8,128)(2,1)S(1)} %collective-permute-done.6), channel_id=1, source_target_pairs={{0,8},{8,16},{16,24},{24,32},{32,40},{40,48},{48,56},{56,64},{64,7... | collective-permute-start | bytes 184328 | tf_op jit(solution)/shard_map/ppermute | solution.py:16
  99.3 6.5 %collective-permute-start.15 = (bf16[40,2,3,128]{3,0,2,1:T(8,128)(2,1)S(1)}, bf16[40,2,3,128]{3,0,2,1:T(8,128)(2,1)S(1)}, u32[]{:S(2)}, u32[]{:S(2)}) collective-permute-start(bf16[40,2,3,128]{3,0,2,1:T(8,128)(2,1)S(1)} %collective-permute-done.14), channel_id=1, source_target_pairs={{0,120},{8,0},{16,8},{24,16},{32,24},{40,32},{48,40},{56,48},{64,5... | collective-permute-start | bytes 184328 | tf_op jit(solution)/shard_map/ppermute | solution.py:16
  103.9 6.2 %collective-permute-start.8 = (bf16[40,2,3,128]{3,0,2,1:T(8,128)(2,1)S(1)}, bf16[40,2,3,128]{3,0,2,1:T(8,128)(2,1)S(1)}, u32[]{:S(2)}, u32[]{:S(2)}) collective-permute-start(bf16[40,2,3,128]{3,0,2,1:T(8,128)(2,1)S(1)} %collective-permute-done.7), channel_id=1, source_target_pairs={{0,8},{8,16},{16,24},{24,32},{32,40},{40,48},{48,56},{56,64},{64,7... | collective-permute-start | bytes 184328 | tf_op jit(solution)/shard_map/ppermute | solution.py:16
  105.9 26.4 %collective-permute-start.18 = (bf16[32,3,128]{2,0,1:T(8,128)(2,1)S(1)}, bf16[32,3,128]{2,0,1:T(8,128)(2,1)S(1)}, u32[]{:S(2)}, u32[]{:S(2)}) collective-permute-start(bf16[32,3,128]{2,0,1:T(8,128)(2,1)S(1)} %convert_bitcast_fusion.2), channel_id=1, source_target_pairs={{128,0},{136,8},{144,16},{152,24},{160,32},{168,40},{176,48},{184,... | collective-permute-start | bytes 73736 | tf_op jit(solution)/shard_map/ppermute | solution.py:16
  110.1 5.0 %collective-permute-start.16 = (bf16[40,2,3,128]{3,0,2,1:T(8,128)(2,1)S(1)}, bf16[40,2,3,128]{3,0,2,1:T(8,128)(2,1)S(1)}, u32[]{:S(2)}, u32[]{:S(2)}) collective-permute-start(bf16[40,2,3,128]{3,0,2,1:T(8,128)(2,1)S(1)} %collective-permute-done.15), channel_id=1, source_target_pairs={{0,120},{8,0},{16,8},{24,16},{32,24},{40,32},{48,40},{56,48},{64,5... | collective-permute-start | bytes 184328 | tf_op jit(solution)/shard_map/ppermute | solution.py:16
  115.0 9.3 %collective-permute-start.9 = (bf16[40,2,3,128]{3,0,2,1:T(8,128)(2,1)S(1)}, bf16[40,2,3,128]{3,0,2,1:T(8,128)(2,1)S(1)}, u32[]{:S(2)}, u32[]{:S(2)}) collective-permute-start(bf16[40,2,3,128]{3,0,2,1:T(8,128)(2,1)S(1)} %collective-permute-done.8), channel_id=1, source_target_pairs={{0,8},{8,16},{16,24},{24,32},{32,40},{40,48},{48,56},{56,64},{64,7... | collective-permute-start | bytes 184328 | tf_op jit(solution)/shard_map/ppermute | solution.py:16
  117.0 13.6 %collective-permute-start.17 = (bf16[40,2,3,128]{3,0,2,1:T(8,128)(2,1)S(1)}, bf16[40,2,3,128]{3,0,2,1:T(8,128)(2,1)S(1)}, u32[]{:S(2)}, u32[]{:S(2)}) collective-permute-start(bf16[40,2,3,128]{3,0,2,1:T(8,128)(2,1)S(1)} %collective-permute-done.16), channel_id=1, source_target_pairs={{0,120},{8,0},{16,8},{24,16},{32,24},{40,32},{48,40},{56,48},{64,5... | collective-permute-start | bytes 184328 | tf_op jit(solution)/shard_map/ppermute | solution.py:16
  124.3 6.3 %collective-permute-start.10 = (bf16[40,2,3,128]{3,0,2,1:T(8,128)(2,1)S(1)}, bf16[40,2,3,128]{3,0,2,1:T(8,128)(2,1)S(1)}, u32[]{:S(2)}, u32[]{:S(2)}) collective-permute-start(bf16[40,2,3,128]{3,0,2,1:T(8,128)(2,1)S(1)} %collective-permute-done.9), channel_id=1, source_target_pairs={{0,8},{8,16},{16,24},{24,32},{32,40},{40,48},{48,56},{56,64},{64,7... | collective-permute-start | bytes 184328 | tf_op jit(solution)/shard_map/ppermute | solution.py:16
  134.0 15.9 %collective-permute-start.27 = (f32[8,3,129]{2,0,1:T(8,128)S(1)}, f32[8,3,129]{2,0,1:T(8,128)S(1)}, u32[]{:S(2)}, u32[]{:S(2)}) collective-permute-start(f32[8,3,129]{2,0,1:T(8,128)S(1)} %pad_maximum_fusion.2), channel_id=1, source_target_pairs={{0,128},{8,136},{16,144},{24,152},{32,160},{40,168},{48,176},{56,1... | collective-permute-start | bytes 37160 | tf_op jit(solution)/shard_map/ppermute | solution.py:16
  137.1 14.3 %collective-permute-start.28 = (f32[8,3,129]{2,0,1:T(8,128)S(1)}, f32[8,3,129]{2,0,1:T(8,128)S(1)}, u32[]{:S(2)}, u32[]{:S(2)}) collective-permute-start(f32[8,3,129]{2,0,1:T(8,128)S(1)} %pad_maximum_fusion.3), channel_id=1, source_target_pairs={{0,256},{8,264},{16,272},{24,280},{32,288},{40,296},{48,304},{56,3... | collective-permute-start | bytes 37160 | tf_op jit(solution)/shard_map/ppermute | solution.py:16
  141.5 11.2 %collective-permute-start.29 = (f32[8,3,129]{2,0,1:T(8,128)S(1)}, f32[8,3,129]{2,0,1:T(8,128)S(1)}, u32[]{:S(2)}, u32[]{:S(2)}) collective-permute-start(f32[8,3,129]{2,0,1:T(8,128)S(1)} %pad_maximum_fusion.4), channel_id=1, source_target_pairs={{0,384},{8,392},{16,400},{24,408},{32,416},{40,424},{48,432},{56,4... | collective-permute-start | bytes 37160 | tf_op jit(solution)/shard_map/ppermute | solution.py:16
  144.4 9.7 %collective-permute-start.30 = (f32[8,3,129]{2,0,1:T(8,128)S(1)}, f32[8,3,129]{2,0,1:T(8,128)S(1)}, u32[]{:S(2)}, u32[]{:S(2)}) collective-permute-start(f32[8,3,129]{2,0,1:T(8,128)S(1)} %pad_maximum_fusion.5), channel_id=1, source_target_pairs={{0,512},{8,520},{16,528},{24,536},{32,544},{40,552},{48,560},{56,5... | collective-permute-start | bytes 37160 | tf_op jit(solution)/shard_map/ppermute | solution.py:16
  148.3 5.9 %collective-permute-start.31 = (f32[8,3,129]{2,0,1:T(8,128)S(1)}, f32[8,3,129]{2,0,1:T(8,128)S(1)}, u32[]{:S(2)}, u32[]{:S(2)}) collective-permute-start(f32[8,3,129]{2,0,1:T(8,128)S(1)} %pad_maximum_fusion.6), channel_id=1, source_target_pairs={{0,640},{8,648},{16,656},{24,664},{32,672},{40,680},{48,688},{56,6... | collective-permute-start | bytes 37160 | tf_op jit(solution)/shard_map/ppermute | solution.py:16
  149.9 4.4 %collective-permute-start.32 = (f32[8,3,129]{2,0,1:T(8,128)S(1)}, f32[8,3,129]{2,0,1:T(8,128)S(1)}, u32[]{:S(2)}, u32[]{:S(2)}) collective-permute-start(f32[8,3,129]{2,0,1:T(8,128)S(1)} %pad_maximum_fusion.7), channel_id=1, source_target_pairs={{0,768},{8,776},{16,784},{24,792},{32,800},{40,808},{48,816},{56,8... | collective-permute-start | bytes 37160 | tf_op jit(solution)/shard_map/ppermute | solution.py:16
  151.3 3.1 %collective-permute-start.33 = (f32[8,3,129]{2,0,1:T(8,128)S(1)}, f32[8,3,129]{2,0,1:T(8,128)S(1)}, u32[]{:S(2)}, u32[]{:S(2)}) collective-permute-start(f32[8,3,129]{2,0,1:T(8,128)S(1)} %pad_maximum_fusion.8), channel_id=1, source_target_pairs={{0,896},{8,904},{16,912},{24,920},{32,928},{40,936},{48,944},{56,9... | collective-permute-start | bytes 37160 | tf_op jit(solution)/shard_map/ppermute | solution.py:16
  152.7 3.1 %collective-permute-start.19 = (f32[32,3,129]{2,0,1:T(8,128)S(1)}, f32[32,3,129]{2,0,1:T(8,128)S(1)}, u32[]{:S(2)}, u32[]{:S(2)}) collective-permute-start(f32[32,3,129]{2,0,1:T(8,128)S(1)} %pad_maximum_fusion.1), channel_id=1, source_target_pairs={{0,128},{8,136},{16,144},{24,152},{32,160},{40,168},{48,176},{56,1... | collective-permute-start | bytes 148616 | tf_op jit(solution)/shard_map/ppermute | solution.py:16
Sparse Core Ops, SparseCore 0:
  157.7 36.9 all-gather.1

commit v2 on v1

--- a/solution.py
+++ b/solution.py
@@ -7,13 +7,10 @@
 RATE_TOP = 32
 SEG_ROWS = 1024
 ROW = 16
+TOK_DEV = 256
 
 
 NEG_FILL = -1e30
-
-
-def send(array, pairs):
-    return lax.ppermute(array, "seq", pairs)
 
 
 def pick_rows(states, chooser, spacing):
@@ -82,20 +79,21 @@
     return packed[..., :-1], packed[..., -1]
 
 
-def ring_gather(block, seq_count):
-    forward = [(s, (s // ROW) * ROW + (s % ROW + 1) % ROW) for s in range(seq_count)]
-    backward = [(s, (s // ROW) * ROW + (s % ROW - 1) % ROW) for s in range(seq_count)]
-    ahead = [None] * ROW
-    ahead[0] = block
-    moving = block
-    for step in range(1, ROW // 2 + 1):
-        moving = send(moving, forward)
-        ahead[step] = moving
-    moving = block
-    for step in range(1, ROW // 2):
-        moving = send(moving, backward)
-        ahead[ROW - step] = moving
-    return jnp.stack(ahead)
+SEQ_AXES = ("sy", "sz")
+ROW_AXES = "sz"
+
+
+def split3(value):
+    high = value.astype(jnp.bfloat16)
+    rest = value - high.astype(jnp.float32)
+    middle = rest.astype(jnp.bfloat16)
+    low = (rest - middle.astype(jnp.float32)).astype(jnp.bfloat16)
+    return jnp.stack([high, middle, low], axis=-1)
+
+
+def join3(parts):
+    parts = parts.astype(jnp.float32)
+    return parts[..., 0] + parts[..., 1] + parts[..., 2]
 
 
 def local(queries, key_states, value_states, level_offsets, out_weight):
@@ -103,11 +101,12 @@
     head_count = level_offsets.shape[1]
     head_width = queries.shape[1] // head_count
     scale_factor = head_width ** (-0.5)
-    seq_count = lax.axis_size("seq")
-    seq_index = lax.axis_index("seq")
-    row_y = seq_index // ROW
-    row_z = seq_index % ROW
-    rows_total = seq_count // ROW
+    rows_total = lax.axis_size("sy")
+    row_len = lax.axis_size("sz")
+    seq_count = rows_total * row_len
+    row_y = lax.axis_index("sy")
+    row_z = lax.axis_index("sz")
+    seq_index = row_y * row_len + row_z
     query_all = queries.reshape(row_count, head_count, head_width)
     key_all = key_states.reshape(row_count, head_count, head_width)
     value_all = value_states.reshape(row_count, head_count, head_width)
@@ -119,7 +118,7 @@
     arrived = []
     for shift in range(span0 - 1, 0, -1):
         pairs = [(s, s + shift) for s in range(seq_count) if s % span0 + shift < span0]
-        arrived.append(send(pair0, pairs))
+        arrived.append(lax.ppermute(pair0, SEQ_AXES, pairs))
     buffer0 = jnp.concatenate(arrived + [pair0], axis=0)
     shape0 = (row_count, span0 * row_count)
     key_index = lax.broadcasted_iota(jnp.int32, shape0, 1)
@@ -135,30 +134,30 @@
     chooser2, query2, pair2 = level_setup(query_all, key_all, value_all, level_offsets[2], RATE_TOP)
     count1 = pair1.shape[0]
     count2 = pair2.shape[0]
-    ring = ring_gather(jnp.concatenate([pair1, pair2], axis=0), seq_count)
+    ring = lax.all_gather(jnp.concatenate([pair1, pair2], axis=0), ROW_AXES)
     row1 = ring[:, :count1]
     row2 = ring[:, count1:]
 
     def own_row(query_rows, row_blocks, count):
-        keys = row_blocks.reshape(ROW * count, 2, head_count, head_width)
-        shape = (count, ROW * count)
+        keys = row_blocks.reshape(row_len * count, 2, head_count, head_width)
+        shape = (count, row_len * count)
         key_index = lax.broadcasted_iota(jnp.int32, shape, 1)
         query_index = lax.broadcasted_iota(jnp.int32, shape, 0)
-        offset = key_index // count
+        source = key_index // count
         allowed = jnp.where(
-            offset == 0, key_index % count <= query_index, offset <= row_z
+            source == row_z, key_index % count <= query_index, source < row_z
         )
         return attend(query_rows, keys[:, 0], keys[:, 1], allowed, scale_factor)
 
     def whole_row(query_rows, row_blocks, count):
-        keys = row_blocks.reshape(ROW * count, 2, head_count, head_width)
+        keys = row_blocks.reshape(row_len * count, 2, head_count, head_width)
         return attend(query_rows, keys[:, 0], keys[:, 1], None, scale_factor)
 
-    up = [(s, s - ROW) for s in range(seq_count) if (s // ROW) % 2 == 1]
-    down = [(s, s + ROW) for s in range(seq_count) if (s // ROW) % 2 == 0]
-    visiting1 = send(query1, up)
+    up = [(s, s - row_len) for s in range(seq_count) if (s // row_len) % 2 == 1]
+    down = [(s, s + row_len) for s in range(seq_count) if (s // row_len) % 2 == 0]
+    visiting1 = lax.ppermute(query1, SEQ_AXES, up)
     own_out1, own_lse1 = own_row(query1, row1, count1)
-    cross1 = send(pack(*whole_row(visiting1, row1, count1)), down)
+    cross1 = lax.ppermute(pack(*whole_row(visiting1, row1, count1)), SEQ_AXES, down)
     cross_out1, cross_lse1 = unpack(cross1)
     cross_lse1 = jnp.where(row_y % 2 == 1, cross_lse1, NEG_FILL)
     out1, lse1 = merge([own_out1, cross_out1], [own_lse1, cross_lse1])
@@ -167,21 +166,17 @@
     full_lses.append(full_lse)
 
     own_out2, own_lse2 = own_row(query2, row2, count2)
-    visiting = []
-    for gap in range(1, rows_total):
-        pairs = [(s, s - gap * ROW) for s in range(seq_count) if s // ROW >= gap]
-        visiting.append(send(query2, pairs))
-    visiting2 = jnp.concatenate(visiting, axis=0)
-    cross_out, cross_lse = whole_row(visiting2, row2, count2)
-    outs2 = [own_out2]
-    lses2 = [own_lse2]
-    for gap in range(1, rows_total):
-        pairs = [(s, s + gap * ROW) for s in range(seq_count) if s // ROW + gap < rows_total]
-        part = slice((gap - 1) * count2, gap * count2)
-        back_out, back_lse = unpack(send(pack(cross_out[part], cross_lse[part]), pairs))
-        outs2.append(back_out)
-        lses2.append(jnp.where(row_y >= gap, back_lse, NEG_FILL))
-    out2, lse2 = merge(outs2, lses2)
+    column_queries = lax.all_gather(query2, "sy", tiled=True)
+    cross_out, cross_lse = whole_row(column_queries, row2, count2)
+    packed = pack(cross_out, cross_lse).reshape(rows_total, count2, head_count, head_width + 1)
+    returned = lax.all_to_all(packed, "sy", 0, 0, tiled=True)
+    back_out, back_lse = unpack(returned)
+    source_row = lax.broadcasted_iota(jnp.int32, back_lse.shape, 0)
+    back_lse = jnp.where(source_row < row_y, back_lse, NEG_FILL)
+    out2, lse2 = merge(
+        [own_out2] + [back_out[i] for i in range(rows_total)],
+        [own_lse2] + [back_lse[i] for i in range(rows_total)],
+    )
     full_out, full_lse = spread_back(out2, lse2, chooser2)
     full_outs.append(full_out)
     full_lses.append(full_lse)
@@ -203,16 +198,20 @@
 
 
 def solution(mesh):
+    seq_count, head_count = mesh.devices.shape
+    split = jax.sharding.Mesh(
+        mesh.devices.reshape(seq_count // ROW, ROW, head_count), SEQ_AXES + ("head",)
+    )
     return jax.shard_map(
         local,
-        mesh=mesh,
+        mesh=split,
         in_specs=(
-            P("seq", "head"),
-            P("seq", "head"),
-            P("seq", "head"),
+            P(SEQ_AXES, "head"),
+            P(SEQ_AXES, "head"),
+            P(SEQ_AXES, "head"),
             P(None, "head"),
             P(None, "head"),
         ),
-        out_specs=P("seq", "head"),
+        out_specs=P(SEQ_AXES, "head"),
         check_vma=False,
     )

time: 207 us -> 161 us (0.78)
  starting transfers between devices: 98.3 us -> 23.2 us
  blocking collectives: 0 us -> 58.9 us
  waiting for transfers between devices: 69.7 us -> 41.9 us
  matrix products: 12.5 us -> 9.66 us
    ppermute x34 -> x5, starting transfers between devices: 98.3 us -> 17.3 us  [the longest x3 13.4 us: local(): arrived.append(lax.ppermute(pair0, SEQ_AXES, pairs))]
    all_gather x0 -> x2, blocking collectives: none -> 58.9 us  [the longest x1 40.4 us: local(): ring = lax.all_gather(jnp.concatenate([pair1, pair2], axis=0), ROW_AXES)]
    ppermute x34 -> x5, waiting for transfers between devices: 32.6 us -> 3.37 us  [the longest x1 1.97 us: local(): lax.ppermute(pack(*whole_row(visiting1, row1, count1)), SEQ_AXES, down)]
    all_to_all x0 -> x1, starting transfers between devices: none -> 5.82 us  [local(): returned = lax.all_to_all(packed, 'sy', 0, 0, tiled=True)]
    dot_general x6, matrix products: 3.77 us -> 0.98 us  [pick_rows(): jnp.einsum('nrhd,rh->nhd', grouped, chooser, preferred_element_type=jnp.f...]
  transfers between devices with their start and end apart: 35 -> 7, of which waited for: 11 -> 3; matrix products, arithmetic and copies ran while one was open for 5% -> 6% of each run, Pallas kernels for 0% -> 0%
where the time goes in v2:
time: 161 us
  blocking collectives  58.9 us (37%)
  waiting for transfers between devices  41.9 us (26%)
  starting transfers between devices  23.2 us (14%)
  between operations  14 us (9%)
  matrix products  9.66 us (6%)
  local copies, waits for them, and re-layouts  6.57 us (4%)
  other arithmetic  6.43 us (4%)
    all_gather x1, blocking collectives, local(): ring = lax.all_gather(jnp.concatenate([pair1, pair2], axis=0), ROW_AXES)  40.4 us
    all_gather x1, waiting for transfers between devices, local(): lax.all_gather(heads_out, 'head', axis=1, tiled=True)  38.5 us
    all_gather x1, blocking collectives, local(): column_queries = lax.all_gather(query2, 'sy', tiled=True)  18.5 us
    ppermute x3, starting transfers between devices, local(): arrived.append(lax.ppermute(pair0, SEQ_AXES, pairs))  13.4 us
    all_to_all x1, starting transfers between devices, local(): returned = lax.all_to_all(packed, 'sy', 0, 0, tiled=True)  5.82 us
    dot_general x1, matrix products, local(): jnp.dot(lax.all_gather(heads_out, 'head', axis=1, tiled=True), out_weight...  4.73 us
  transfers between devices with their start and end apart: 7, of which 3 were waited for; matrix products, arithmetic and copies ran while one was open for 6% of the time, Pallas kernels for 0%

profile of v2, /device:TPU:1, one launch (start us, length us, event | category | flops | bytes accessed | tf_op | source)
XLA Modules:
  0.0 160.6 jit_solution(8187564020631268077)
XLA Ops:
  6.5 1.1 copy.51
  7.7 0.2 copy.53
  7.8 1.1 copy.50
  8.9 0.2 copy.52
  9.1 0.8 pad_maximum_fusion
  9.9 4.8 %collective-permute-start.2 = (bf16[256,2,3,128]{3,0,2,1:T(8,128)(2,1)}, bf16[256,2,3,128]{3,0,2,1:T(8,128)(2,1)S(1)}, u32[]{:S(2)}, u32[]{:S(2)}) collective-permute-start(bf16[256,2,3,128]{3,0,2,1:T(8,128)(2,1)} %pad_maximum_fusion), channel_id=1, source_target_pairs={{0,8},{8,16},{16,24},{32,40},{40,48},{48,56},{64,72},{72,80},{80,8... | collective-permute-start | bytes 1179656 | tf_op jit(solution)/shard_map/ppermute | solution.py:121
  14.7 6.5 %collective-permute-start.1 = (bf16[256,2,3,128]{3,0,2,1:T(8,128)(2,1)}, bf16[256,2,3,128]{3,0,2,1:T(8,128)(2,1)}, u32[]{:S(2)}, u32[]{:S(2)}) collective-permute-start(bf16[256,2,3,128]{3,0,2,1:T(8,128)(2,1)} %pad_maximum_fusion), channel_id=1, source_target_pairs={{0,16},{8,24},{32,48},{40,56},{64,80},{72,88},{96,112},{104,120},{... | collective-permute-start | bytes 1179656 | tf_op jit(solution)/shard_map/ppermute | solution.py:121
  21.2 2.0 %collective-permute-start = (bf16[256,2,3,128]{3,0,2,1:T(8,128)(2,1)}, bf16[256,2,3,128]{3,0,2,1:T(8,128)(2,1)}, u32[]{:S(2)}, u32[]{:S(2)}) collective-permute-start(bf16[256,2,3,128]{3,0,2,1:T(8,128)(2,1)} %pad_maximum_fusion), channel_id=1, source_target_pairs={{0,24},{32,56},{64,88},{96,120},{128,152},{160,184},{192,216},{224... | collective-permute-start | bytes 1179656 | tf_op jit(solution)/shard_map/ppermute | solution.py:121
  23.3 1.0 reshape_reshape.25
  24.3 1.0 reshape_reshape.24
  25.4 0.2 fusion.15
  25.6 0.2 fusion.17
  25.9 0.1 fusion.9
  26.0 18.5 %all_gather.14 = bf16[64,3,128]{2,0,1:T(8,128)(2,1)S(1)} all-gather(bf16[8,3,128]{2,0,1:T(8,128)(2,1)S(1)} %convert_bitcast_fusion.3), channel_id=1, replica_groups=mesh['sy'=8,'sz'=16,'head'=8] {'sy'}, dimensions={0}, use_global_device_ids=true | all-gather | bytes 55296 | tf_op jit(solution)/shard_map/all_gather | solution.py:169
  44.7 0.1 fusion.13
  44.8 40.4 %all-gather = bf16[640,2,3,128]{3,0,2,1:T(8,128)(2,1)S(1)} all-gather(bf16[40,2,3,128]{3,0,2,1:T(8,128)(2,1)S(1)} %maximum_maximum_fusion.1), channel_id=2, replica_groups=mesh['sy'=8,'sz'=16,'head'=8] {'sz'}, dimensions={0}, use_global_device_ids=true | all-gather | bytes 1044480 | tf_op jit(solution)/shard_map/all_gather | solution.py:137
  85.3 0.3 fusion.76
  85.6 0.2 fusion.29
  85.8 0.2 convolution_bitcast_fusion
  86.1 0.2 copy.59
  86.3 0.7 pad_maximum_fusion.1
  87.0 5.8 %all-to-all-start = ((f32[8,8,3,129]{3,1,2,0:T(8,128)}), f32[8,8,3,129]{3,1,2,0:T(8,128)S(1)}, u32[]{:S(2)}, u32[]{:S(2)}) async-start(f32[8,8,3,129]{3,1,2,0:T(8,128)} %pad_maximum_fusion.1), calls=%async_computation | async-start | bytes 393216 | tf_op jit(solution)/shard_map/all_to_all | solution.py:172
  92.9 0.2 fusion.19
  93.1 1.3 collective-permute-start.3
  94.6 0.3 fusion.79
  94.9 0.2 fusion.21
  95.1 0.2 convolution_bitcast_fusion.1
  95.4 0.2 fusion.77
  95.7 0.2 fusion.40
  95.9 0.2 fusion.7
  96.1 0.2 convolution_bitcast_fusion.3
  96.3 1.4 collective-permute-done.3
  97.7 0.3 fusion.78
  98.0 0.2 fusion.22
  98.2 0.2 convolution_bitcast_fusion.2
  98.6 2.6 %collective-permute-start.4 = (f32[32,3,129]{2,0,1:T(8,128)S(1)}, f32[32,3,129]{2,0,1:T(8,128)S(1)}, u32[]{:S(2)}, u32[]{:S(2)}) collective-permute-start(f32[32,3,129]{2,0,1:T(8,128)S(1)} %pad_maximum_fusion.2), channel_id=1, source_target_pairs={{0,128},{8,136},{16,144},{24,152},{32,160},{40,168},{48,176},{56,1... | collective-permute-start | bytes 148616 | tf_op jit(solution)/shard_map/ppermute | solution.py:160
  101.2 0.1 copy.54
  101.6 2.0 %collective-permute-done.4 = f32[32,3,129]{2,0,1:T(8,128)S(1)} collective-permute-done((f32[32,3,129]{2,0,1:T(8,128)S(1)}, f32[32,3,129]{2,0,1:T(8,128)S(1)}, u32[]{:S(2)}, u32[]{:S(2)}) %collective-permute-start.4) | collective-permute-done | bytes 49568 | tf_op jit(solution)/shard_map/ppermute | solution.py:160
  104.2 0.2 copy.64
  104.4 0.2 copy.88
  105.5 0.2 copy.69
  105.8 1.2 maximum_maximum_fusion
  107.0 0.7 fusion.1
  107.7 0.7 fusion
  108.4 1.2 fusion.3
  109.8 0.7 divide_convert_fusion.4
  110.5 38.5 %all-gather.3.cloned.1.call-done = bf16[256,3072]{0,1:T(8,128)(2,1)} async-done(((bf16[256,384]{0,1:T(8,128)(2,1)}), bf16[256,3072]{0,1:T(8,128)(2,1)}) %all-gather.3.cloned.1.call-update) | async-done | bytes 1572880 | tf_op jit(solution)/shard_map/all_gather | solution.py:193
  149.0 4.7 %convolution_convert_fusion = bf16[256,640]{1,0:T(8,128)(2,1)} fusion(bf16[256,3072]{0,1:T(8,128)(2,1)} %all-gather.3.cloned.1.call-done, bf16[3072,640]{1,0:T(8,128)(2,1)} %param.9), kind=kOutput, calls=%fused_computation.7 | convolution fusion | flops 1006796800 | bytes 5832704 | tf_op jit(solution)/shard_map/dot_general | solution.py:192
  (82 shorter events, 2.7 us)
Async XLA Ops:
  6.5 18.8 %copy-start = (bf16[256,384]{1,0:T(8,128)(2,1)S(1)}, bf16[256,384]{1,0:T(8,128)(2,1)}, u32[]{:S(2)}) copy-start(bf16[256,384]{1,0:T(8,128)(2,1)} %param.7) | copy-start | bytes 589828
  6.5 19.0 %copy-start.1 = (bf16[256,384]{1,0:T(8,128)(2,1)S(1)}, bf16[256,384]{1,0:T(8,128)(2,1)}, u32[]{:S(2)}) copy-start(bf16[256,384]{1,0:T(8,128)(2,1)} %param.6) | copy-start | bytes 589828
  6.5 18.7 %copy-start.3 = (s32[3,3]{1,0:T(4,128)S(1)}, s32[3,3]{1,0:T(4,128)}, u32[]{:S(2)}) copy-start(s32[3,3]{1,0:T(4,128)} %param.8) | copy-start | bytes 112
  6.5 19.2 %copy-start.2 = (bf16[256,384]{1,0:T(8,128)(2,1)S(1)}, bf16[256,384]{1,0:T(8,128)(2,1)}, u32[]{:S(2)}) copy-start(bf16[256,384]{1,0:T(8,128)(2,1)} %param.5) | copy-start | bytes 589828
  9.9 95.9 %collective-permute-start.2 = (bf16[256,2,3,128]{3,0,2,1:T(8,128)(2,1)}, bf16[256,2,3,128]{3,0,2,1:T(8,128)(2,1)S(1)}, u32[]{:S(2)}, u32[]{:S(2)}) collective-permute-start(bf16[256,2,3,128]{3,0,2,1:T(8,128)(2,1)} %pad_maximum_fusion), channel_id=1, source_target_pairs={{0,8},{8,16},{16,24},{32,40},{40,48},{48,56},{64,72},{72,80},{80,8... | collective-permute-start | bytes 1179656 | tf_op jit(solution)/shard_map/ppermute | solution.py:121
  14.7 91.1 %collective-permute-start.1 = (bf16[256,2,3,128]{3,0,2,1:T(8,128)(2,1)}, bf16[256,2,3,128]{3,0,2,1:T(8,128)(2,1)}, u32[]{:S(2)}, u32[]{:S(2)}) collective-permute-start(bf16[256,2,3,128]{3,0,2,1:T(8,128)(2,1)} %pad_maximum_fusion), channel_id=1, source_target_pairs={{0,16},{8,24},{32,48},{40,56},{64,80},{72,88},{96,112},{104,120},{... | collective-permute-start | bytes 1179656 | tf_op jit(solution)/shard_map/ppermute | solution.py:121
  21.2 84.5 %collective-permute-start = (bf16[256,2,3,128]{3,0,2,1:T(8,128)(2,1)}, bf16[256,2,3,128]{3,0,2,1:T(8,128)(2,1)}, u32[]{:S(2)}, u32[]{:S(2)}) collective-permute-start(bf16[256,2,3,128]{3,0,2,1:T(8,128)(2,1)} %pad_maximum_fusion), channel_id=1, source_target_pairs={{0,24},{32,56},{64,88},{96,120},{128,152},{160,184},{192,216},{224... | collective-permute-start | bytes 1179656 | tf_op jit(solution)/shard_map/ppermute | solution.py:121
  87.0 17.4 %all-to-all-start = ((f32[8,8,3,129]{3,1,2,0:T(8,128)}), f32[8,8,3,129]{3,1,2,0:T(8,128)S(1)}, u32[]{:S(2)}, u32[]{:S(2)}) async-start(f32[8,8,3,129]{3,1,2,0:T(8,128)} %pad_maximum_fusion.1), calls=%async_computation | async-start | bytes 393216 | tf_op jit(solution)/shard_map/all_to_all | solution.py:172
  92.9 56.1 %all-gather.3.cloned.1.call-start = ((), (), s32[]{:S(2)}) async-start(), calls=%async_computation.1 | async-start | bytes 1769472 | tf_op jit(solution)/shard_map/all_gather | solution.py:193
  93.1 4.6 %collective-permute-start.3 = (bf16[32,3,128]{2,0,1:T(8,128)(2,1)S(1)}, bf16[32,3,128]{2,0,1:T(8,128)(2,1)S(1)}, u32[]{:S(2)}, u32[]{:S(2)}) collective-permute-start(bf16[32,3,128]{2,0,1:T(8,128)(2,1)S(1)} %convert_bitcast_fusion.2), channel_id=1, source_target_pairs={{128,0},{136,8},{144,16},{152,24},{160,32},{168,40},{176,48},{184,... | collective-permute-start | bytes 73736 | tf_op jit(solution)/shard_map/ppermute | solution.py:158
  98.6 5.0 %collective-permute-start.4 = (f32[32,3,129]{2,0,1:T(8,128)S(1)}, f32[32,3,129]{2,0,1:T(8,128)S(1)}, u32[]{:S(2)}, u32[]{:S(2)}) collective-permute-start(f32[32,3,129]{2,0,1:T(8,128)S(1)} %pad_maximum_fusion.2), channel_id=1, source_target_pairs={{0,128},{8,136},{16,144},{24,152},{32,160},{40,168},{48,176},{56,1... | collective-permute-start | bytes 148616 | tf_op jit(solution)/shard_map/ppermute | solution.py:160
Sparse Core Ops, SparseCore 0:
  110.7 38.3 all-gather.2

commit v3 on v2

--- a/solution.py
+++ b/solution.py
@@ -166,9 +166,15 @@
     full_lses.append(full_lse)
 
     own_out2, own_lse2 = own_row(query2, row2, count2)
-    column_queries = lax.all_gather(query2, "sy", tiled=True)
-    cross_out, cross_lse = whole_row(column_queries, row2, count2)
+    visiting = [query2]
+    for gap in range(1, rows_total):
+        pairs = [(s, s - gap * row_len) for s in range(seq_count) if s // row_len >= gap]
+        visiting.append(lax.ppermute(query2, SEQ_AXES, pairs))
+    cross_out, cross_lse = whole_row(jnp.concatenate(visiting, axis=0), row2, count2)
     packed = pack(cross_out, cross_lse).reshape(rows_total, count2, head_count, head_width + 1)
+    doubled = jnp.concatenate([packed, packed], axis=0)
+    start = (rows_total - row_y) % rows_total
+    packed = lax.dynamic_slice_in_dim(doubled, start, rows_total, axis=0)
     returned = lax.all_to_all(packed, "sy", 0, 0, tiled=True)
     back_out, back_lse = unpack(returned)
     source_row = lax.broadcasted_iota(jnp.int32, back_lse.shape, 0)

time: 161 us -> 156 us (0.969)
  blocking collectives: 58.9 us -> 42.3 us
  starting transfers between devices: 23.2 us -> 28.5 us
  waiting for transfers between devices: 41.9 us -> 46.2 us
  matrix products: 9.66 us -> 11.6 us
    all_gather x1 -> x0, blocking collectives: 18.5 us -> none  [local(): column_queries = lax.all_gather(query2, 'sy', tiled=True)]
    ppermute x0 -> x7, starting transfers between devices: none -> 9.04 us  [local(): visiting.append(lax.ppermute(query2, SEQ_AXES, pairs))]
    all_to_all x1, waiting for transfers between devices: 0.01 us -> 8.46 us  [local(): returned = lax.all_to_all(packed, 'sy', 0, 0, tiled=True)]
    ppermute x3, starting transfers between devices: 13.4 us -> 6.88 us  [local(): arrived.append(lax.ppermute(pair0, SEQ_AXES, pairs))]
    all_gather x1, waiting for transfers between devices: 38.5 us -> 36 us  [local(): lax.all_gather(heads_out, 'head', axis=1, tiled=True)]
    ppermute x1, waiting for transfers between devices: 1.97 us -> 0.01 us  [local(): lax.ppermute(pack(*whole_row(visiting1, row1, count1)), SEQ_AXES, down)]
    dot_general x6, matrix products: 0.98 us -> 2.85 us  [pick_rows(): jnp.einsum('nrhd,rh->nhd', grouped, chooser, preferred_element_type=jnp.f...]
    unnamed x13 -> x17, local copies, waits for them, and re-layouts: 2.68 us -> 0.83 us
  transfers between devices with their start and end apart: 7 -> 14, of which waited for: 3 -> 3; matrix products, arithmetic and copies ran while one was open for 6% -> 8% of each run, Pallas kernels for 0% -> 0%
where the time goes in v3:
time: 156 us
  waiting for transfers between devices  46.2 us (30%)
  blocking collectives  42.3 us (27%)
  starting transfers between devices  28.5 us (18%)
  between operations  14.1 us (9%)
  matrix products  11.6 us (7%)
  other arithmetic  7.19 us (5%)
  local copies, waits for them, and re-layouts  5.73 us (4%)
    all_gather x1, blocking collectives, local(): ring = lax.all_gather(jnp.concatenate([pair1, pair2], axis=0), ROW_AXES)  42.3 us
    all_gather x1, waiting for transfers between devices, local(): lax.all_gather(heads_out, 'head', axis=1, tiled=True)  36 us
    ppermute x7, starting transfers between devices, local(): visiting.append(lax.ppermute(query2, SEQ_AXES, pairs))  9.04 us
    all_to_all x1, waiting for transfers between devices, local(): returned = lax.all_to_all(packed, 'sy', 0, 0, tiled=True)  8.46 us
    all_to_all x1, starting transfers between devices, local(): returned = lax.all_to_all(packed, 'sy', 0, 0, tiled=True)  7.54 us
    ppermute x3, starting transfers between devices, local(): arrived.append(lax.ppermute(pair0, SEQ_AXES, pairs))  6.88 us
    dot_general x1, matrix products, local(): jnp.dot(lax.all_gather(heads_out, 'head', axis=1, tiled=True), out_weight...  4.73 us
    ppermute x1, starting transfers between devices, local(): lax.ppermute(pack(*whole_row(visiting1, row1, count1)), SEQ_AXES, down)  3.72 us
  transfers between devices with their start and end apart: 14, of which 3 were waited for; matrix products, arithmetic and copies ran while one was open for 8% of the time, Pallas kernels for 0%

profile of v3, /device:TPU:1, one launch (start us, length us, event | category | flops | bytes accessed | tf_op | source)
XLA Modules:
  0.0 155.5 jit_solution(4323745370231982354)
XLA Ops:
  6.5 1.1 reshape_reshape.26
  7.6 0.8 fusion.64
  8.6 1.3 collective-permute-start.5
  9.9 1.3 collective-permute-start.6
  11.2 1.3 collective-permute-start.7
  12.5 1.3 collective-permute-start.8
  13.8 1.3 collective-permute-start.9
  15.1 1.0 reshape_reshape.25
  16.1 1.0 reshape_reshape.24
  17.1 1.1 fusion.18
  18.3 1.1 fusion.20
  19.8 42.3 %all-gather = bf16[640,2,3,128]{3,0,2,1:T(8,128)(2,1)S(1)} all-gather(bf16[40,2,3,128]{3,0,2,1:T(8,128)(2,1)S(1)} %maximum_maximum_fusion.1), channel_id=2, replica_groups=mesh['sy'=8,'sz'=16,'head'=8] {'sz'}, dimensions={0}, use_global_device_ids=true | all-gather | bytes 1044480 | tf_op jit(solution)/shard_map/all_gather | solution.py:137
  62.1 0.2 fusion.80
  62.5 0.2 convolution_bitcast_fusion.3
  62.7 0.2 fusion.22
  63.1 0.3 fusion.82
  63.4 0.2 fusion.24
  63.6 0.2 convolution_bitcast_fusion.1
  64.4 0.2 copy.52
  64.6 0.2 fusion.7
  64.8 0.8 pad_maximum_fusion
  65.9 1.3 collective-permute-start.10
  67.3 1.3 collective-permute-start.11
  68.6 1.3 collective-permute-start.3
  69.9 1.3 collective-permute-start.2
  71.3 3.5 %collective-permute-start.1 = (bf16[256,2,3,128]{3,0,2,1:T(8,128)(2,1)}, bf16[256,2,3,128]{3,0,2,1:T(8,128)(2,1)}, u32[]{:S(2)}, u32[]{:S(2)}) collective-permute-start(bf16[256,2,3,128]{3,0,2,1:T(8,128)(2,1)} %pad_maximum_fusion), channel_id=1, source_target_pairs={{0,16},{8,24},{32,48},{40,56},{64,80},{72,88},{96,112},{104,120},{... | collective-permute-start | bytes 1179656 | tf_op jit(solution)/shard_map/ppermute | solution.py:121
  74.8 1.7 %collective-permute-done.10 = bf16[8,3,128]{2,0,1:T(8,128)(2,1)S(1)} collective-permute-done((bf16[8,3,128]{2,0,1:T(8,128)(2,1)S(1)}, bf16[8,3,128]{2,0,1:T(8,128)(2,1)S(1)}, u32[]{:S(2)}, u32[]{:S(2)}) %collective-permute-start.10) | collective-permute-done | bytes 6176 | tf_op jit(solution)/shard_map/ppermute | solution.py:172
  76.5 2.0 %collective-permute-start = (bf16[256,2,3,128]{3,0,2,1:T(8,128)(2,1)}, bf16[256,2,3,128]{3,0,2,1:T(8,128)(2,1)}, u32[]{:S(2)}, u32[]{:S(2)}) collective-permute-start(bf16[256,2,3,128]{3,0,2,1:T(8,128)(2,1)} %pad_maximum_fusion), channel_id=1, source_target_pairs={{0,24},{32,56},{64,88},{96,120},{128,152},{160,184},{192,216},{224... | collective-permute-start | bytes 1179656 | tf_op jit(solution)/shard_map/ppermute | solution.py:121
  78.6 0.3 fusion.79
  78.9 0.2 fusion.32
  79.1 0.2 convolution_bitcast_fusion
  79.4 0.2 copy.59
  79.6 0.3 fusion.81
  79.9 0.2 fusion.25
  80.1 0.2 convolution_bitcast_fusion.2
  80.5 3.7 %collective-permute-start.4 = (f32[32,3,129]{2,0,1:T(8,128)S(1)}, f32[32,3,129]{2,0,1:T(8,128)S(1)}, u32[]{:S(2)}, u32[]{:S(2)}) collective-permute-start(f32[32,3,129]{2,0,1:T(8,128)S(1)} %pad_maximum_fusion.1), channel_id=1, source_target_pairs={{0,128},{8,136},{16,144},{24,152},{32,160},{40,168},{48,176},{56,1... | collective-permute-start | bytes 148616 | tf_op jit(solution)/shard_map/ppermute | solution.py:160
  84.2 0.7 fusion.10
  85.0 7.5 %all-to-all-start = ((f32[8,8,3,129]{3,1,2,0:T(8,128)}), f32[8,8,3,129]{3,1,2,0:T(8,128)S(1)}, u32[]{:S(2)}, u32[]{:S(2)}) async-start(f32[8,8,3,129]{3,1,2,0:T(8,128)} %fusion.10), calls=%async_computation | async-start | bytes 393216 | tf_op jit(solution)/shard_map/all_to_all | solution.py:178
  93.2 0.2 copy.64
  93.4 8.5 %all-to-all-done = f32[8,8,3,129]{3,1,2,0:T(8,128)S(1)} async-done(((f32[8,8,3,129]{3,1,2,0:T(8,128)}), f32[8,8,3,129]{3,1,2,0:T(8,128)S(1)}, u32[]{:S(2)}, u32[]{:S(2)}) %all-to-all-start) | async-done | bytes 99104 | tf_op jit(solution)/shard_map/all_to_all | solution.py:178
  101.9 0.2 copy.88
  103.2 1.2 maximum_maximum_fusion
  104.5 0.7 fusion.1
  105.2 0.7 fusion
  105.9 1.2 fusion.3
  107.3 0.7 divide_convert_fusion.4
  108.0 36.0 %all-gather.3.cloned.1.call-done = bf16[256,3072]{0,1:T(8,128)(2,1)} async-done(((bf16[256,384]{0,1:T(8,128)(2,1)}), bf16[256,3072]{0,1:T(8,128)(2,1)}) %all-gather.3.cloned.1.call-update) | async-done | bytes 1572880 | tf_op jit(solution)/shard_map/all_gather | solution.py:199
  143.9 4.7 %convolution_convert_fusion = bf16[256,640]{1,0:T(8,128)(2,1)} fusion(bf16[256,3072]{0,1:T(8,128)(2,1)} %all-gather.3.cloned.1.call-done, bf16[3072,640]{1,0:T(8,128)(2,1)} %param.9), kind=kOutput, calls=%fused_computation.7 | convolution fusion | flops 1006796800 | bytes 5832704 | tf_op jit(solution)/shard_map/dot_general | solution.py:198
  (100 shorter events, 4.0 us)
Async XLA Ops:
  6.5 56.2 %copy-start.2 = (bf16[256,384]{1,0:T(8,128)(2,1)S(1)}, bf16[256,384]{1,0:T(8,128)(2,1)}, u32[]{:S(2)}) copy-start(bf16[256,384]{1,0:T(8,128)(2,1)} %param.5) | copy-start | bytes 589828
  8.6 57.3 %collective-permute-start.5 = (bf16[8,3,128]{2,0,1:T(8,128)(2,1)S(1)}, bf16[8,3,128]{2,0,1:T(8,128)(2,1)S(1)}, u32[]{:S(2)}, u32[]{:S(2)}) collective-permute-start(bf16[8,3,128]{2,0,1:T(8,128)(2,1)S(1)} %get-tuple-element.12), channel_id=1, source_target_pairs={{128,0},{136,8},{144,16},{152,24},{160,32},{168,40},{176,48},{184,... | collective-permute-start | bytes 18440 | tf_op jit(solution)/shard_map/ppermute | solution.py:172
  9.9 57.4 %collective-permute-start.6 = (bf16[8,3,128]{2,0,1:T(8,128)(2,1)S(1)}, bf16[8,3,128]{2,0,1:T(8,128)(2,1)S(1)}, u32[]{:S(2)}, u32[]{:S(2)}) collective-permute-start(bf16[8,3,128]{2,0,1:T(8,128)(2,1)S(1)} %get-tuple-element.12), channel_id=1, source_target_pairs={{256,0},{264,8},{272,16},{280,24},{288,32},{296,40},{304,48},{312,... | collective-permute-start | bytes 18440 | tf_op jit(solution)/shard_map/ppermute | solution.py:172
  11.2 57.4 %collective-permute-start.7 = (bf16[8,3,128]{2,0,1:T(8,128)(2,1)S(1)}, bf16[8,3,128]{2,0,1:T(8,128)(2,1)S(1)}, u32[]{:S(2)}, u32[]{:S(2)}) collective-permute-start(bf16[8,3,128]{2,0,1:T(8,128)(2,1)S(1)} %get-tuple-element.12), channel_id=1, source_target_pairs={{384,0},{392,8},{400,16},{408,24},{416,32},{424,40},{432,48},{440,... | collective-permute-start | bytes 18440 | tf_op jit(solution)/shard_map/ppermute | solution.py:172
  12.5 57.4 %collective-permute-start.8 = (bf16[8,3,128]{2,0,1:T(8,128)(2,1)S(1)}, bf16[8,3,128]{2,0,1:T(8,128)(2,1)S(1)}, u32[]{:S(2)}, u32[]{:S(2)}) collective-permute-start(bf16[8,3,128]{2,0,1:T(8,128)(2,1)S(1)} %get-tuple-element.12), channel_id=1, source_target_pairs={{512,0},{520,8},{528,16},{536,24},{544,32},{552,40},{560,48},{568,... | collective-permute-start | bytes 18440 | tf_op jit(solution)/shard_map/ppermute | solution.py:172
  13.8 57.5 %collective-permute-start.9 = (bf16[8,3,128]{2,0,1:T(8,128)(2,1)S(1)}, bf16[8,3,128]{2,0,1:T(8,128)(2,1)S(1)}, u32[]{:S(2)}, u32[]{:S(2)}) collective-permute-start(bf16[8,3,128]{2,0,1:T(8,128)(2,1)S(1)} %get-tuple-element.12), channel_id=1, source_target_pairs={{640,0},{648,8},{656,16},{664,24},{672,32},{680,40},{688,48},{696,... | collective-permute-start | bytes 18440 | tf_op jit(solution)/shard_map/ppermute | solution.py:172
  19.7 44.2 %copy-start = (bf16[256,384]{1,0:T(8,128)(2,1)S(1)}, bf16[256,384]{1,0:T(8,128)(2,1)}, u32[]{:S(2)}) copy-start(bf16[256,384]{1,0:T(8,128)(2,1)} %param.7) | copy-start | bytes 589828
  19.8 44.3 %copy-start.1 = (bf16[256,384]{1,0:T(8,128)(2,1)S(1)}, bf16[256,384]{1,0:T(8,128)(2,1)}, u32[]{:S(2)}) copy-start(bf16[256,384]{1,0:T(8,128)(2,1)} %param.6) | copy-start | bytes 589828
  65.9 10.6 %collective-permute-start.10 = (bf16[8,3,128]{2,0,1:T(8,128)(2,1)S(1)}, bf16[8,3,128]{2,0,1:T(8,128)(2,1)S(1)}, u32[]{:S(2)}, u32[]{:S(2)}) collective-permute-start(bf16[8,3,128]{2,0,1:T(8,128)(2,1)S(1)} %get-tuple-element.12), channel_id=1, source_target_pairs={{768,0},{776,8},{784,16},{792,24},{800,32},{808,40},{816,48},{824,... | collective-permute-start | bytes 18440 | tf_op jit(solution)/shard_map/ppermute | solution.py:172
  67.3 11.3 %collective-permute-start.11 = (bf16[8,3,128]{2,0,1:T(8,128)(2,1)S(1)}, bf16[8,3,128]{2,0,1:T(8,128)(2,1)S(1)}, u32[]{:S(2)}, u32[]{:S(2)}) collective-permute-start(bf16[8,3,128]{2,0,1:T(8,128)(2,1)S(1)} %get-tuple-element.12), channel_id=1, source_target_pairs={{896,0},{904,8},{912,16},{920,24},{928,32},{936,40},{944,48},{952,... | collective-permute-start | bytes 18440 | tf_op jit(solution)/shard_map/ppermute | solution.py:172
  68.6 11.0 %collective-permute-start.3 = (bf16[32,3,128]{2,0,1:T(8,128)(2,1)S(1)}, bf16[32,3,128]{2,0,1:T(8,128)(2,1)S(1)}, u32[]{:S(2)}, u32[]{:S(2)}) collective-permute-start(bf16[32,3,128]{2,0,1:T(8,128)(2,1)S(1)} %convert_bitcast_fusion.2), channel_id=1, source_target_pairs={{128,0},{136,8},{144,16},{152,24},{160,32},{168,40},{176,48},{184,... | collective-permute-start | bytes 73736 | tf_op jit(solution)/shard_map/ppermute | solution.py:158
  69.9 33.3 %collective-permute-start.2 = (bf16[256,2,3,128]{3,0,2,1:T(8,128)(2,1)}, bf16[256,2,3,128]{3,0,2,1:T(8,128)(2,1)S(1)}, u32[]{:S(2)}, u32[]{:S(2)}) collective-permute-start(bf16[256,2,3,128]{3,0,2,1:T(8,128)(2,1)} %pad_maximum_fusion), channel_id=1, source_target_pairs={{0,8},{8,16},{16,24},{32,40},{40,48},{48,56},{64,72},{72,80},{80,8... | collective-permute-start | bytes 1179656 | tf_op jit(solution)/shard_map/ppermute | solution.py:121
  71.3 32.0 %collective-permute-start.1 = (bf16[256,2,3,128]{3,0,2,1:T(8,128)(2,1)}, bf16[256,2,3,128]{3,0,2,1:T(8,128)(2,1)}, u32[]{:S(2)}, u32[]{:S(2)}) collective-permute-start(bf16[256,2,3,128]{3,0,2,1:T(8,128)(2,1)} %pad_maximum_fusion), channel_id=1, source_target_pairs={{0,16},{8,24},{32,48},{40,56},{64,80},{72,88},{96,112},{104,120},{... | collective-permute-start | bytes 1179656 | tf_op jit(solution)/shard_map/ppermute | solution.py:121
  76.5 26.7 %collective-permute-start = (bf16[256,2,3,128]{3,0,2,1:T(8,128)(2,1)}, bf16[256,2,3,128]{3,0,2,1:T(8,128)(2,1)}, u32[]{:S(2)}, u32[]{:S(2)}) collective-permute-start(bf16[256,2,3,128]{3,0,2,1:T(8,128)(2,1)} %pad_maximum_fusion), channel_id=1, source_target_pairs={{0,24},{32,56},{64,88},{96,120},{128,152},{160,184},{192,216},{224... | collective-permute-start | bytes 1179656 | tf_op jit(solution)/shard_map/ppermute | solution.py:121
  80.5 12.0 %collective-permute-start.4 = (f32[32,3,129]{2,0,1:T(8,128)S(1)}, f32[32,3,129]{2,0,1:T(8,128)S(1)}, u32[]{:S(2)}, u32[]{:S(2)}) collective-permute-start(f32[32,3,129]{2,0,1:T(8,128)S(1)} %pad_maximum_fusion.1), channel_id=1, source_target_pairs={{0,128},{8,136},{16,144},{24,152},{32,160},{40,168},{48,176},{56,1... | collective-permute-start | bytes 148616 | tf_op jit(solution)/shard_map/ppermute | solution.py:160
  85.0 16.9 %all-to-all-start = ((f32[8,8,3,129]{3,1,2,0:T(8,128)}), f32[8,8,3,129]{3,1,2,0:T(8,128)S(1)}, u32[]{:S(2)}, u32[]{:S(2)}) async-start(f32[8,8,3,129]{3,1,2,0:T(8,128)} %fusion.10), calls=%async_computation | async-start | bytes 393216 | tf_op jit(solution)/shard_map/all_to_all | solution.py:178
  92.5 51.4 %all-gather.3.cloned.1.call-start = ((), (), s32[]{:S(2)}) async-start(), calls=%async_computation.1 | async-start | bytes 1769472 | tf_op jit(solution)/shard_map/all_gather | solution.py:199
Sparse Core Ops, SparseCore 0:
  108.1 35.7 all-gather.2

commit v4 on v3

--- a/solution.py
+++ b/solution.py
@@ -134,9 +134,10 @@
     chooser2, query2, pair2 = level_setup(query_all, key_all, value_all, level_offsets[2], RATE_TOP)
     count1 = pair1.shape[0]
     count2 = pair2.shape[0]
-    ring = lax.all_gather(jnp.concatenate([pair1, pair2], axis=0), ROW_AXES)
+    spare = jnp.zeros_like(pair2[:4])
+    ring = lax.all_gather(jnp.concatenate([pair1, pair2, spare], axis=0), ROW_AXES)
     row1 = ring[:, :count1]
-    row2 = ring[:, count1:]
+    row2 = ring[:, count1 : count1 + count2]
 
     def own_row(query_rows, row_blocks, count):
         keys = row_blocks.reshape(row_len * count, 2, head_count, head_width)

time: 156 us -> 185 us (1.19)
  waiting for transfers between devices: 46.2 us -> 110 us
  blocking collectives: 42.3 us -> 0 us
  starting transfers between devices: 28.5 us -> 33.4 us
  local copies, waits for them, and re-layouts: 5.73 us -> 9.33 us
    all_gather x0 -> x1, waiting for transfers between devices: none -> 58.8 us  [local(): lax.all_gather(jnp.concatenate([pair1, pair2, spare], axis=0), ROW_AXES)]
    all_gather x1 -> x0, blocking collectives: 42.3 us -> none  [local(): ring = lax.all_gather(jnp.concatenate([pair1, pair2], axis=0), ROW_AXES)]
    ppermute x7, waiting for transfers between devices: 1.74 us -> 8.08 us  [local(): visiting.append(lax.ppermute(query2, SEQ_AXES, pairs))]
    ppermute x3, starting transfers between devices: 6.88 us -> 12 us  [local(): arrived.append(lax.ppermute(pair0, SEQ_AXES, pairs))]
  transfers between devices with their start and end apart: 14 -> 15, of which waited for: 3 -> 5; matrix products, arithmetic and copies ran while one was open for 8% -> 8% of each run, Pallas kernels for 0% -> 0%
where the time goes in v4:
time: 185 us; the launch traced here: 184 us
  waiting for transfers between devices  110 us (59%)
  starting transfers between devices  33.4 us (18%)
  between operations  14.1 us (8%)
  matrix products  11.5 us (6%)
  local copies, waits for them, and re-layouts  9.33 us (5%)
  other arithmetic  5.43 us (3%)
    all_gather x1, waiting for transfers between devices, local(): lax.all_gather(jnp.concatenate([pair1, pair2, spare], axis=0), ROW_AXES)  58.8 us
    all_gather x1, waiting for transfers between devices, local(): lax.all_gather(heads_out, 'head', axis=1, tiled=True)  35.1 us
    ppermute x3, starting transfers between devices, local(): arrived.append(lax.ppermute(pair0, SEQ_AXES, pairs))  12 us
    ppermute x7, starting transfers between devices, local(): visiting.append(lax.ppermute(query2, SEQ_AXES, pairs))  9.04 us
    ppermute x7, waiting for transfers between devices, local(): visiting.append(lax.ppermute(query2, SEQ_AXES, pairs))  8.08 us
    all_to_all x1, waiting for transfers between devices, local(): returned = lax.all_to_all(packed, 'sy', 0, 0, tiled=True)  7.91 us
    all_to_all x1, starting transfers between devices, local(): returned = lax.all_to_all(packed, 'sy', 0, 0, tiled=True)  7.22 us
    dot_general x1, matrix products, local(): jnp.dot(lax.all_gather(heads_out, 'head', axis=1, tiled=True), out_weight...  4.73 us
  transfers between devices with their start and end apart: 15, of which 5 were waited for; matrix products, arithmetic and copies ran while one was open for 8% of the time, Pallas kernels for 0%

profile of v4, /device:TPU:1, one launch (start us, length us, event | category | flops | bytes accessed | tf_op | source)
XLA Modules:
  0.0 184.0 jit_solution(10599500904159214967)
XLA Ops:
  6.5 1.0 reshape_reshape.26
  7.6 0.8 fusion.64
  8.6 1.3 collective-permute-start.5
  9.9 1.3 collective-permute-start.6
  11.2 1.3 collective-permute-start.7
  12.5 1.3 collective-permute-start.8
  13.8 1.3 collective-permute-start.9
  15.1 1.0 reshape_reshape.25
  16.1 1.0 reshape_reshape.24
  17.1 1.1 fusion.18
  18.3 1.1 fusion.20
  19.9 0.7 copy.80
  20.6 0.2 fusion.22
  21.6 0.2 fusion.7
  22.3 1.3 collective-permute-start.10
  23.6 4.8 %collective-permute-start.2 = (bf16[256,2,3,128]{3,0,2,1:T(8,128)(2,1)S(1)}, bf16[256,2,3,128]{3,0,2,1:T(8,128)(2,1)S(1)}, u32[]{:S(2)}, u32[]{:S(2)}) collective-permute-start(bf16[256,2,3,128]{3,0,2,1:T(8,128)(2,1)S(1)} %pad_maximum_fusion), channel_id=1, source_target_pairs={{0,8},{8,16},{16,24},{32,40},{40,48},{48,56},{64,72},{72,80},{80,8... | collective-permute-start | bytes 1179656 | tf_op jit(solution)/shard_map/ppermute | solution.py:121
  28.5 5.8 %collective-permute-start.1 = (bf16[256,2,3,128]{3,0,2,1:T(8,128)(2,1)S(1)}, bf16[256,2,3,128]{3,0,2,1:T(8,128)(2,1)S(1)}, u32[]{:S(2)}, u32[]{:S(2)}) collective-permute-start(bf16[256,2,3,128]{3,0,2,1:T(8,128)(2,1)S(1)} %pad_maximum_fusion), channel_id=1, source_target_pairs={{0,16},{8,24},{32,48},{40,56},{64,80},{72,88},{96,112},{104,120},{... | collective-permute-start | bytes 1179656 | tf_op jit(solution)/shard_map/ppermute | solution.py:121
  34.3 1.3 collective-permute-start
  35.7 1.3 collective-permute-start.11
  37.0 1.3 collective-permute-start.3
  38.3 8.1 %collective-permute-done.11 = bf16[8,3,128]{2,0,1:T(8,128)(2,1)S(1)} collective-permute-done((bf16[8,3,128]{2,0,1:T(8,128)(2,1)S(1)}, bf16[8,3,128]{2,0,1:T(8,128)(2,1)S(1)}, u32[]{:S(2)}, u32[]{:S(2)}) %collective-permute-start.11) | collective-permute-done | bytes 6176 | tf_op jit(solution)/shard_map/ppermute | solution.py:173
  46.4 0.3 collective-permute-done
  46.8 0.7 fusion.1
  47.5 0.7 fusion
  48.2 1.2 fusion.3
  49.4 58.8 %all-gather.6.cloned.1.call-done = bf16[704,2,3,128]{3,1,2,0:T(2,128)(2,1)} async-done(((bf16[44,2,3,128]{3,1,2,0:T(2,128)(2,1)}), bf16[704,2,3,128]{3,1,2,0:T(2,128)(2,1)}) %all-gather.6.cloned.1.call-update) | async-done | bytes 1081360 | tf_op jit(solution)/shard_map/all_gather | solution.py:138
  108.2 1.1 slice.92
  109.3 0.3 fusion.79
  109.6 0.2 fusion.32
  109.8 0.2 convolution_bitcast_fusion
  110.0 1.7 slice.88
  111.9 0.3 fusion.81
  112.2 0.2 fusion.25
  112.4 0.2 convolution_bitcast_fusion.2
  112.7 0.3 fusion.82
  113.0 0.2 fusion.24
  113.2 0.2 convolution_bitcast_fusion.1
  113.5 0.2 copy.86
  113.7 0.2 fusion.80
  114.3 3.8 %collective-permute-start.4 = (f32[32,3,129]{2,0,1:T(8,128)S(1)}, f32[32,3,129]{2,0,1:T(8,128)S(1)}, u32[]{:S(2)}, u32[]{:S(2)}) collective-permute-start(f32[32,3,129]{2,0,1:T(8,128)S(1)} %pad_maximum_fusion.1), channel_id=1, source_target_pairs={{0,128},{8,136},{16,144},{24,152},{32,160},{40,168},{48,176},{56,1... | collective-permute-start | bytes 148616 | tf_op jit(solution)/shard_map/ppermute | solution.py:161
  118.1 0.7 fusion.10
  118.9 0.2 convolution_bitcast_fusion.3
  119.1 7.2 %all-to-all-start = ((f32[8,8,3,129]{3,1,2,0:T(8,128)}), f32[8,8,3,129]{3,1,2,0:T(8,128)S(1)}, u32[]{:S(2)}, u32[]{:S(2)}) async-start(f32[8,8,3,129]{3,1,2,0:T(8,128)} %fusion.10), calls=%async_computation | async-start | bytes 393216 | tf_op jit(solution)/shard_map/all_to_all | solution.py:179
  127.2 7.9 %all-to-all-done = f32[8,8,3,129]{3,1,2,0:T(8,128)S(1)} async-done(((f32[8,8,3,129]{3,1,2,0:T(8,128)}), f32[8,8,3,129]{3,1,2,0:T(8,128)S(1)}, u32[]{:S(2)}, u32[]{:S(2)}) %all-to-all-start) | async-done | bytes 99104 | tf_op jit(solution)/shard_map/all_to_all | solution.py:179
  135.1 0.2 copy.115
  136.6 0.7 divide_convert_fusion.4
  137.3 35.1 %all-gather.4.cloned.1.call-done = bf16[256,3072]{0,1:T(8,128)(2,1)} async-done(((bf16[256,384]{0,1:T(8,128)(2,1)}), bf16[256,3072]{0,1:T(8,128)(2,1)}) %all-gather.4.cloned.1.call-update) | async-done | bytes 1572880 | tf_op jit(solution)/shard_map/all_gather | solution.py:200
  172.4 4.7 %convolution_convert_fusion = bf16[256,640]{1,0:T(8,128)(2,1)} fusion(bf16[256,3072]{0,1:T(8,128)(2,1)} %all-gather.4.cloned.1.call-done, bf16[3072,640]{1,0:T(8,128)(2,1)} %param.9), kind=kOutput, calls=%fused_computation.7 | convolution fusion | flops 1006796800 | bytes 5832704 | tf_op jit(solution)/shard_map/dot_general | solution.py:199
  (107 shorter events, 4.7 us)
Async XLA Ops:
  6.5 14.1 %copy-start.2 = (bf16[256,384]{1,0:T(8,128)(2,1)S(1)}, bf16[256,384]{1,0:T(8,128)(2,1)}, u32[]{:S(2)}) copy-start(bf16[256,384]{1,0:T(8,128)(2,1)} %param.5) | copy-start | bytes 589828
  6.5 14.3 %copy-start = (bf16[256,384]{1,0:T(8,128)(2,1)S(1)}, bf16[256,384]{1,0:T(8,128)(2,1)}, u32[]{:S(2)}) copy-start(bf16[256,384]{1,0:T(8,128)(2,1)} %param.7) | copy-start | bytes 589828
  6.5 14.5 %copy-start.1 = (bf16[256,384]{1,0:T(8,128)(2,1)S(1)}, bf16[256,384]{1,0:T(8,128)(2,1)}, u32[]{:S(2)}) copy-start(bf16[256,384]{1,0:T(8,128)(2,1)} %param.6) | copy-start | bytes 589828
  6.5 101.7 %all-gather.6.cloned.1.call-start = ((), (), s32[]{:S(2)}) async-start(), calls=%async_computation.2 | async-start | bytes 1148928 | tf_op jit(solution)/shard_map/all_gather | solution.py:138
  8.6 13.7 %collective-permute-start.5 = (bf16[8,3,128]{2,0,1:T(8,128)(2,1)S(1)}, bf16[8,3,128]{2,0,1:T(8,128)(2,1)S(1)}, u32[]{:S(2)}, u32[]{:S(2)}) collective-permute-start(bf16[8,3,128]{2,0,1:T(8,128)(2,1)S(1)} %get-tuple-element.12), channel_id=1, source_target_pairs={{128,0},{136,8},{144,16},{152,24},{160,32},{168,40},{176,48},{184,... | collective-permute-start | bytes 18440 | tf_op jit(solution)/shard_map/ppermute | solution.py:173
  9.9 13.7 %collective-permute-start.6 = (bf16[8,3,128]{2,0,1:T(8,128)(2,1)S(1)}, bf16[8,3,128]{2,0,1:T(8,128)(2,1)S(1)}, u32[]{:S(2)}, u32[]{:S(2)}) collective-permute-start(bf16[8,3,128]{2,0,1:T(8,128)(2,1)S(1)} %get-tuple-element.12), channel_id=1, source_target_pairs={{256,0},{264,8},{272,16},{280,24},{288,32},{296,40},{304,48},{312,... | collective-permute-start | bytes 18440 | tf_op jit(solution)/shard_map/ppermute | solution.py:173
  11.2 17.3 %collective-permute-start.7 = (bf16[8,3,128]{2,0,1:T(8,128)(2,1)S(1)}, bf16[8,3,128]{2,0,1:T(8,128)(2,1)S(1)}, u32[]{:S(2)}, u32[]{:S(2)}) collective-permute-start(bf16[8,3,128]{2,0,1:T(8,128)(2,1)S(1)} %get-tuple-element.12), channel_id=1, source_target_pairs={{384,0},{392,8},{400,16},{408,24},{416,32},{424,40},{432,48},{440,... | collective-permute-start | bytes 18440 | tf_op jit(solution)/shard_map/ppermute | solution.py:173
  12.5 21.8 %collective-permute-start.8 = (bf16[8,3,128]{2,0,1:T(8,128)(2,1)S(1)}, bf16[8,3,128]{2,0,1:T(8,128)(2,1)S(1)}, u32[]{:S(2)}, u32[]{:S(2)}) collective-permute-start(bf16[8,3,128]{2,0,1:T(8,128)(2,1)S(1)} %get-tuple-element.12), channel_id=1, source_target_pairs={{512,0},{520,8},{528,16},{536,24},{544,32},{552,40},{560,48},{568,... | collective-permute-start | bytes 18440 | tf_op jit(solution)/shard_map/ppermute | solution.py:173
  13.8 21.9 %collective-permute-start.9 = (bf16[8,3,128]{2,0,1:T(8,128)(2,1)S(1)}, bf16[8,3,128]{2,0,1:T(8,128)(2,1)S(1)}, u32[]{:S(2)}, u32[]{:S(2)}) collective-permute-start(bf16[8,3,128]{2,0,1:T(8,128)(2,1)S(1)} %get-tuple-element.12), channel_id=1, source_target_pairs={{640,0},{648,8},{656,16},{664,24},{672,32},{680,40},{688,48},{696,... | collective-permute-start | bytes 18440 | tf_op jit(solution)/shard_map/ppermute | solution.py:173
  22.3 14.7 %collective-permute-start.10 = (bf16[8,3,128]{2,0,1:T(8,128)(2,1)S(1)}, bf16[8,3,128]{2,0,1:T(8,128)(2,1)S(1)}, u32[]{:S(2)}, u32[]{:S(2)}) collective-permute-start(bf16[8,3,128]{2,0,1:T(8,128)(2,1)S(1)} %get-tuple-element.12), channel_id=1, source_target_pairs={{768,0},{776,8},{784,16},{792,24},{800,32},{808,40},{816,48},{824,... | collective-permute-start | bytes 18440 | tf_op jit(solution)/shard_map/ppermute | solution.py:173
  23.6 22.8 %collective-permute-start.2 = (bf16[256,2,3,128]{3,0,2,1:T(8,128)(2,1)S(1)}, bf16[256,2,3,128]{3,0,2,1:T(8,128)(2,1)S(1)}, u32[]{:S(2)}, u32[]{:S(2)}) collective-permute-start(bf16[256,2,3,128]{3,0,2,1:T(8,128)(2,1)S(1)} %pad_maximum_fusion), channel_id=1, source_target_pairs={{0,8},{8,16},{16,24},{32,40},{40,48},{48,56},{64,72},{72,80},{80,8... | collective-permute-start | bytes 1179656 | tf_op jit(solution)/shard_map/ppermute | solution.py:121
  28.5 17.9 %collective-permute-start.1 = (bf16[256,2,3,128]{3,0,2,1:T(8,128)(2,1)S(1)}, bf16[256,2,3,128]{3,0,2,1:T(8,128)(2,1)S(1)}, u32[]{:S(2)}, u32[]{:S(2)}) collective-permute-start(bf16[256,2,3,128]{3,0,2,1:T(8,128)(2,1)S(1)} %pad_maximum_fusion), channel_id=1, source_target_pairs={{0,16},{8,24},{32,48},{40,56},{64,80},{72,88},{96,112},{104,120},{... | collective-permute-start | bytes 1179656 | tf_op jit(solution)/shard_map/ppermute | solution.py:121
  34.3 12.4 %collective-permute-start = (bf16[256,2,3,128]{3,0,2,1:T(8,128)(2,1)S(1)}, bf16[256,2,3,128]{3,0,2,1:T(8,128)(2,1)S(1)}, u32[]{:S(2)}, u32[]{:S(2)}) collective-permute-start(bf16[256,2,3,128]{3,0,2,1:T(8,128)(2,1)S(1)} %pad_maximum_fusion), channel_id=1, source_target_pairs={{0,24},{32,56},{64,88},{96,120},{128,152},{160,184},{192,216},{224... | collective-permute-start | bytes 1179656 | tf_op jit(solution)/shard_map/ppermute | solution.py:121
  35.7 10.7 %collective-permute-start.11 = (bf16[8,3,128]{2,0,1:T(8,128)(2,1)S(1)}, bf16[8,3,128]{2,0,1:T(8,128)(2,1)S(1)}, u32[]{:S(2)}, u32[]{:S(2)}) collective-permute-start(bf16[8,3,128]{2,0,1:T(8,128)(2,1)S(1)} %get-tuple-element.12), channel_id=1, source_target_pairs={{896,0},{904,8},{912,16},{920,24},{928,32},{936,40},{944,48},{952,... | collective-permute-start | bytes 18440 | tf_op jit(solution)/shard_map/ppermute | solution.py:173
  37.0 74.9 %collective-permute-start.3 = (bf16[32,3,128]{2,0,1:T(8,128)(2,1)S(1)}, bf16[32,3,128]{2,0,1:T(8,128)(2,1)S(1)}, u32[]{:S(2)}, u32[]{:S(2)}) collective-permute-start(bf16[32,3,128]{2,0,1:T(8,128)(2,1)S(1)} %convert_bitcast_fusion.2), channel_id=1, source_target_pairs={{128,0},{136,8},{144,16},{152,24},{160,32},{168,40},{176,48},{184,... | collective-permute-start | bytes 73736 | tf_op jit(solution)/shard_map/ppermute | solution.py:159
  114.3 12.0 %collective-permute-start.4 = (f32[32,3,129]{2,0,1:T(8,128)S(1)}, f32[32,3,129]{2,0,1:T(8,128)S(1)}, u32[]{:S(2)}, u32[]{:S(2)}) collective-permute-start(f32[32,3,129]{2,0,1:T(8,128)S(1)} %pad_maximum_fusion.1), channel_id=1, source_target_pairs={{0,128},{8,136},{16,144},{24,152},{32,160},{40,168},{48,176},{56,1... | collective-permute-start | bytes 148616 | tf_op jit(solution)/shard_map/ppermute | solution.py:161
  119.1 16.1 %all-to-all-start = ((f32[8,8,3,129]{3,1,2,0:T(8,128)}), f32[8,8,3,129]{3,1,2,0:T(8,128)S(1)}, u32[]{:S(2)}, u32[]{:S(2)}) async-start(f32[8,8,3,129]{3,1,2,0:T(8,128)} %fusion.10), calls=%async_computation | async-start | bytes 393216 | tf_op jit(solution)/shard_map/all_to_all | solution.py:179
  126.3 46.1 %all-gather.4.cloned.1.call-start = ((), (), s32[]{:S(2)}) async-start(), calls=%async_computation.1 | async-start | bytes 1769472 | tf_op jit(solution)/shard_map/all_gather | solution.py:200
Sparse Core Ops, SparseCore 0:
  20.7 87.4 all-gather.5
  137.4 34.9 all-gather.3

commit v5 on v2

--- a/solution.py
+++ b/solution.py
@@ -79,8 +79,7 @@
     return packed[..., :-1], packed[..., -1]
 
 
-SEQ_AXES = ("sy", "sz")
-ROW_AXES = "sz"
+SEQ_AXES = ("sy", "zh", "zl")
 
 
 def split3(value):
@@ -102,10 +101,11 @@
     head_width = queries.shape[1] // head_count
     scale_factor = head_width ** (-0.5)
     rows_total = lax.axis_size("sy")
-    row_len = lax.axis_size("sz")
+    group = lax.axis_size("zl")
+    row_len = group * lax.axis_size("zh")
     seq_count = rows_total * row_len
     row_y = lax.axis_index("sy")
-    row_z = lax.axis_index("sz")
+    row_z = lax.axis_index("zh") * group + lax.axis_index("zl")
     seq_index = row_y * row_len + row_z
     query_all = queries.reshape(row_count, head_count, head_width)
     key_all = key_states.reshape(row_count, head_count, head_width)
@@ -134,7 +134,8 @@
     chooser2, query2, pair2 = level_setup(query_all, key_all, value_all, level_offsets[2], RATE_TOP)
     count1 = pair1.shape[0]
     count2 = pair2.shape[0]
-    ring = lax.all_gather(jnp.concatenate([pair1, pair2], axis=0), ROW_AXES)
+    ring = lax.all_gather(jnp.concatenate([pair1, pair2], axis=0), "zl")
+    ring = lax.all_gather(ring, "zh").reshape(row_len, *ring.shape[1:])
     row1 = ring[:, :count1]
     row2 = ring[:, count1:]
 
@@ -166,8 +167,11 @@
     full_lses.append(full_lse)
 
     own_out2, own_lse2 = own_row(query2, row2, count2)
-    column_queries = lax.all_gather(query2, "sy", tiled=True)
-    cross_out, cross_lse = whole_row(column_queries, row2, count2)
+    copies = jnp.broadcast_to(query2[None], (rows_total,) + query2.shape)
+    column_queries = lax.all_to_all(copies, "sy", 0, 0, tiled=True)
+    cross_out, cross_lse = whole_row(
+        column_queries.reshape(rows_total * count2, head_count, head_width), row2, count2
+    )
     packed = pack(cross_out, cross_lse).reshape(rows_total, count2, head_count, head_width + 1)
     returned = lax.all_to_all(packed, "sy", 0, 0, tiled=True)
     back_out, back_lse = unpack(returned)
@@ -199,8 +203,10 @@
 
 def solution(mesh):
     seq_count, head_count = mesh.devices.shape
+    group = SEG_ROWS // TOK_DEV
     split = jax.sharding.Mesh(
-        mesh.devices.reshape(seq_count // ROW, ROW, head_count), SEQ_AXES + ("head",)
+        mesh.devices.reshape(seq_count // ROW, ROW // group, group, head_count),
+        SEQ_AXES + ("head",),
     )
     return jax.shard_map(
         local,

time: 161 us -> 180 us (1.12)
  blocking collectives: 58.9 us -> 69.5 us
  starting transfers between devices: 23.2 us -> 29.9 us
    all_gather x2, blocking collectives: 58.9 us -> 69.5 us  [the longest x1 46.1 us: local(): ring = lax.all_gather(ring, 'zh').reshape(row_len, *ring.shape[1:])]
    all_to_all x1, waiting for transfers between devices: 0.01 us -> 8.55 us  [local(): returned = lax.all_to_all(packed, 'sy', 0, 0, tiled=True)]
    all_to_all x0 -> x1, starting transfers between devices: none -> 6.82 us  [local(): column_queries = lax.all_to_all(copies, 'sy', 0, 0, tiled=True)]
    all_gather x1, waiting for transfers between devices: 38.5 us -> 32.8 us  [local(): lax.all_gather(heads_out, 'head', axis=1, tiled=True)]
  transfers between devices with their start and end apart: 7 -> 8, of which waited for: 3 -> 3; matrix products, arithmetic and copies ran while one was open for 6% -> 7% of each run, Pallas kernels for 0% -> 0%
where the time goes in v5:
time: 180 us; the launch traced here: 179 us
  blocking collectives  69.5 us (39%)
  waiting for transfers between devices  42.1 us (23%)
  starting transfers between devices  29.9 us (17%)
  between operations  14 us (8%)
  matrix products  9.68 us (5%)
  other arithmetic  7.82 us (4%)
  local copies, waits for them, and re-layouts  6.28 us (3%)
    all_gather x1, blocking collectives, local(): ring = lax.all_gather(ring, 'zh').reshape(row_len, *ring.shape[1:])  46.1 us
    all_gather x1, waiting for transfers between devices, local(): lax.all_gather(heads_out, 'head', axis=1, tiled=True)  32.8 us
    all_gather x1, blocking collectives, local(): ring = lax.all_gather(jnp.concatenate([pair1, pair2], axis=0), 'zl')  23.4 us
    ppermute x3, starting transfers between devices, local(): arrived.append(lax.ppermute(pair0, SEQ_AXES, pairs))  12 us
    all_to_all x1, waiting for transfers between devices, local(): returned = lax.all_to_all(packed, 'sy', 0, 0, tiled=True)  8.55 us
    all_to_all x1, starting transfers between devices, local(): column_queries = lax.all_to_all(copies, 'sy', 0, 0, tiled=True)  6.82 us
    all_to_all x1, starting transfers between devices, local(): returned = lax.all_to_all(packed, 'sy', 0, 0, tiled=True)  6.57 us
    dot_general x1, matrix products, local(): jnp.dot(lax.all_gather(heads_out, 'head', axis=1, tiled=True), out_weight...  4.73 us
  transfers between devices with their start and end apart: 8, of which 3 were waited for; matrix products, arithmetic and copies ran while one was open for 7% of the time, Pallas kernels for 0%

profile of v5, /device:TPU:1, one launch (start us, length us, event | category | flops | bytes accessed | tf_op | source)
XLA Modules:
  0.0 179.2 jit_solution(13897235512741040308)
XLA Ops:
  6.5 1.1 copy.52
  7.7 0.2 copy.54
  7.8 1.1 copy.51
  9.1 0.8 pad_maximum_fusion
  9.9 4.8 %collective-permute-start.2 = (bf16[256,2,3,128]{3,0,2,1:T(8,128)(2,1)}, bf16[256,2,3,128]{3,0,2,1:T(8,128)(2,1)S(1)}, u32[]{:S(2)}, u32[]{:S(2)}) collective-permute-start(bf16[256,2,3,128]{3,0,2,1:T(8,128)(2,1)} %pad_maximum_fusion), channel_id=1, source_target_pairs={{0,8},{8,16},{16,24},{32,40},{40,48},{48,56},{64,72},{72,80},{80,8... | collective-permute-start | bytes 1179656 | tf_op jit(solution)/shard_map/ppermute | solution.py:121
  14.7 5.8 %collective-permute-start.1 = (bf16[256,2,3,128]{3,0,2,1:T(8,128)(2,1)}, bf16[256,2,3,128]{3,0,2,1:T(8,128)(2,1)S(1)}, u32[]{:S(2)}, u32[]{:S(2)}) collective-permute-start(bf16[256,2,3,128]{3,0,2,1:T(8,128)(2,1)} %pad_maximum_fusion), channel_id=1, source_target_pairs={{0,16},{8,24},{32,48},{40,56},{64,80},{72,88},{96,112},{104,120},{... | collective-permute-start | bytes 1179656 | tf_op jit(solution)/shard_map/ppermute | solution.py:121
  20.5 1.3 collective-permute-start
  21.8 0.8 fusion.63
  22.6 0.6 iota_compare_fusion.4
  23.3 1.0 reshape_reshape.26
  24.4 0.6 broadcast_in_dim.153
  25.0 6.8 %all-to-all-start = ((bf16[8,8,3,128]{3,1,2,0:T(8,128)(2,1)}), bf16[8,8,3,128]{3,1,2,0:T(8,128)(2,1)S(1)}, u32[]{:S(2)}, u32[]{:S(2)}) async-start(bf16[8,8,3,128]{3,1,2,0:T(8,128)(2,1)} %broadcast_in_dim.153), calls=%async_computation | async-start | bytes 98304 | tf_op jit(solution)/shard_map/all_to_all | solution.py:171
  31.9 0.2 fusion.19
  32.1 1.3 collective-permute-start.3
  33.6 0.2 fusion.15
  33.8 0.2 fusion.17
  34.3 23.4 %all-gather = bf16[160,2,3,128]{3,0,2,1:T(8,128)(2,1)S(1)} all-gather(bf16[40,2,3,128]{3,0,2,1:T(8,128)(2,1)S(1)} %maximum_maximum_fusion.1), channel_id=2, replica_groups=mesh['sy'=8,'zh'=4,'zl'=4,'head'=8] {'zl'}, dimensions={0}, use_global_device_ids=true | all-gather | bytes 307200 | tf_op jit(solution)/shard_map/all_gather | solution.py:137
  57.7 46.1 %all-gather.1 = bf16[16,40,2,3,128]{4,1,0,3,2:T(8,128)(2,1)S(1)} all-gather(bf16[4,40,2,3,128]{4,1,0,3,2:T(8,128)(2,1)S(1)} %bitcast.185), channel_id=3, replica_groups=mesh['sy'=8,'zh'=4,'zl'=4,'head'=8] {'zh'}, dimensions={0}, use_global_device_ids=true | all-gather | bytes 1228800 | tf_op jit(solution)/shard_map/all_gather | solution.py:138
  104.0 0.3 fusion.81
  104.4 0.2 fusion.21
  104.6 0.2 convolution_bitcast_fusion.1
  104.9 0.2 fusion.79
  105.1 0.2 fusion.42
  105.3 0.2 fusion.7
  105.6 0.2 convolution_bitcast_fusion.3
  105.8 0.3 fusion.80
  106.1 0.2 fusion.22
  106.3 0.2 convolution_bitcast_fusion.2
  106.7 3.2 %collective-permute-start.4 = (f32[32,3,129]{2,0,1:T(8,128)S(1)}, f32[32,3,129]{2,0,1:T(8,128)S(1)}, u32[]{:S(2)}, u32[]{:S(2)}) collective-permute-start(f32[32,3,129]{2,0,1:T(8,128)S(1)} %pad_maximum_fusion.2), channel_id=1, source_target_pairs={{0,128},{8,136},{16,144},{24,152},{32,160},{40,168},{48,176},{56,1... | collective-permute-start | bytes 148616 | tf_op jit(solution)/shard_map/ppermute | solution.py:161
  109.9 0.5 iota_compare_fusion.6
  110.8 0.7 collective-permute-done.4
  112.1 0.2 copy.66
  112.3 0.3 fusion.78
  112.6 0.2 fusion.29
  112.8 0.2 convolution_bitcast_fusion
  113.1 0.2 copy.61
  113.3 0.7 pad_maximum_fusion.1
  114.0 6.6 %all-to-all-start.1 = ((f32[8,8,3,129]{3,1,2,0:T(8,128)}), f32[8,8,3,129]{3,1,2,0:T(8,128)S(1)}, u32[]{:S(2)}, u32[]{:S(2)}) async-start(f32[8,8,3,129]{3,1,2,0:T(8,128)} %pad_maximum_fusion.1), calls=%async_computation.1 | async-start | bytes 393216 | tf_op jit(solution)/shard_map/all_to_all | solution.py:176
  120.7 8.5 %all-to-all-done.1 = f32[8,8,3,129]{3,1,2,0:T(8,128)S(1)} async-done(((f32[8,8,3,129]{3,1,2,0:T(8,128)}), f32[8,8,3,129]{3,1,2,0:T(8,128)S(1)}, u32[]{:S(2)}, u32[]{:S(2)}) %all-to-all-start.1) | async-done | bytes 99104 | tf_op jit(solution)/shard_map/all_to_all | solution.py:176
  129.2 0.2 copy.90
  129.7 0.7 broadcast_select_fusion.1
  131.0 0.2 copy.71
  131.4 0.7 fusion.1
  132.1 0.7 fusion
  132.8 1.2 fusion.3
  134.1 0.7 divide_convert_fusion.4
  134.9 32.8 %all-gather.4.cloned.1.call-done = bf16[256,3072]{0,1:T(8,128)(2,1)} async-done(((bf16[256,384]{0,1:T(8,128)(2,1)}), bf16[256,3072]{0,1:T(8,128)(2,1)}) %all-gather.4.cloned.1.call-update) | async-done | bytes 1572880 | tf_op jit(solution)/shard_map/all_gather | solution.py:197
  167.6 4.7 %convolution_convert_fusion = bf16[256,640]{1,0:T(8,128)(2,1)} fusion(bf16[256,3072]{0,1:T(8,128)(2,1)} %all-gather.4.cloned.1.call-done, bf16[3072,640]{1,0:T(8,128)(2,1)} %param.9), kind=kOutput, calls=%fused_computation.7 | convolution fusion | flops 1006796800 | bytes 5832704 | tf_op jit(solution)/shard_map/dot_general | solution.py:196
  (85 shorter events, 3.3 us)
Async XLA Ops:
  6.5 26.9 %copy-start = (bf16[256,384]{1,0:T(8,128)(2,1)S(1)}, bf16[256,384]{1,0:T(8,128)(2,1)}, u32[]{:S(2)}) copy-start(bf16[256,384]{1,0:T(8,128)(2,1)} %param.7) | copy-start | bytes 589828
  6.5 27.0 %copy-start.1 = (bf16[256,384]{1,0:T(8,128)(2,1)S(1)}, bf16[256,384]{1,0:T(8,128)(2,1)}, u32[]{:S(2)}) copy-start(bf16[256,384]{1,0:T(8,128)(2,1)} %param.6) | copy-start | bytes 589828
  6.5 25.4 %copy-start.2 = (bf16[256,384]{1,0:T(8,128)(2,1)S(1)}, bf16[256,384]{1,0:T(8,128)(2,1)}, u32[]{:S(2)}) copy-start(bf16[256,384]{1,0:T(8,128)(2,1)} %param.5) | copy-start | bytes 589828
  9.9 121.4 %collective-permute-start.2 = (bf16[256,2,3,128]{3,0,2,1:T(8,128)(2,1)}, bf16[256,2,3,128]{3,0,2,1:T(8,128)(2,1)S(1)}, u32[]{:S(2)}, u32[]{:S(2)}) collective-permute-start(bf16[256,2,3,128]{3,0,2,1:T(8,128)(2,1)} %pad_maximum_fusion), channel_id=1, source_target_pairs={{0,8},{8,16},{16,24},{32,40},{40,48},{48,56},{64,72},{72,80},{80,8... | collective-permute-start | bytes 1179656 | tf_op jit(solution)/shard_map/ppermute | solution.py:121
  14.7 116.5 %collective-permute-start.1 = (bf16[256,2,3,128]{3,0,2,1:T(8,128)(2,1)}, bf16[256,2,3,128]{3,0,2,1:T(8,128)(2,1)S(1)}, u32[]{:S(2)}, u32[]{:S(2)}) collective-permute-start(bf16[256,2,3,128]{3,0,2,1:T(8,128)(2,1)} %pad_maximum_fusion), channel_id=1, source_target_pairs={{0,16},{8,24},{32,48},{40,56},{64,80},{72,88},{96,112},{104,120},{... | collective-permute-start | bytes 1179656 | tf_op jit(solution)/shard_map/ppermute | solution.py:121
  20.5 110.7 %collective-permute-start = (bf16[256,2,3,128]{3,0,2,1:T(8,128)(2,1)}, bf16[256,2,3,128]{3,0,2,1:T(8,128)(2,1)S(1)}, u32[]{:S(2)}, u32[]{:S(2)}) collective-permute-start(bf16[256,2,3,128]{3,0,2,1:T(8,128)(2,1)} %pad_maximum_fusion), channel_id=1, source_target_pairs={{0,24},{32,56},{64,88},{96,120},{128,152},{160,184},{192,216},{224... | collective-permute-start | bytes 1179656 | tf_op jit(solution)/shard_map/ppermute | solution.py:121
  25.0 87.3 %all-to-all-start = ((bf16[8,8,3,128]{3,1,2,0:T(8,128)(2,1)}), bf16[8,8,3,128]{3,1,2,0:T(8,128)(2,1)S(1)}, u32[]{:S(2)}, u32[]{:S(2)}) async-start(bf16[8,8,3,128]{3,1,2,0:T(8,128)(2,1)} %broadcast_in_dim.153), calls=%async_computation | async-start | bytes 98304 | tf_op jit(solution)/shard_map/all_to_all | solution.py:171
  32.1 73.6 %collective-permute-start.3 = (bf16[32,3,128]{2,0,1:T(8,128)(2,1)S(1)}, bf16[32,3,128]{2,0,1:T(8,128)(2,1)S(1)}, u32[]{:S(2)}, u32[]{:S(2)}) collective-permute-start(bf16[32,3,128]{2,0,1:T(8,128)(2,1)S(1)} %convert_bitcast_fusion.2), channel_id=1, source_target_pairs={{128,0},{136,8},{144,16},{152,24},{160,32},{168,40},{176,48},{184,... | collective-permute-start | bytes 73736 | tf_op jit(solution)/shard_map/ppermute | solution.py:159
  106.7 4.8 %collective-permute-start.4 = (f32[32,3,129]{2,0,1:T(8,128)S(1)}, f32[32,3,129]{2,0,1:T(8,128)S(1)}, u32[]{:S(2)}, u32[]{:S(2)}) collective-permute-start(f32[32,3,129]{2,0,1:T(8,128)S(1)} %pad_maximum_fusion.2), channel_id=1, source_target_pairs={{0,128},{8,136},{16,144},{24,152},{32,160},{40,168},{48,176},{56,1... | collective-permute-start | bytes 148616 | tf_op jit(solution)/shard_map/ppermute | solution.py:161
  110.5 18.9 %copy-start.3 = (pred[8]{0:T(512)(128)(4,1)S(1)}, pred[8]{0:T(512)(128)(4,1)}, u32[]{:S(2)}) copy-start(pred[8]{0:T(512)(128)(4,1)} %iota_compare_fusion.6) | copy-start | bytes 28
  114.0 15.2 %all-to-all-start.1 = ((f32[8,8,3,129]{3,1,2,0:T(8,128)}), f32[8,8,3,129]{3,1,2,0:T(8,128)S(1)}, u32[]{:S(2)}, u32[]{:S(2)}) async-start(f32[8,8,3,129]{3,1,2,0:T(8,128)} %pad_maximum_fusion.1), calls=%async_computation.1 | async-start | bytes 393216 | tf_op jit(solution)/shard_map/all_to_all | solution.py:176
  120.6 47.0 %all-gather.4.cloned.1.call-start = ((), (), s32[]{:S(2)}) async-start(), calls=%async_computation.2 | async-start | bytes 1769472 | tf_op jit(solution)/shard_map/all_gather | solution.py:197
Sparse Core Ops, SparseCore 0:
  135.0 32.5 all-gather.3

commit v6 on v5

--- a/solution.py
+++ b/solution.py
@@ -134,8 +134,15 @@
     chooser2, query2, pair2 = level_setup(query_all, key_all, value_all, level_offsets[2], RATE_TOP)
     count1 = pair1.shape[0]
     count2 = pair2.shape[0]
-    ring = lax.all_gather(jnp.concatenate([pair1, pair2], axis=0), "zl")
-    ring = lax.all_gather(ring, "zh").reshape(row_len, *ring.shape[1:])
+    moving = jnp.concatenate([pair1, pair2], axis=0)
+    backward = [
+        (s, (s // row_len) * row_len + (s % row_len - 1) % row_len) for s in range(seq_count)
+    ]
+    held = [moving] + [None] * (row_len - 1)
+    for step in range(1, row_len):
+        moving = lax.ppermute(moving, SEQ_AXES, backward)
+        held[row_len - step] = moving
+    ring = jnp.stack(held)
     row1 = ring[:, :count1]
     row2 = ring[:, count1:]
 
@@ -144,10 +151,8 @@
         shape = (count, row_len * count)
         key_index = lax.broadcasted_iota(jnp.int32, shape, 1)
         query_index = lax.broadcasted_iota(jnp.int32, shape, 0)
-        source = key_index // count
-        allowed = jnp.where(
-            source == row_z, key_index % count <= query_index, source < row_z
-        )
+        offset = key_index // count
+        allowed = jnp.where(offset == 0, key_index % count <= query_index, offset <= row_z)
         return attend(query_rows, keys[:, 0], keys[:, 1], allowed, scale_factor)
 
     def whole_row(query_rows, row_blocks, count):

time: 180 us -> 220 us (1.22)
  starting transfers between devices: 29.9 us -> 106 us
  blocking collectives: 69.5 us -> 0 us
  waiting for transfers between devices: 42.1 us -> 67.8 us
  local copies, waits for them, and re-layouts: 6.28 us -> 10.8 us
  matrix products: 9.68 us -> 11.9 us
    ppermute x0 -> x15, starting transfers between devices: none -> 75.5 us  [local(): moving = lax.ppermute(moving, SEQ_AXES, backward)]
    all_gather x2 -> x0, blocking collectives: 69.5 us -> none  [the longest x1 46.1 us: local(): ring = lax.all_gather(ring, 'zh').reshape(row_len, *ring.shape[1:])]
    ppermute x0 -> x15, waiting for transfers between devices: none -> 15 us  [local(): moving = lax.ppermute(moving, SEQ_AXES, backward)]
    all_gather x1, waiting for transfers between devices: 32.8 us -> 45.1 us  [local(): lax.all_gather(heads_out, 'head', axis=1, tiled=True)]
    unnamed x13 -> x77, local copies, waits for them, and re-layouts: 2.68 us -> 5.06 us
    dot_general x5, matrix products: 1.87 us -> 4.14 us  [attend(): jnp.einsum('qhd,khd->hqk', query_rows, key_rows, preferred_element_type=j...]
  transfers between devices with their start and end apart: 8 -> 23, of which waited for: 3 -> 15; matrix products, arithmetic and copies ran while one was open for 7% -> 8% of each run, Pallas kernels for 0% -> 0%
where the time goes in v6:
time: 220 us; the launch traced here: 219 us
  starting transfers between devices  106 us (48%)
  waiting for transfers between devices  67.8 us (31%)
  between operations  14.4 us (7%)
  matrix products  11.9 us (5%)
  local copies, waits for them, and re-layouts  10.8 us (5%)
  other arithmetic  8.09 us (4%)
    ppermute x15, starting transfers between devices, local(): moving = lax.ppermute(moving, SEQ_AXES, backward)  75.5 us
    all_gather x1, waiting for transfers between devices, local(): lax.all_gather(heads_out, 'head', axis=1, tiled=True)  45.1 us
    ppermute x15, waiting for transfers between devices, local(): moving = lax.ppermute(moving, SEQ_AXES, backward)  15 us
    ppermute x3, starting transfers between devices, local(): arrived.append(lax.ppermute(pair0, SEQ_AXES, pairs))  12 us
    all_to_all x1, waiting for transfers between devices, local(): returned = lax.all_to_all(packed, 'sy', 0, 0, tiled=True)  7.69 us
    all_to_all x1, starting transfers between devices, local(): column_queries = lax.all_to_all(copies, 'sy', 0, 0, tiled=True)  6.82 us
    all_to_all x1, starting transfers between devices, local(): returned = lax.all_to_all(packed, 'sy', 0, 0, tiled=True)  6.43 us
    unnamed x77, local copies, waits for them, and re-layouts  5.06 us
  transfers between devices with their start and end apart: 23, of which 15 were waited for; matrix products, arithmetic and copies ran while one was open for 8% of the time, Pallas kernels for 0%

profile of v6, /device:TPU:1, one launch (start us, length us, event | category | flops | bytes accessed | tf_op | source)
XLA Modules:
  0.0 219.1 jit_solution(12902741771242521561)
XLA Ops:
  6.5 1.1 copy.97
  7.8 1.1 copy.96
  9.1 4.8 %collective-permute-start.2 = (bf16[256,2,3,128]{3,0,2,1:T(8,128)(2,1)S(1)}, bf16[256,2,3,128]{3,0,2,1:T(8,128)(2,1)S(1)}, u32[]{:S(2)}, u32[]{:S(2)}) collective-permute-start(bf16[256,2,3,128]{3,0,2,1:T(8,128)(2,1)S(1)} %pad_maximum_fusion), channel_id=1, source_target_pairs={{0,8},{8,16},{16,24},{32,40},{40,48},{48,56},{64,72},{72,80},{80,8... | collective-permute-start | bytes 1179656 | tf_op jit(solution)/shard_map/ppermute | solution.py:121
  14.0 5.8 %collective-permute-start.1 = (bf16[256,2,3,128]{3,0,2,1:T(8,128)(2,1)S(1)}, bf16[256,2,3,128]{3,0,2,1:T(8,128)(2,1)S(1)}, u32[]{:S(2)}, u32[]{:S(2)}) collective-permute-start(bf16[256,2,3,128]{3,0,2,1:T(8,128)(2,1)S(1)} %pad_maximum_fusion), channel_id=1, source_target_pairs={{0,16},{8,24},{32,48},{40,56},{64,80},{72,88},{96,112},{104,120},{... | collective-permute-start | bytes 1179656 | tf_op jit(solution)/shard_map/ppermute | solution.py:121
  19.8 1.3 collective-permute-start
  21.1 1.0 reshape_reshape.25
  22.1 1.0 reshape_reshape.24
  25.7 10.7 %collective-permute-start.3 = (bf16[40,2,3,128]{3,0,2,1:T(8,128)(2,1)S(1)}, bf16[40,2,3,128]{3,0,2,1:T(8,128)(2,1)S(1)}, u32[]{:S(2)}, u32[]{:S(2)}) collective-permute-start(bf16[40,2,3,128]{3,0,2,1:T(8,128)(2,1)S(1)} %maximum_maximum_fusion.1), channel_id=1, source_target_pairs={{0,120},{8,0},{16,8},{24,16},{32,24},{40,32},{48,40},{56,48},{64,5... | collective-permute-start | bytes 184328 | tf_op jit(solution)/shard_map/ppermute | solution.py:143
  37.2 6.8 %all-to-all-start = ((bf16[8,8,3,128]{3,1,2,0:T(8,128)(2,1)}), bf16[8,8,3,128]{3,1,2,0:T(8,128)(2,1)}, u32[]{:S(2)}, u32[]{:S(2)}) async-start(bf16[8,8,3,128]{3,1,2,0:T(8,128)(2,1)} %broadcast_in_dim.153), calls=%async_computation | async-start | bytes 98304 | tf_op jit(solution)/shard_map/all_to_all | solution.py:176
  44.8 1.3 collective-permute-start.18
  46.4 3.4 %collective-permute-start.4 = (bf16[40,2,3,128]{3,0,2,1:T(8,128)(2,1)S(1)}, bf16[40,2,3,128]{3,0,2,1:T(8,128)(2,1)S(1)}, u32[]{:S(2)}, u32[]{:S(2)}) collective-permute-start(bf16[40,2,3,128]{3,0,2,1:T(8,128)(2,1)S(1)} %collective-permute-done.3), channel_id=1, source_target_pairs={{0,120},{8,0},{16,8},{24,16},{32,24},{40,32},{48,40},{56,48},{64,5... | collective-permute-start | bytes 184328 | tf_op jit(solution)/shard_map/ppermute | solution.py:143
  49.8 2.0 collective-permute-done.4
  51.8 4.6 %collective-permute-start.5 = (bf16[40,2,3,128]{3,0,2,1:T(8,128)(2,1)S(1)}, bf16[40,2,3,128]{3,0,2,1:T(8,128)(2,1)S(1)}, u32[]{:S(2)}, u32[]{:S(2)}) collective-permute-start(bf16[40,2,3,128]{3,0,2,1:T(8,128)(2,1)S(1)} %collective-permute-done.4), channel_id=1, source_target_pairs={{0,120},{8,0},{16,8},{24,16},{32,24},{40,32},{48,40},{56,48},{64,5... | collective-permute-start | bytes 184328 | tf_op jit(solution)/shard_map/ppermute | solution.py:143
  56.4 1.3 collective-permute-done.5
  57.7 5.0 %collective-permute-start.6 = (bf16[40,2,3,128]{3,0,2,1:T(8,128)(2,1)S(1)}, bf16[40,2,3,128]{3,0,2,1:T(8,128)(2,1)S(1)}, u32[]{:S(2)}, u32[]{:S(2)}) collective-permute-start(bf16[40,2,3,128]{3,0,2,1:T(8,128)(2,1)S(1)} %collective-permute-done.5), channel_id=1, source_target_pairs={{0,120},{8,0},{16,8},{24,16},{32,24},{40,32},{48,40},{56,48},{64,5... | collective-permute-start | bytes 184328 | tf_op jit(solution)/shard_map/ppermute | solution.py:143
  62.7 1.2 collective-permute-done.6
  64.0 4.9 %collective-permute-start.7 = (bf16[40,2,3,128]{3,0,2,1:T(8,128)(2,1)S(1)}, bf16[40,2,3,128]{3,0,2,1:T(8,128)(2,1)S(1)}, u32[]{:S(2)}, u32[]{:S(2)}) collective-permute-start(bf16[40,2,3,128]{3,0,2,1:T(8,128)(2,1)S(1)} %collective-permute-done.6), channel_id=1, source_target_pairs={{0,120},{8,0},{16,8},{24,16},{32,24},{40,32},{48,40},{56,48},{64,5... | collective-permute-start | bytes 184328 | tf_op jit(solution)/shard_map/ppermute | solution.py:143
  68.9 1.3 collective-permute-done.7
  70.1 4.9 %collective-permute-start.8 = (bf16[40,2,3,128]{3,0,2,1:T(8,128)(2,1)S(1)}, bf16[40,2,3,128]{3,0,2,1:T(8,128)(2,1)S(1)}, u32[]{:S(2)}, u32[]{:S(2)}) collective-permute-start(bf16[40,2,3,128]{3,0,2,1:T(8,128)(2,1)S(1)} %collective-permute-done.7), channel_id=1, source_target_pairs={{0,120},{8,0},{16,8},{24,16},{32,24},{40,32},{48,40},{56,48},{64,5... | collective-permute-start | bytes 184328 | tf_op jit(solution)/shard_map/ppermute | solution.py:143
  75.0 1.3 collective-permute-done.8
  76.3 4.9 %collective-permute-start.9 = (bf16[40,2,3,128]{3,0,2,1:T(8,128)(2,1)S(1)}, bf16[40,2,3,128]{3,0,2,1:T(8,128)(2,1)S(1)}, u32[]{:S(2)}, u32[]{:S(2)}) collective-permute-start(bf16[40,2,3,128]{3,0,2,1:T(8,128)(2,1)S(1)} %collective-permute-done.8), channel_id=1, source_target_pairs={{0,120},{8,0},{16,8},{24,16},{32,24},{40,32},{48,40},{56,48},{64,5... | collective-permute-start | bytes 184328 | tf_op jit(solution)/shard_map/ppermute | solution.py:143
  81.2 1.8 collective-permute-done.9
  83.0 5.1 %collective-permute-start.10 = (bf16[40,2,3,128]{3,0,2,1:T(8,128)(2,1)S(1)}, bf16[40,2,3,128]{3,0,2,1:T(8,128)(2,1)}, u32[]{:S(2)}, u32[]{:S(2)}) collective-permute-start(bf16[40,2,3,128]{3,0,2,1:T(8,128)(2,1)S(1)} %collective-permute-done.9), channel_id=1, source_target_pairs={{0,120},{8,0},{16,8},{24,16},{32,24},{40,32},{48,40},{56,48},{64,5... | collective-permute-start | bytes 184328 | tf_op jit(solution)/shard_map/ppermute | solution.py:143
  88.6 0.8 copy.100
  90.9 3.5 %collective-permute-start.11 = (bf16[40,2,3,128]{3,0,2,1:T(8,128)(2,1)}, bf16[40,2,3,128]{3,0,2,1:T(8,128)(2,1)S(1)}, u32[]{:S(2)}, u32[]{:S(2)}) collective-permute-start(bf16[40,2,3,128]{3,0,2,1:T(8,128)(2,1)} %collective-permute-done.10), channel_id=1, source_target_pairs={{0,120},{8,0},{16,8},{24,16},{32,24},{40,32},{48,40},{56,48},{64,5... | collective-permute-start | bytes 184328 | tf_op jit(solution)/shard_map/ppermute | solution.py:143
  94.4 0.7 bitcast_dynamic-update-slice_fusion.14
  95.1 1.9 collective-permute-done.11
  97.0 3.8 %collective-permute-start.12 = (bf16[40,2,3,128]{3,0,2,1:T(8,128)(2,1)S(1)}, bf16[40,2,3,128]{3,0,2,1:T(8,128)(2,1)S(1)}, u32[]{:S(2)}, u32[]{:S(2)}) collective-permute-start(bf16[40,2,3,128]{3,0,2,1:T(8,128)(2,1)S(1)} %collective-permute-done.11), channel_id=1, source_target_pairs={{0,120},{8,0},{16,8},{24,16},{32,24},{40,32},{48,40},{56,48},{64,5... | collective-permute-start | bytes 184328 | tf_op jit(solution)/shard_map/ppermute | solution.py:143
  101.3 0.7 collective-permute-done.12
  102.0 4.9 %collective-permute-start.13 = (bf16[40,2,3,128]{3,0,2,1:T(8,128)(2,1)S(1)}, bf16[40,2,3,128]{3,0,2,1:T(8,128)(2,1)S(1)}, u32[]{:S(2)}, u32[]{:S(2)}) collective-permute-start(bf16[40,2,3,128]{3,0,2,1:T(8,128)(2,1)S(1)} %collective-permute-done.12), channel_id=1, source_target_pairs={{0,120},{8,0},{16,8},{24,16},{32,24},{40,32},{48,40},{56,48},{64,5... | collective-permute-start | bytes 184328 | tf_op jit(solution)/shard_map/ppermute | solution.py:143
  107.1 1.1 collective-permute-done.13
  108.2 4.9 %collective-permute-start.14 = (bf16[40,2,3,128]{3,0,2,1:T(8,128)(2,1)S(1)}, bf16[40,2,3,128]{3,0,2,1:T(8,128)(2,1)S(1)}, u32[]{:S(2)}, u32[]{:S(2)}) collective-permute-start(bf16[40,2,3,128]{3,0,2,1:T(8,128)(2,1)S(1)} %collective-permute-done.13), channel_id=1, source_target_pairs={{0,120},{8,0},{16,8},{24,16},{32,24},{40,32},{48,40},{56,48},{64,5... | collective-permute-start | bytes 184328 | tf_op jit(solution)/shard_map/ppermute | solution.py:143
  113.1 0.7 fusion.1
  114.4 4.9 %collective-permute-start.15 = (bf16[40,2,3,128]{3,0,2,1:T(8,128)(2,1)S(1)}, bf16[40,2,3,128]{3,0,2,1:T(8,128)(2,1)S(1)}, u32[]{:S(2)}, u32[]{:S(2)}) collective-permute-start(bf16[40,2,3,128]{3,0,2,1:T(8,128)(2,1)S(1)} %collective-permute-done.14), channel_id=1, source_target_pairs={{0,120},{8,0},{16,8},{24,16},{32,24},{40,32},{48,40},{56,48},{64,5... | collective-permute-start | bytes 184328 | tf_op jit(solution)/shard_map/ppermute | solution.py:143
  119.3 0.7 fusion
  120.5 4.9 %collective-permute-start.16 = (bf16[40,2,3,128]{3,0,2,1:T(8,128)(2,1)S(1)}, bf16[40,2,3,128]{3,0,2,1:T(8,128)(2,1)S(1)}, u32[]{:S(2)}, u32[]{:S(2)}) collective-permute-start(bf16[40,2,3,128]{3,0,2,1:T(8,128)(2,1)S(1)} %collective-permute-done.15), channel_id=1, source_target_pairs={{0,120},{8,0},{16,8},{24,16},{32,24},{40,32},{48,40},{56,48},{64,5... | collective-permute-start | bytes 184328 | tf_op jit(solution)/shard_map/ppermute | solution.py:143
  125.4 1.2 fusion.3
  126.9 5.3 %collective-permute-start.17 = (bf16[40,2,3,128]{3,0,2,1:T(8,128)(2,1)S(1)}, bf16[40,2,3,128]{3,0,2,1:T(8,128)(2,1)S(1)}, u32[]{:S(2)}, u32[]{:S(2)}) collective-permute-start(bf16[40,2,3,128]{3,0,2,1:T(8,128)(2,1)S(1)} %collective-permute-done.16), channel_id=1, source_target_pairs={{0,120},{8,0},{16,8},{24,16},{32,24},{40,32},{48,40},{56,48},{64,5... | collective-permute-start | bytes 184328 | tf_op jit(solution)/shard_map/ppermute | solution.py:143
  132.2 1.3 collective-permute-done.17
  133.6 0.8 bitcast_dynamic-update-slice_fusion.6
  134.7 1.1 fusion.78
  136.3 1.1 fusion.80
  137.9 1.1 fusion.81
  140.3 4.1 %collective-permute-start.19 = (f32[32,3,129]{2,0,1:T(8,128)S(1)}, f32[32,3,129]{2,0,1:T(8,128)S(1)}, u32[]{:S(2)}, u32[]{:S(2)}) collective-permute-start(f32[32,3,129]{2,0,1:T(8,128)S(1)} %pad_maximum_fusion.2), channel_id=1, source_target_pairs={{0,128},{8,136},{16,144},{24,152},{32,160},{40,168},{48,176},{56,1... | collective-permute-start | bytes 148616 | tf_op jit(solution)/shard_map/ppermute | solution.py:166
  145.2 6.4 %all-to-all-start.1 = ((f32[8,8,3,129]{3,1,2,0:T(8,128)}), f32[8,8,3,129]{3,1,2,0:T(8,128)S(1)}, u32[]{:S(2)}, u32[]{:S(2)}) async-start(f32[8,8,3,129]{3,1,2,0:T(8,128)} %pad_maximum_fusion.1), calls=%async_computation.1 | async-start | bytes 393216 | tf_op jit(solution)/shard_map/all_to_all | solution.py:181
  152.6 7.7 %all-to-all-done.1 = f32[8,8,3,129]{3,1,2,0:T(8,128)S(1)} async-done(((f32[8,8,3,129]{3,1,2,0:T(8,128)}), f32[8,8,3,129]{3,1,2,0:T(8,128)S(1)}, u32[]{:S(2)}, u32[]{:S(2)}) %all-to-all-start.1) | async-done | bytes 99104 | tf_op jit(solution)/shard_map/all_to_all | solution.py:181
  162.5 45.1 %all-gather.2.cloned.1.call-done = bf16[256,3072]{0,1:T(8,128)(2,1)} async-done(((bf16[256,384]{0,1:T(8,128)(2,1)}), bf16[256,3072]{0,1:T(8,128)(2,1)}) %all-gather.2.cloned.1.call-update) | async-done | bytes 1572880 | tf_op jit(solution)/shard_map/all_gather | solution.py:202
  207.6 4.7 %convolution_convert_fusion = bf16[256,640]{1,0:T(8,128)(2,1)} fusion(bf16[256,3072]{0,1:T(8,128)(2,1)} %all-gather.2.cloned.1.call-done, bf16[3072,640]{1,0:T(8,128)(2,1)} %param.9), kind=kOutput, calls=%fused_computation.7 | convolution fusion | flops 1006796800 | bytes 5832704 | tf_op jit(solution)/shard_map/dot_general | solution.py:201
  (179 shorter events, 15.1 us)
Async XLA Ops:
  6.5 17.2 %copy-start = (bf16[256,384]{1,0:T(8,128)(2,1)S(1)}, bf16[256,384]{1,0:T(8,128)(2,1)}, u32[]{:S(2)}) copy-start(bf16[256,384]{1,0:T(8,128)(2,1)} %param.7) | copy-start | bytes 589828
  6.5 17.4 %copy-start.1 = (bf16[256,384]{1,0:T(8,128)(2,1)S(1)}, bf16[256,384]{1,0:T(8,128)(2,1)}, u32[]{:S(2)}) copy-start(bf16[256,384]{1,0:T(8,128)(2,1)} %param.6) | copy-start | bytes 589828
  6.5 16.6 %copy-start.28 = (s32[3,3]{1,0:T(4,128)S(1)}, s32[3,3]{1,0:T(4,128)}, u32[]{:S(2)}) copy-start(s32[3,3]{1,0:T(4,128)} %param.8) | copy-start | bytes 112
  6.5 29.8 %copy-start.2 = (bf16[256,384]{1,0:T(8,128)(2,1)S(1)}, bf16[256,384]{1,0:T(8,128)(2,1)}, u32[]{:S(2)}) copy-start(bf16[256,384]{1,0:T(8,128)(2,1)} %param.5) | copy-start | bytes 589828
  9.1 97.8 %collective-permute-start.2 = (bf16[256,2,3,128]{3,0,2,1:T(8,128)(2,1)S(1)}, bf16[256,2,3,128]{3,0,2,1:T(8,128)(2,1)S(1)}, u32[]{:S(2)}, u32[]{:S(2)}) collective-permute-start(bf16[256,2,3,128]{3,0,2,1:T(8,128)(2,1)S(1)} %pad_maximum_fusion), channel_id=1, source_target_pairs={{0,8},{8,16},{16,24},{32,40},{40,48},{48,56},{64,72},{72,80},{80,8... | collective-permute-start | bytes 1179656 | tf_op jit(solution)/shard_map/ppermute | solution.py:121
  14.0 93.0 %collective-permute-start.1 = (bf16[256,2,3,128]{3,0,2,1:T(8,128)(2,1)S(1)}, bf16[256,2,3,128]{3,0,2,1:T(8,128)(2,1)S(1)}, u32[]{:S(2)}, u32[]{:S(2)}) collective-permute-start(bf16[256,2,3,128]{3,0,2,1:T(8,128)(2,1)S(1)} %pad_maximum_fusion), channel_id=1, source_target_pairs={{0,16},{8,24},{32,48},{40,56},{64,80},{72,88},{96,112},{104,120},{... | collective-permute-start | bytes 1179656 | tf_op jit(solution)/shard_map/ppermute | solution.py:121
  19.8 87.2 %collective-permute-start = (bf16[256,2,3,128]{3,0,2,1:T(8,128)(2,1)S(1)}, bf16[256,2,3,128]{3,0,2,1:T(8,128)(2,1)S(1)}, u32[]{:S(2)}, u32[]{:S(2)}) collective-permute-start(bf16[256,2,3,128]{3,0,2,1:T(8,128)(2,1)S(1)} %pad_maximum_fusion), channel_id=1, source_target_pairs={{0,24},{32,56},{64,88},{96,120},{128,152},{160,184},{192,216},{224... | collective-permute-start | bytes 1179656 | tf_op jit(solution)/shard_map/ppermute | solution.py:121
  25.7 20.7 %collective-permute-start.3 = (bf16[40,2,3,128]{3,0,2,1:T(8,128)(2,1)S(1)}, bf16[40,2,3,128]{3,0,2,1:T(8,128)(2,1)S(1)}, u32[]{:S(2)}, u32[]{:S(2)}) collective-permute-start(bf16[40,2,3,128]{3,0,2,1:T(8,128)(2,1)S(1)} %maximum_maximum_fusion.1), channel_id=1, source_target_pairs={{0,120},{8,0},{16,8},{24,16},{32,24},{40,32},{48,40},{56,48},{64,5... | collective-permute-start | bytes 184328 | tf_op jit(solution)/shard_map/ppermute | solution.py:143
  37.2 97.5 %all-to-all-start = ((bf16[8,8,3,128]{3,1,2,0:T(8,128)(2,1)}), bf16[8,8,3,128]{3,1,2,0:T(8,128)(2,1)}, u32[]{:S(2)}, u32[]{:S(2)}) async-start(bf16[8,8,3,128]{3,1,2,0:T(8,128)(2,1)} %broadcast_in_dim.153), calls=%async_computation | async-start | bytes 98304 | tf_op jit(solution)/shard_map/all_to_all | solution.py:176
  44.8 91.5 %collective-permute-start.18 = (bf16[32,3,128]{2,0,1:T(8,128)(2,1)}, bf16[32,3,128]{2,0,1:T(8,128)(2,1)}, u32[]{:S(2)}, u32[]{:S(2)}) collective-permute-start(bf16[32,3,128]{2,0,1:T(8,128)(2,1)} %convert_bitcast_fusion.2), channel_id=1, source_target_pairs={{128,0},{136,8},{144,16},{152,24},{160,32},{168,40},{176,48},{184,... | collective-permute-start | bytes 73736 | tf_op jit(solution)/shard_map/ppermute | solution.py:164
  46.4 44.4 %copy-start.4 = (bf16[40,2,3,128]{3,0,2,1:T(8,128)(2,1)}, bf16[40,2,3,128]{3,0,2,1:T(8,128)(2,1)S(1)}, u32[]{:S(2)}) copy-start(bf16[40,2,3,128]{3,0,2,1:T(8,128)(2,1)S(1)} %collective-permute-done.3) | copy-start | bytes 184324
  46.4 5.4 %collective-permute-start.4 = (bf16[40,2,3,128]{3,0,2,1:T(8,128)(2,1)S(1)}, bf16[40,2,3,128]{3,0,2,1:T(8,128)(2,1)S(1)}, u32[]{:S(2)}, u32[]{:S(2)}) collective-permute-start(bf16[40,2,3,128]{3,0,2,1:T(8,128)(2,1)S(1)} %collective-permute-done.3), channel_id=1, source_target_pairs={{0,120},{8,0},{16,8},{24,16},{32,24},{40,32},{48,40},{56,48},{64,5... | collective-permute-start | bytes 184328 | tf_op jit(solution)/shard_map/ppermute | solution.py:143
  51.8 36.8 %copy-start.6 = (bf16[40,2,3,128]{3,0,2,1:T(8,128)(2,1)}, bf16[40,2,3,128]{3,0,2,1:T(8,128)(2,1)S(1)}, u32[]{:S(2)}) copy-start(bf16[40,2,3,128]{3,0,2,1:T(8,128)(2,1)S(1)} %collective-permute-done.4) | copy-start | bytes 184324
  51.8 5.9 %collective-permute-start.5 = (bf16[40,2,3,128]{3,0,2,1:T(8,128)(2,1)S(1)}, bf16[40,2,3,128]{3,0,2,1:T(8,128)(2,1)S(1)}, u32[]{:S(2)}, u32[]{:S(2)}) collective-permute-start(bf16[40,2,3,128]{3,0,2,1:T(8,128)(2,1)S(1)} %collective-permute-done.4), channel_id=1, source_target_pairs={{0,120},{8,0},{16,8},{24,16},{32,24},{40,32},{48,40},{56,48},{64,5... | collective-permute-start | bytes 184328 | tf_op jit(solution)/shard_map/ppermute | solution.py:143
  57.7 33.2 %copy-start.8 = (bf16[40,2,3,128]{3,0,2,1:T(8,128)(2,1)}, bf16[40,2,3,128]{3,0,2,1:T(8,128)(2,1)S(1)}, u32[]{:S(2)}) copy-start(bf16[40,2,3,128]{3,0,2,1:T(8,128)(2,1)S(1)} %collective-permute-done.5) | copy-start | bytes 184324
  57.7 6.3 %collective-permute-start.6 = (bf16[40,2,3,128]{3,0,2,1:T(8,128)(2,1)S(1)}, bf16[40,2,3,128]{3,0,2,1:T(8,128)(2,1)S(1)}, u32[]{:S(2)}, u32[]{:S(2)}) collective-permute-start(bf16[40,2,3,128]{3,0,2,1:T(8,128)(2,1)S(1)} %collective-permute-done.5), channel_id=1, source_target_pairs={{0,120},{8,0},{16,8},{24,16},{32,24},{40,32},{48,40},{56,48},{64,5... | collective-permute-start | bytes 184328 | tf_op jit(solution)/shard_map/ppermute | solution.py:143
  64.0 26.9 %copy-start.10 = (bf16[40,2,3,128]{3,0,2,1:T(8,128)(2,1)}, bf16[40,2,3,128]{3,0,2,1:T(8,128)(2,1)S(1)}, u32[]{:S(2)}) copy-start(bf16[40,2,3,128]{3,0,2,1:T(8,128)(2,1)S(1)} %collective-permute-done.6) | copy-start | bytes 184324
  64.0 6.2 %collective-permute-start.7 = (bf16[40,2,3,128]{3,0,2,1:T(8,128)(2,1)S(1)}, bf16[40,2,3,128]{3,0,2,1:T(8,128)(2,1)S(1)}, u32[]{:S(2)}, u32[]{:S(2)}) collective-permute-start(bf16[40,2,3,128]{3,0,2,1:T(8,128)(2,1)S(1)} %collective-permute-done.6), channel_id=1, source_target_pairs={{0,120},{8,0},{16,8},{24,16},{32,24},{40,32},{48,40},{56,48},{64,5... | collective-permute-start | bytes 184328 | tf_op jit(solution)/shard_map/ppermute | solution.py:143
  70.1 20.7 %copy-start.12 = (bf16[40,2,3,128]{3,0,2,1:T(8,128)(2,1)}, bf16[40,2,3,128]{3,0,2,1:T(8,128)(2,1)S(1)}, u32[]{:S(2)}) copy-start(bf16[40,2,3,128]{3,0,2,1:T(8,128)(2,1)S(1)} %collective-permute-done.7) | copy-start | bytes 184324
  70.1 6.2 %collective-permute-start.8 = (bf16[40,2,3,128]{3,0,2,1:T(8,128)(2,1)S(1)}, bf16[40,2,3,128]{3,0,2,1:T(8,128)(2,1)S(1)}, u32[]{:S(2)}, u32[]{:S(2)}) collective-permute-start(bf16[40,2,3,128]{3,0,2,1:T(8,128)(2,1)S(1)} %collective-permute-done.7), channel_id=1, source_target_pairs={{0,120},{8,0},{16,8},{24,16},{32,24},{40,32},{48,40},{56,48},{64,5... | collective-permute-start | bytes 184328 | tf_op jit(solution)/shard_map/ppermute | solution.py:143
  76.3 14.6 %copy-start.14 = (bf16[40,2,3,128]{3,0,2,1:T(8,128)(2,1)}, bf16[40,2,3,128]{3,0,2,1:T(8,128)(2,1)S(1)}, u32[]{:S(2)}) copy-start(bf16[40,2,3,128]{3,0,2,1:T(8,128)(2,1)S(1)} %collective-permute-done.8) | copy-start | bytes 184324
  76.3 6.7 %collective-permute-start.9 = (bf16[40,2,3,128]{3,0,2,1:T(8,128)(2,1)S(1)}, bf16[40,2,3,128]{3,0,2,1:T(8,128)(2,1)S(1)}, u32[]{:S(2)}, u32[]{:S(2)}) collective-permute-start(bf16[40,2,3,128]{3,0,2,1:T(8,128)(2,1)S(1)} %collective-permute-done.8), channel_id=1, source_target_pairs={{0,120},{8,0},{16,8},{24,16},{32,24},{40,32},{48,40},{56,48},{64,5... | collective-permute-start | bytes 184328 | tf_op jit(solution)/shard_map/ppermute | solution.py:143
  83.0 7.9 %copy-start.16 = (bf16[40,2,3,128]{3,0,2,1:T(8,128)(2,1)}, bf16[40,2,3,128]{3,0,2,1:T(8,128)(2,1)S(1)}, u32[]{:S(2)}) copy-start(bf16[40,2,3,128]{3,0,2,1:T(8,128)(2,1)S(1)} %collective-permute-done.9) | copy-start | bytes 184324
  83.0 7.9 %collective-permute-start.10 = (bf16[40,2,3,128]{3,0,2,1:T(8,128)(2,1)S(1)}, bf16[40,2,3,128]{3,0,2,1:T(8,128)(2,1)}, u32[]{:S(2)}, u32[]{:S(2)}) collective-permute-start(bf16[40,2,3,128]{3,0,2,1:T(8,128)(2,1)S(1)} %collective-permute-done.9), channel_id=1, source_target_pairs={{0,120},{8,0},{16,8},{24,16},{32,24},{40,32},{48,40},{56,48},{64,5... | collective-permute-start | bytes 184328 | tf_op jit(solution)/shard_map/ppermute | solution.py:143
  89.5 23.6 %copy-start.3 = (bf16[256,384]{0,1:T(8,128)(2,1)S(1)}, bf16[256,384]{0,1:T(8,128)(2,1)}, u32[]{:S(2)}) copy-start(bf16[256,384]{0,1:T(8,128)(2,1)} %copy.100) | copy-start | bytes 589828
  90.9 6.1 %collective-permute-start.11 = (bf16[40,2,3,128]{3,0,2,1:T(8,128)(2,1)}, bf16[40,2,3,128]{3,0,2,1:T(8,128)(2,1)S(1)}, u32[]{:S(2)}, u32[]{:S(2)}) collective-permute-start(bf16[40,2,3,128]{3,0,2,1:T(8,128)(2,1)} %collective-permute-done.10), channel_id=1, source_target_pairs={{0,120},{8,0},{16,8},{24,16},{32,24},{40,32},{48,40},{56,48},{64,5... | collective-permute-start | bytes 184328 | tf_op jit(solution)/shard_map/ppermute | solution.py:143
  97.0 5.0 %collective-permute-start.12 = (bf16[40,2,3,128]{3,0,2,1:T(8,128)(2,1)S(1)}, bf16[40,2,3,128]{3,0,2,1:T(8,128)(2,1)S(1)}, u32[]{:S(2)}, u32[]{:S(2)}) collective-permute-start(bf16[40,2,3,128]{3,0,2,1:T(8,128)(2,1)S(1)} %collective-permute-done.11), channel_id=1, source_target_pairs={{0,120},{8,0},{16,8},{24,16},{32,24},{40,32},{48,40},{56,48},{64,5... | collective-permute-start | bytes 184328 | tf_op jit(solution)/shard_map/ppermute | solution.py:143
  102.0 6.2 %collective-permute-start.13 = (bf16[40,2,3,128]{3,0,2,1:T(8,128)(2,1)S(1)}, bf16[40,2,3,128]{3,0,2,1:T(8,128)(2,1)S(1)}, u32[]{:S(2)}, u32[]{:S(2)}) collective-permute-start(bf16[40,2,3,128]{3,0,2,1:T(8,128)(2,1)S(1)} %collective-permute-done.12), channel_id=1, source_target_pairs={{0,120},{8,0},{16,8},{24,16},{32,24},{40,32},{48,40},{56,48},{64,5... | collective-permute-start | bytes 184328 | tf_op jit(solution)/shard_map/ppermute | solution.py:143
  108.2 6.2 %collective-permute-start.14 = (bf16[40,2,3,128]{3,0,2,1:T(8,128)(2,1)S(1)}, bf16[40,2,3,128]{3,0,2,1:T(8,128)(2,1)S(1)}, u32[]{:S(2)}, u32[]{:S(2)}) collective-permute-start(bf16[40,2,3,128]{3,0,2,1:T(8,128)(2,1)S(1)} %collective-permute-done.13), channel_id=1, source_target_pairs={{0,120},{8,0},{16,8},{24,16},{32,24},{40,32},{48,40},{56,48},{64,5... | collective-permute-start | bytes 184328 | tf_op jit(solution)/shard_map/ppermute | solution.py:143
  114.4 6.2 %collective-permute-start.15 = (bf16[40,2,3,128]{3,0,2,1:T(8,128)(2,1)S(1)}, bf16[40,2,3,128]{3,0,2,1:T(8,128)(2,1)S(1)}, u32[]{:S(2)}, u32[]{:S(2)}) collective-permute-start(bf16[40,2,3,128]{3,0,2,1:T(8,128)(2,1)S(1)} %collective-permute-done.14), channel_id=1, source_target_pairs={{0,120},{8,0},{16,8},{24,16},{32,24},{40,32},{48,40},{56,48},{64,5... | collective-permute-start | bytes 184328 | tf_op jit(solution)/shard_map/ppermute | solution.py:143
  120.0 14.5 %copy-start.17 = (bf16[40,2,3,128]{3,0,2,1:T(8,128)(2,1)S(1)}, bf16[40,2,3,128]{3,0,2,1:T(8,128)(2,1)}, u32[]{:S(2)}) copy-start(bf16[40,2,3,128]{3,0,2,1:T(8,128)(2,1)} %copy-done.16) | copy-start | bytes 184324
  120.0 14.5 %copy-start.15 = (bf16[40,2,3,128]{3,0,2,1:T(8,128)(2,1)S(1)}, bf16[40,2,3,128]{3,0,2,1:T(8,128)(2,1)}, u32[]{:S(2)}) copy-start(bf16[40,2,3,128]{3,0,2,1:T(8,128)(2,1)} %copy-done.14) | copy-start | bytes 184324
  120.0 14.5 %copy-start.13 = (bf16[40,2,3,128]{3,0,2,1:T(8,128)(2,1)S(1)}, bf16[40,2,3,128]{3,0,2,1:T(8,128)(2,1)}, u32[]{:S(2)}) copy-start(bf16[40,2,3,128]{3,0,2,1:T(8,128)(2,1)} %copy-done.12) | copy-start | bytes 184324
  120.0 14.5 %copy-start.11 = (bf16[40,2,3,128]{3,0,2,1:T(8,128)(2,1)S(1)}, bf16[40,2,3,128]{3,0,2,1:T(8,128)(2,1)}, u32[]{:S(2)}) copy-start(bf16[40,2,3,128]{3,0,2,1:T(8,128)(2,1)} %copy-done.10) | copy-start | bytes 184324
  120.0 14.5 %copy-start.9 = (bf16[40,2,3,128]{3,0,2,1:T(8,128)(2,1)S(1)}, bf16[40,2,3,128]{3,0,2,1:T(8,128)(2,1)}, u32[]{:S(2)}) copy-start(bf16[40,2,3,128]{3,0,2,1:T(8,128)(2,1)} %copy-done.8) | copy-start | bytes 184324
  120.0 14.6 %copy-start.7 = (bf16[40,2,3,128]{3,0,2,1:T(8,128)(2,1)S(1)}, bf16[40,2,3,128]{3,0,2,1:T(8,128)(2,1)}, u32[]{:S(2)}) copy-start(bf16[40,2,3,128]{3,0,2,1:T(8,128)(2,1)} %copy-done.6) | copy-start | bytes 184324
  120.0 14.6 %copy-start.5 = (bf16[40,2,3,128]{3,0,2,1:T(8,128)(2,1)S(1)}, bf16[40,2,3,128]{3,0,2,1:T(8,128)(2,1)}, u32[]{:S(2)}) copy-start(bf16[40,2,3,128]{3,0,2,1:T(8,128)(2,1)} %copy-done.4) | copy-start | bytes 184324
  120.5 6.3 %collective-permute-start.16 = (bf16[40,2,3,128]{3,0,2,1:T(8,128)(2,1)S(1)}, bf16[40,2,3,128]{3,0,2,1:T(8,128)(2,1)S(1)}, u32[]{:S(2)}, u32[]{:S(2)}) collective-permute-start(bf16[40,2,3,128]{3,0,2,1:T(8,128)(2,1)S(1)} %collective-permute-done.15), channel_id=1, source_target_pairs={{0,120},{8,0},{16,8},{24,16},{32,24},{40,32},{48,40},{56,48},{64,5... | collective-permute-start | bytes 184328 | tf_op jit(solution)/shard_map/ppermute | solution.py:143
  126.9 6.6 %collective-permute-start.17 = (bf16[40,2,3,128]{3,0,2,1:T(8,128)(2,1)S(1)}, bf16[40,2,3,128]{3,0,2,1:T(8,128)(2,1)S(1)}, u32[]{:S(2)}, u32[]{:S(2)}) collective-permute-start(bf16[40,2,3,128]{3,0,2,1:T(8,128)(2,1)S(1)} %collective-permute-done.16), channel_id=1, source_target_pairs={{0,120},{8,0},{16,8},{24,16},{32,24},{40,32},{48,40},{56,48},{64,5... | collective-permute-start | bytes 184328 | tf_op jit(solution)/shard_map/ppermute | solution.py:143
  136.0 3.7 %copy-start.19 = (bf16[8,3,128]{2,0,1:T(8,128)(2,1)S(1)}, bf16[8,3,128]{2,0,1:T(8,128)(2,1)}, u32[]{:S(2)}) copy-start(bf16[8,3,128]{2,0,1:T(8,128)(2,1)} %copy-done.18) | copy-start | bytes 18436
  136.3 15.5 %copy-start.25 = (pred[8,3]{0,1:T(4,128)(4,1)S(1)}, pred[8,3]{0,1:T(4,128)(4,1)}, u32[]{:S(2)}) copy-start(pred[8,3]{0,1:T(4,128)(4,1)} %get-tuple-element.15) | copy-start | bytes 76
  137.6 14.9 %copy-start.23 = (f32[256,3]{0,1:T(4,128)S(1)}, f32[256,3]{0,1:T(4,128)}, u32[]{:S(2)}) copy-start(f32[256,3]{0,1:T(4,128)} %mul.135) | copy-start | bytes 9220
  137.9 22.6 %copy-start.26 = (pred[8]{0:T(512)(128)(4,1)S(1)}, pred[8]{0:T(512)(128)(4,1)}, u32[]{:S(2)}) copy-start(pred[8]{0:T(512)(128)(4,1)} %iota_compare_fusion.6) | copy-start | bytes 28
  138.9 21.8 %copy-start.27 = (pred[32,3]{0,1:T(4,128)(4,1)S(1)}, pred[32,3]{0,1:T(4,128)(4,1)}, u32[]{:S(2)}) copy-start(pred[32,3]{0,1:T(4,128)(4,1)} %get-tuple-element.18) | copy-start | bytes 292
  140.2 21.3 %copy-start.22 = (f32[256,3]{0,1:T(4,128)S(1)}, f32[256,3]{0,1:T(4,128)}, u32[]{:S(2)}) copy-start(f32[256,3]{0,1:T(4,128)} %mul.143) | copy-start | bytes 9220
  140.3 11.4 %collective-permute-start.19 = (f32[32,3,129]{2,0,1:T(8,128)S(1)}, f32[32,3,129]{2,0,1:T(8,128)S(1)}, u32[]{:S(2)}, u32[]{:S(2)}) collective-permute-start(f32[32,3,129]{2,0,1:T(8,128)S(1)} %pad_maximum_fusion.2), channel_id=1, source_target_pairs={{0,128},{8,136},{16,144},{24,152},{32,160},{40,168},{48,176},{56,1... | collective-permute-start | bytes 148616 | tf_op jit(solution)/shard_map/ppermute | solution.py:166
  145.2 15.1 %all-to-all-start.1 = ((f32[8,8,3,129]{3,1,2,0:T(8,128)}), f32[8,8,3,129]{3,1,2,0:T(8,128)S(1)}, u32[]{:S(2)}, u32[]{:S(2)}) async-start(f32[8,8,3,129]{3,1,2,0:T(8,128)} %pad_maximum_fusion.1), calls=%async_computation.1 | async-start | bytes 393216 | tf_op jit(solution)/shard_map/all_to_all | solution.py:181
  151.6 55.9 %all-gather.2.cloned.1.call-start = ((), (), s32[]{:S(2)}) async-start(), calls=%async_computation.2 | async-start | bytes 1769472 | tf_op jit(solution)/shard_map/all_gather | solution.py:202
  (4 other events, 5.5 us)
Sparse Core Ops, SparseCore 0:
  162.6 44.9 all-gather.1

commit v7 on v5

--- a/solution.py
+++ b/solution.py
@@ -134,8 +134,7 @@
     chooser2, query2, pair2 = level_setup(query_all, key_all, value_all, level_offsets[2], RATE_TOP)
     count1 = pair1.shape[0]
     count2 = pair2.shape[0]
-    ring = lax.all_gather(jnp.concatenate([pair1, pair2], axis=0), "zl")
-    ring = lax.all_gather(ring, "zh").reshape(row_len, *ring.shape[1:])
+    ring = lax.all_gather(jnp.concatenate([pair1, pair2], axis=0), ("zh", "zl"))
     row1 = ring[:, :count1]
     row2 = ring[:, count1:]
 

time: 180 us -> 160 us (0.89)
  blocking collectives: 69.5 us -> 48.3 us
    all_gather x2 -> x1, blocking collectives: 69.5 us -> 48.3 us  [local(): ring = lax.all_gather(jnp.concatenate([pair1, pair2], axis=0), ('zh', 'zl'))]
  transfers between devices with their start and end apart: 8 -> 8, of which waited for: 3 -> 3; matrix products, arithmetic and copies ran while one was open for 7% -> 8% of each run, Pallas kernels for 0% -> 0%
where the time goes in v7:
time: 160 us
  blocking collectives  48.3 us (30%)
  waiting for transfers between devices  42.5 us (27%)
  starting transfers between devices  31.5 us (20%)
  between operations  14 us (9%)
  matrix products  9.68 us (6%)
  other arithmetic  7.82 us (5%)
  local copies, waits for them, and re-layouts  6.28 us (4%)
    all_gather x1, blocking collectives, local(): ring = lax.all_gather(jnp.concatenate([pair1, pair2], axis=0), ('zh', 'zl'))  48.3 us
    all_gather x1, waiting for transfers between devices, local(): lax.all_gather(heads_out, 'head', axis=1, tiled=True)  33.2 us
    ppermute x3, starting transfers between devices, local(): arrived.append(lax.ppermute(pair0, SEQ_AXES, pairs))  12 us
    all_to_all x1, waiting for transfers between devices, local(): returned = lax.all_to_all(packed, 'sy', 0, 0, tiled=True)  8.55 us
    all_to_all x1, starting transfers between devices, local(): returned = lax.all_to_all(packed, 'sy', 0, 0, tiled=True)  8 us
    all_to_all x1, starting transfers between devices, local(): column_queries = lax.all_to_all(copies, 'sy', 0, 0, tiled=True)  6.82 us
    dot_general x1, matrix products, local(): jnp.dot(lax.all_gather(heads_out, 'head', axis=1, tiled=True), out_weight...  4.73 us
    ppermute x1, starting transfers between devices, local(): lax.ppermute(pack(*whole_row(visiting1, row1, count1)), SEQ_AXES, down)  3.37 us
  transfers between devices with their start and end apart: 8, of which 3 were waited for; matrix products, arithmetic and copies ran while one was open for 8% of the time, Pallas kernels for 0%

profile of v7, /device:TPU:1, one launch (start us, length us, event | category | flops | bytes accessed | tf_op | source)
XLA Modules:
  0.0 160.0 jit_solution(13678382697205978157)
XLA Ops:
  6.5 1.1 copy.52
  7.7 0.2 copy.54
  7.8 1.1 copy.51
  8.9 0.2 copy.53
  9.1 0.8 pad_maximum_fusion
  9.9 4.8 %collective-permute-start.2 = (bf16[256,2,3,128]{3,0,2,1:T(8,128)(2,1)}, bf16[256,2,3,128]{3,0,2,1:T(8,128)(2,1)S(1)}, u32[]{:S(2)}, u32[]{:S(2)}) collective-permute-start(bf16[256,2,3,128]{3,0,2,1:T(8,128)(2,1)} %pad_maximum_fusion), channel_id=1, source_target_pairs={{0,8},{8,16},{16,24},{32,40},{40,48},{48,56},{64,72},{72,80},{80,8... | collective-permute-start | bytes 1179656 | tf_op jit(solution)/shard_map/ppermute | solution.py:121
  14.7 5.8 %collective-permute-start.1 = (bf16[256,2,3,128]{3,0,2,1:T(8,128)(2,1)}, bf16[256,2,3,128]{3,0,2,1:T(8,128)(2,1)S(1)}, u32[]{:S(2)}, u32[]{:S(2)}) collective-permute-start(bf16[256,2,3,128]{3,0,2,1:T(8,128)(2,1)} %pad_maximum_fusion), channel_id=1, source_target_pairs={{0,16},{8,24},{32,48},{40,56},{64,80},{72,88},{96,112},{104,120},{... | collective-permute-start | bytes 1179656 | tf_op jit(solution)/shard_map/ppermute | solution.py:121
  20.5 1.3 collective-permute-start
  21.8 0.8 fusion.63
  22.6 0.6 iota_compare_fusion.4
  23.3 1.0 reshape_reshape.26
  24.4 0.6 broadcast_in_dim.153
  25.0 6.8 %all-to-all-start = ((bf16[8,8,3,128]{3,1,2,0:T(8,128)(2,1)}), bf16[8,8,3,128]{3,1,2,0:T(8,128)(2,1)S(1)}, u32[]{:S(2)}, u32[]{:S(2)}) async-start(bf16[8,8,3,128]{3,1,2,0:T(8,128)(2,1)} %broadcast_in_dim.153), calls=%async_computation | async-start | bytes 98304 | tf_op jit(solution)/shard_map/all_to_all | solution.py:170
  31.9 0.2 fusion.19
  32.1 1.3 collective-permute-start.3
  33.6 0.2 fusion.15
  33.8 0.2 fusion.17
  34.3 48.3 %all-gather = bf16[640,2,3,128]{3,0,2,1:T(8,128)(2,1)S(1)} all-gather(bf16[40,2,3,128]{3,0,2,1:T(8,128)(2,1)S(1)} %maximum_maximum_fusion.1), channel_id=2, replica_groups=mesh['sy'=8,'zh'=4,'zl'=4,'head'=8] {'zh','zl'}, dimensions={0}, use_global_device_ids=true | all-gather | bytes 1044480 | tf_op jit(solution)/shard_map/all_gather | solution.py:137
  82.8 0.3 fusion.81
  83.1 0.2 fusion.21
  83.3 0.2 convolution_bitcast_fusion.1
  83.6 0.2 fusion.79
  83.9 0.2 fusion.42
  84.1 0.2 fusion.7
  84.3 0.2 convolution_bitcast_fusion.3
  84.5 0.3 fusion.80
  84.8 0.2 fusion.22
  85.0 0.2 convolution_bitcast_fusion.2
  85.4 3.4 %collective-permute-start.4 = (f32[32,3,129]{2,0,1:T(8,128)S(1)}, f32[32,3,129]{2,0,1:T(8,128)S(1)}, u32[]{:S(2)}, u32[]{:S(2)}) collective-permute-start(f32[32,3,129]{2,0,1:T(8,128)S(1)} %pad_maximum_fusion.2), channel_id=1, source_target_pairs={{0,128},{8,136},{16,144},{24,152},{32,160},{40,168},{48,176},{56,1... | collective-permute-start | bytes 148616 | tf_op jit(solution)/shard_map/ppermute | solution.py:160
  88.8 0.5 iota_compare_fusion.6
  89.7 0.7 collective-permute-done.4
  91.0 0.2 copy.66
  91.2 0.3 fusion.78
  91.5 0.2 fusion.29
  91.7 0.2 convolution_bitcast_fusion
  92.0 0.2 copy.61
  92.2 0.7 pad_maximum_fusion.1
  92.9 8.0 %all-to-all-start.1 = ((f32[8,8,3,129]{3,1,2,0:T(8,128)}), f32[8,8,3,129]{3,1,2,0:T(8,128)S(1)}, u32[]{:S(2)}, u32[]{:S(2)}) async-start(f32[8,8,3,129]{3,1,2,0:T(8,128)} %pad_maximum_fusion.1), calls=%async_computation.1 | async-start | bytes 393216 | tf_op jit(solution)/shard_map/all_to_all | solution.py:175
  101.0 8.5 %all-to-all-done.1 = f32[8,8,3,129]{3,1,2,0:T(8,128)S(1)} async-done(((f32[8,8,3,129]{3,1,2,0:T(8,128)}), f32[8,8,3,129]{3,1,2,0:T(8,128)S(1)}, u32[]{:S(2)}, u32[]{:S(2)}) %all-to-all-start.1) | async-done | bytes 99104 | tf_op jit(solution)/shard_map/all_to_all | solution.py:175
  109.6 0.2 copy.90
  110.0 0.7 broadcast_select_fusion.1
  111.4 0.2 copy.71
  111.7 0.7 fusion.1
  112.4 0.7 fusion
  113.1 1.2 fusion.3
  114.5 0.7 divide_convert_fusion.4
  115.2 33.2 %all-gather.3.cloned.1.call-done = bf16[256,3072]{0,1:T(8,128)(2,1)} async-done(((bf16[256,384]{0,1:T(8,128)(2,1)}), bf16[256,3072]{0,1:T(8,128)(2,1)}) %all-gather.3.cloned.1.call-update) | async-done | bytes 1572880 | tf_op jit(solution)/shard_map/all_gather | solution.py:196
  148.4 4.7 %convolution_convert_fusion = bf16[256,640]{1,0:T(8,128)(2,1)} fusion(bf16[256,3072]{0,1:T(8,128)(2,1)} %all-gather.3.cloned.1.call-done, bf16[3072,640]{1,0:T(8,128)(2,1)} %param.9), kind=kOutput, calls=%fused_computation.7 | convolution fusion | flops 1006796800 | bytes 5832704 | tf_op jit(solution)/shard_map/dot_general | solution.py:195
  (84 shorter events, 3.2 us)
Async XLA Ops:
  6.5 26.9 %copy-start = (bf16[256,384]{1,0:T(8,128)(2,1)S(1)}, bf16[256,384]{1,0:T(8,128)(2,1)}, u32[]{:S(2)}) copy-start(bf16[256,384]{1,0:T(8,128)(2,1)} %param.7) | copy-start | bytes 589828
  6.5 27.0 %copy-start.1 = (bf16[256,384]{1,0:T(8,128)(2,1)S(1)}, bf16[256,384]{1,0:T(8,128)(2,1)}, u32[]{:S(2)}) copy-start(bf16[256,384]{1,0:T(8,128)(2,1)} %param.6) | copy-start | bytes 589828
  6.5 25.4 %copy-start.2 = (bf16[256,384]{1,0:T(8,128)(2,1)S(1)}, bf16[256,384]{1,0:T(8,128)(2,1)}, u32[]{:S(2)}) copy-start(bf16[256,384]{1,0:T(8,128)(2,1)} %param.5) | copy-start | bytes 589828
  9.9 101.7 %collective-permute-start.2 = (bf16[256,2,3,128]{3,0,2,1:T(8,128)(2,1)}, bf16[256,2,3,128]{3,0,2,1:T(8,128)(2,1)S(1)}, u32[]{:S(2)}, u32[]{:S(2)}) collective-permute-start(bf16[256,2,3,128]{3,0,2,1:T(8,128)(2,1)} %pad_maximum_fusion), channel_id=1, source_target_pairs={{0,8},{8,16},{16,24},{32,40},{40,48},{48,56},{64,72},{72,80},{80,8... | collective-permute-start | bytes 1179656 | tf_op jit(solution)/shard_map/ppermute | solution.py:121
  14.7 96.9 %collective-permute-start.1 = (bf16[256,2,3,128]{3,0,2,1:T(8,128)(2,1)}, bf16[256,2,3,128]{3,0,2,1:T(8,128)(2,1)S(1)}, u32[]{:S(2)}, u32[]{:S(2)}) collective-permute-start(bf16[256,2,3,128]{3,0,2,1:T(8,128)(2,1)} %pad_maximum_fusion), channel_id=1, source_target_pairs={{0,16},{8,24},{32,48},{40,56},{64,80},{72,88},{96,112},{104,120},{... | collective-permute-start | bytes 1179656 | tf_op jit(solution)/shard_map/ppermute | solution.py:121
  20.5 91.1 %collective-permute-start = (bf16[256,2,3,128]{3,0,2,1:T(8,128)(2,1)}, bf16[256,2,3,128]{3,0,2,1:T(8,128)(2,1)S(1)}, u32[]{:S(2)}, u32[]{:S(2)}) collective-permute-start(bf16[256,2,3,128]{3,0,2,1:T(8,128)(2,1)} %pad_maximum_fusion), channel_id=1, source_target_pairs={{0,24},{32,56},{64,88},{96,120},{128,152},{160,184},{192,216},{224... | collective-permute-start | bytes 1179656 | tf_op jit(solution)/shard_map/ppermute | solution.py:121
  25.0 66.2 %all-to-all-start = ((bf16[8,8,3,128]{3,1,2,0:T(8,128)(2,1)}), bf16[8,8,3,128]{3,1,2,0:T(8,128)(2,1)S(1)}, u32[]{:S(2)}, u32[]{:S(2)}) async-start(bf16[8,8,3,128]{3,1,2,0:T(8,128)(2,1)} %broadcast_in_dim.153), calls=%async_computation | async-start | bytes 98304 | tf_op jit(solution)/shard_map/all_to_all | solution.py:170
  32.1 52.4 %collective-permute-start.3 = (bf16[32,3,128]{2,0,1:T(8,128)(2,1)S(1)}, bf16[32,3,128]{2,0,1:T(8,128)(2,1)S(1)}, u32[]{:S(2)}, u32[]{:S(2)}) collective-permute-start(bf16[32,3,128]{2,0,1:T(8,128)(2,1)S(1)} %convert_bitcast_fusion.2), channel_id=1, source_target_pairs={{128,0},{136,8},{144,16},{152,24},{160,32},{168,40},{176,48},{184,... | collective-permute-start | bytes 73736 | tf_op jit(solution)/shard_map/ppermute | solution.py:158
  85.4 5.0 %collective-permute-start.4 = (f32[32,3,129]{2,0,1:T(8,128)S(1)}, f32[32,3,129]{2,0,1:T(8,128)S(1)}, u32[]{:S(2)}, u32[]{:S(2)}) collective-permute-start(f32[32,3,129]{2,0,1:T(8,128)S(1)} %pad_maximum_fusion.2), channel_id=1, source_target_pairs={{0,128},{8,136},{16,144},{24,152},{32,160},{40,168},{48,176},{56,1... | collective-permute-start | bytes 148616 | tf_op jit(solution)/shard_map/ppermute | solution.py:160
  89.5 20.3 %copy-start.3 = (pred[8]{0:T(512)(128)(4,1)S(1)}, pred[8]{0:T(512)(128)(4,1)}, u32[]{:S(2)}) copy-start(pred[8]{0:T(512)(128)(4,1)} %iota_compare_fusion.6) | copy-start | bytes 28
  92.9 16.6 %all-to-all-start.1 = ((f32[8,8,3,129]{3,1,2,0:T(8,128)}), f32[8,8,3,129]{3,1,2,0:T(8,128)S(1)}, u32[]{:S(2)}, u32[]{:S(2)}) async-start(f32[8,8,3,129]{3,1,2,0:T(8,128)} %pad_maximum_fusion.1), calls=%async_computation.1 | async-start | bytes 393216 | tf_op jit(solution)/shard_map/all_to_all | solution.py:175
  101.0 47.4 %all-gather.3.cloned.1.call-start = ((), (), s32[]{:S(2)}) async-start(), calls=%async_computation.2 | async-start | bytes 1769472 | tf_op jit(solution)/shard_map/all_gather | solution.py:196
Sparse Core Ops, SparseCore 0:
  115.3 32.9 all-gather.2

commit v8 on v7

--- a/solution.py
+++ b/solution.py
@@ -157,7 +157,11 @@
     down = [(s, s + row_len) for s in range(seq_count) if (s // row_len) % 2 == 0]
     visiting1 = lax.ppermute(query1, SEQ_AXES, up)
     own_out1, own_lse1 = own_row(query1, row1, count1)
-    cross1 = lax.ppermute(pack(*whole_row(visiting1, row1, count1)), SEQ_AXES, down)
+    early = full_outs[0].astype(jnp.bfloat16)
+    early, cross_send = lax.optimization_barrier(
+        (early, pack(*whole_row(visiting1, row1, count1)))
+    )
+    cross1 = lax.ppermute(cross_send, SEQ_AXES, down)
     cross_out1, cross_lse1 = unpack(cross1)
     cross_lse1 = jnp.where(row_y % 2 == 1, cross_lse1, NEG_FILL)
     out1, lse1 = merge([own_out1, cross_out1], [own_lse1, cross_lse1])
@@ -191,11 +195,48 @@
         jnp.sum(level_weights[..., None] * jnp.stack(full_outs), axis=0)
         / jnp.sum(level_weights, axis=0)[..., None]
     )
-    heads_out = mixed_heads.astype(jnp.bfloat16).reshape(row_count, head_count * head_width)
-    projected = jnp.dot(
-        lax.all_gather(heads_out, "head", axis=1, tiled=True),
-        out_weight,
-        preferred_element_type=jnp.float32,
+    heads_out = mixed_heads.astype(jnp.bfloat16)
+
+    early_all = lax.all_gather(
+        early.reshape(row_count, head_count * head_width), "head", axis=1, tiled=True
+    )
+    projected = jnp.dot(early_all, out_weight, preferred_element_type=jnp.float32)
+    delta = heads_out.astype(jnp.float32) - early.astype(jnp.float32)
+
+    def take(dense, chooser, spacing):
+        grouped = dense.reshape(row_count // spacing, spacing, head_count, head_width)
+        return jnp.sum(jnp.where(chooser[None, :, :, None], grouped, 0.0), axis=1)
+
+    is_mid = jnp.tile(chooser1, (row_count // RATE_MID, 1))
+    picked = jnp.concatenate(
+        [
+            take(delta, chooser1, RATE_MID),
+            take(jnp.where(is_mid[..., None], 0.0, delta), chooser2, RATE_TOP),
+        ],
+        axis=0,
+    )
+    picked_all = lax.all_gather(picked, "head", axis=1, tiled=True)
+    offsets_all = lax.all_gather(level_offsets, "head", axis=1, tiled=True)
+    heads_total = offsets_all.shape[1]
+    weight = out_weight.reshape(heads_total, head_width, out_weight.shape[1])
+    exact = lax.Precision.HIGHEST
+    products = jnp.einsum(
+        "nhd,hdc->hnc", picked_all, weight.astype(jnp.float32), precision=exact
+    )
+    mid_hot = (
+        lax.broadcasted_iota(jnp.int32, (heads_total, RATE_MID), 1)
+        == (offsets_all[1] % RATE_MID)[:, None]
+    ).astype(jnp.float32)
+    top_hot = (
+        lax.broadcasted_iota(jnp.int32, (heads_total, RATE_TOP), 1)
+        == (offsets_all[2] % RATE_TOP)[:, None]
+    ).astype(jnp.float32)
+    fix_mid = jnp.einsum("hnc,hr->nrc", products[:, :count1], mid_hot, precision=exact)
+    fix_top = jnp.einsum("hnc,hr->nrc", products[:, count1:], top_hot, precision=exact)
+    projected = (
+        projected
+        + fix_mid.reshape(row_count, -1)
+        + fix_top.reshape(row_count, -1)
     )
     return projected.astype(jnp.bfloat16)
 

time: 160 us -> 171 us (1.069)
  blocking collectives: 48.3 us -> 84.5 us
  waiting for transfers between devices: 42.5 us -> 11.3 us
  matrix products: 9.68 us -> 17.8 us
  starting transfers between devices: 31.5 us -> 29.4 us
  other arithmetic: 7.82 us -> 5.74 us
    all_gather x0 -> x2, blocking collectives: none -> 36.8 us  [the longest x1 20.2 us: local(): offsets_all = lax.all_gather(level_offsets, 'head', axis=1, tiled=True)]
    all_gather x1, waiting for transfers between devices: 33.2 us -> 0.14 us  [local(): lax.all_gather(early.reshape(row_count, head_count * head_width), 'head',...]
    dot_general x1 -> x4, matrix products: 4.73 us -> 11.3 us  [the longest x1 4.17 us: local(): jnp.einsum('nhd,hdc->hnc', picked_all, weight.astype(jnp.float32), precis...]
    ppermute x1, starting transfers between devices: 3.37 us -> 1.53 us  [local(): cross1 = lax.ppermute(cross_send, SEQ_AXES, down)]
  transfers between devices with their start and end apart: 8 -> 8, of which waited for: 3 -> 3; matrix products, arithmetic and copies ran while one was open for 8% -> 10% of each run, Pallas kernels for 0% -> 0%
where the time goes in v8:
time: 171 us; the launch traced here: 170 us
  blocking collectives  84.5 us (49%)
  starting transfers between devices  29.4 us (17%)
  matrix products  17.8 us (10%)
  between operations  14.1 us (8%)
  waiting for transfers between devices  11.3 us (7%)
  local copies, waits for them, and re-layouts  7.23 us (4%)
  other arithmetic  5.74 us (3%)
    all_gather x1, blocking collectives, local(): ring = lax.all_gather(jnp.concatenate([pair1, pair2], axis=0), ('zh', 'zl'))  47.7 us
    all_gather x1, blocking collectives, local(): offsets_all = lax.all_gather(level_offsets, 'head', axis=1, tiled=True)  20.2 us
    all_gather x1, blocking collectives, local(): picked_all = lax.all_gather(picked, 'head', axis=1, tiled=True)  16.6 us
    ppermute x3, starting transfers between devices, local(): arrived.append(lax.ppermute(pair0, SEQ_AXES, pairs))  12 us
    all_to_all x1, waiting for transfers between devices, local(): returned = lax.all_to_all(packed, 'sy', 0, 0, tiled=True)  9.54 us
    all_to_all x1, starting transfers between devices, local(): column_queries = lax.all_to_all(copies, 'sy', 0, 0, tiled=True)  7.72 us
    all_to_all x1, starting transfers between devices, local(): returned = lax.all_to_all(packed, 'sy', 0, 0, tiled=True)  6.83 us
    dot_general x1, matrix products, local(): jnp.einsum('nhd,hdc->hnc', picked_all, weight.astype(jnp.float32), precis...  4.17 us
  transfers between devices with their start and end apart: 8, of which 3 were waited for; matrix products, arithmetic and copies ran while one was open for 10% of the time, Pallas kernels for 0%

profile of v8, /device:TPU:1, one launch (start us, length us, event | category | flops | bytes accessed | tf_op | source)
XLA Modules:
  0.0 170.0 jit_solution(15506530098371295328)
XLA Ops:
  6.5 1.1 copy.68
  7.8 1.1 copy.67
  9.1 0.8 pad_maximum_fusion
  9.9 4.8 %collective-permute-start.2 = (bf16[256,2,3,128]{3,0,2,1:T(8,128)(2,1)}, bf16[256,2,3,128]{3,0,2,1:T(8,128)(2,1)S(1)}, u32[]{:S(2)}, u32[]{:S(2)}) collective-permute-start(bf16[256,2,3,128]{3,0,2,1:T(8,128)(2,1)} %pad_maximum_fusion), channel_id=1, source_target_pairs={{0,8},{8,16},{16,24},{32,40},{40,48},{48,56},{64,72},{72,80},{80,8... | collective-permute-start | bytes 1179656 | tf_op jit(solution)/shard_map/ppermute | solution.py:121
  14.7 5.8 %collective-permute-start.1 = (bf16[256,2,3,128]{3,0,2,1:T(8,128)(2,1)}, bf16[256,2,3,128]{3,0,2,1:T(8,128)(2,1)S(1)}, u32[]{:S(2)}, u32[]{:S(2)}) collective-permute-start(bf16[256,2,3,128]{3,0,2,1:T(8,128)(2,1)} %pad_maximum_fusion), channel_id=1, source_target_pairs={{0,16},{8,24},{32,48},{40,56},{64,80},{72,88},{96,112},{104,120},{... | collective-permute-start | bytes 1179656 | tf_op jit(solution)/shard_map/ppermute | solution.py:121
  20.5 1.3 collective-permute-start
  21.8 0.8 fusion.85
  22.7 1.1 fusion.27
  23.8 1.3 collective-permute-start.3
  25.1 1.0 reshape_reshape.26
  26.3 0.6 broadcast_in_dim.200
  27.0 7.7 %all-to-all-start = ((bf16[8,8,3,128]{3,1,2,0:T(8,128)(2,1)}), bf16[8,8,3,128]{3,1,2,0:T(8,128)(2,1)S(1)}, u32[]{:S(2)}, u32[]{:S(2)}) async-start(bf16[8,8,3,128]{3,1,2,0:T(8,128)(2,1)} %broadcast_in_dim.200), calls=%async_computation | async-start | bytes 98304 | tf_op jit(solution)/shard_map/all_to_all | solution.py:174
  34.8 0.2 fusion.33
  35.0 0.2 fusion.35
  35.6 47.7 %all-gather = bf16[640,2,3,128]{3,0,2,1:T(8,128)(2,1)S(1)} all-gather(bf16[40,2,3,128]{3,0,2,1:T(8,128)(2,1)S(1)} %maximum_maximum_fusion.1), channel_id=2, replica_groups=mesh['sy'=8,'zh'=4,'zl'=4,'head'=8] {'zh','zl'}, dimensions={0}, use_global_device_ids=true | all-gather | bytes 1044480 | tf_op jit(solution)/shard_map/all_gather | solution.py:137
  83.4 0.2 fusion.104
  83.6 0.2 fusion.60
  83.8 0.2 convolution_bitcast_fusion.3
  84.1 0.3 fusion.105
  84.4 0.2 fusion.38
  84.6 0.2 convolution_bitcast_fusion.1
  85.0 20.2 %all-gather.1 = s32[8,3,3]{2,1,0:T(4,128)S(1)} all-gather(s32[1,3,3]{2,1,0:T(4,128)S(1)} %bitcast.240), channel_id=1, replica_groups=mesh['sy'=8,'zh'=4,'zl'=4,'head'=8] {'head'}, dimensions={0}, use_global_device_ids=true | all-gather | bytes 324 | tf_op jit(solution)/shard_map/all_gather | solution.py:219
  105.4 0.2 fusion.20
  106.1 0.3 fusion.102
  106.4 0.2 fusion.37
  106.6 0.2 convolution_bitcast_fusion.2
  106.9 0.3 fusion.103
  107.2 0.2 fusion.45
  107.4 0.2 convolution_bitcast_fusion
  107.7 0.2 copy.81
  107.9 0.7 pad_maximum_fusion.1
  108.6 6.8 %all-to-all-start.1 = ((f32[8,8,3,129]{3,1,2,0:T(8,128)}), f32[8,8,3,129]{3,1,2,0:T(8,128)S(1)}, u32[]{:S(2)}, u32[]{:S(2)}) async-start(f32[8,8,3,129]{3,1,2,0:T(8,128)} %pad_maximum_fusion.1), calls=%async_computation.1 | async-start | bytes 393216 | tf_op jit(solution)/shard_map/all_to_all | solution.py:179
  115.6 9.5 %all-to-all-done.1 = f32[8,8,3,129]{3,1,2,0:T(8,128)S(1)} async-done(((f32[8,8,3,129]{3,1,2,0:T(8,128)}), f32[8,8,3,129]{3,1,2,0:T(8,128)S(1)}, u32[]{:S(2)}, u32[]{:S(2)}) %all-to-all-start.1) | async-done | bytes 99104 | tf_op jit(solution)/shard_map/all_to_all | solution.py:179
  125.2 0.2 copy.113
  126.3 0.2 copy.89
  126.6 0.7 fusion.1
  127.3 0.7 fusion
  128.0 1.9 %bitcast_convert_fusion = (bf16[256,3,128]{0,2,1:T(8,128)(2,1)}, f32[3,128,256]{2,1,0:T(8,128)S(1)}) fusion(f32[3,1024,256]{2,1,0:T(8,128)S(1)} %get-tuple-element.30, f32[3,256]{1,0:T(4,128)S(1)} %fusion, f32[3,256]{1,0:T(4,128)S(1)} %get-tuple-element.29, pred[256,1024]{0,1:T(8,128)(4,1)S(1)} %fusion.20, bf16[1024,2,3,128]{3,0,2,1:T(8,128)(2,1)S(1)} %maximum_maximum_fusion), kind=kOutput, calls=%fused_computation.37 | convolution fusion | flops 205357056 | bytes 4792320 | tf_op jit(solution)/shard_map/hqk,khd->qhd/dot_general | solution.py:35
  129.9 1.5 collective-permute-start.4
  131.5 1.6 collective-permute-done.4
  133.4 0.2 copy.84
  134.7 0.2 fusion.24
  134.9 16.6 %all_gather.19 = f32[40,24,128]{2,0,1:T(8,128)S(1)} all-gather(f32[40,3,128]{2,0,1:T(8,128)S(1)} %pad_maximum_fusion.3), channel_id=1, replica_groups=mesh['sy'=8,'zh'=4,'zl'=4,'head'=8] {'head'}, dimensions={1}, use_global_device_ids=true | all-gather | bytes 552960 | tf_op jit(solution)/shard_map/all_gather | solution.py:218
  151.5 4.2 %fusion.107 = f32[24,40,640]{2,1,0:T(8,128)S(1)} fusion(f32[40,24,128]{2,0,1:T(8,128)S(1)} %all_gather.19, bf16[24,128,640]{2,1,0:T(8,128)(2,1)} %bitcast.221), kind=kOutput, calls=%fused_computation.204 | convolution fusion | flops 943718400 | bytes 6881280 | tf_op jit(solution)/shard_map/nhd,hdc->hnc/dot_general | solution.py:223
  155.7 0.2 slice.115
  155.9 0.5 fusion.22
  156.6 4.0 %fusion.106 = f32[256,640]{1,0:T(8,128)S(1)} fusion(bf16[256,3072]{0,1:T(8,128)(2,1)} %all-gather.4.cloned.1.call-done, bf16[3072,640]{1,0:T(8,128)(2,1)} %param.9), kind=kOutput, calls=%fused_computation.203 | convolution fusion | flops 1006632960 | bytes 6160384 | tf_op jit(solution)/shard_map/dot_general | solution.py:203
  160.6 2.6 %fusion.14 = bf16[256,640]{1,0:T(8,128)(2,1)} fusion(f32[256,640]{1,0:T(8,128)S(1)} %bitcast.226, f32[256,640]{1,0:T(8,128)S(1)} %fusion.106, f32[24,32,640]{2,1,0:T(8,128)S(1)} %slice.115, s32[24]{0:T(128)S(1)} %get-tuple-element.19), kind=kOutput, calls=%fused_computation.12 | convolution fusion | flops 47677632 | bytes 3604576 | tf_op jit(solution)/shard_map/hnc,hr->nrc/dot_general | solution.py:234
  (105 shorter events, 4.7 us)
Async XLA Ops:
  6.5 28.2 %copy-start = (bf16[256,384]{1,0:T(8,128)(2,1)S(1)}, bf16[256,384]{1,0:T(8,128)(2,1)}, u32[]{:S(2)}) copy-start(bf16[256,384]{1,0:T(8,128)(2,1)} %param.7) | copy-start | bytes 589828
  6.5 28.2 %copy-start.1 = (bf16[256,384]{1,0:T(8,128)(2,1)S(1)}, bf16[256,384]{1,0:T(8,128)(2,1)}, u32[]{:S(2)}) copy-start(bf16[256,384]{1,0:T(8,128)(2,1)} %param.6) | copy-start | bytes 589828
  9.9 116.6 %collective-permute-start.2 = (bf16[256,2,3,128]{3,0,2,1:T(8,128)(2,1)}, bf16[256,2,3,128]{3,0,2,1:T(8,128)(2,1)S(1)}, u32[]{:S(2)}, u32[]{:S(2)}) collective-permute-start(bf16[256,2,3,128]{3,0,2,1:T(8,128)(2,1)} %pad_maximum_fusion), channel_id=1, source_target_pairs={{0,8},{8,16},{16,24},{32,40},{40,48},{48,56},{64,72},{72,80},{80,8... | collective-permute-start | bytes 1179656 | tf_op jit(solution)/shard_map/ppermute | solution.py:121
  14.7 111.8 %collective-permute-start.1 = (bf16[256,2,3,128]{3,0,2,1:T(8,128)(2,1)}, bf16[256,2,3,128]{3,0,2,1:T(8,128)(2,1)S(1)}, u32[]{:S(2)}, u32[]{:S(2)}) collective-permute-start(bf16[256,2,3,128]{3,0,2,1:T(8,128)(2,1)} %pad_maximum_fusion), channel_id=1, source_target_pairs={{0,16},{8,24},{32,48},{40,56},{64,80},{72,88},{96,112},{104,120},{... | collective-permute-start | bytes 1179656 | tf_op jit(solution)/shard_map/ppermute | solution.py:121
  20.5 106.0 %collective-permute-start = (bf16[256,2,3,128]{3,0,2,1:T(8,128)(2,1)}, bf16[256,2,3,128]{3,0,2,1:T(8,128)(2,1)S(1)}, u32[]{:S(2)}, u32[]{:S(2)}) collective-permute-start(bf16[256,2,3,128]{3,0,2,1:T(8,128)(2,1)} %pad_maximum_fusion), channel_id=1, source_target_pairs={{0,24},{32,56},{64,88},{96,120},{128,152},{160,184},{192,216},{224... | collective-permute-start | bytes 1179656 | tf_op jit(solution)/shard_map/ppermute | solution.py:121
  23.8 82.3 %collective-permute-start.3 = (bf16[32,3,128]{2,0,1:T(8,128)(2,1)S(1)}, bf16[32,3,128]{2,0,1:T(8,128)(2,1)S(1)}, u32[]{:S(2)}, u32[]{:S(2)}) collective-permute-start(bf16[32,3,128]{2,0,1:T(8,128)(2,1)S(1)} %convert_bitcast_fusion), channel_id=1, source_target_pairs={{128,0},{136,8},{144,16},{152,24},{160,32},{168,40},{176,48},{184,... | collective-permute-start | bytes 73736 | tf_op jit(solution)/shard_map/ppermute | solution.py:158
  27.0 79.9 %all-to-all-start = ((bf16[8,8,3,128]{3,1,2,0:T(8,128)(2,1)}), bf16[8,8,3,128]{3,1,2,0:T(8,128)(2,1)S(1)}, u32[]{:S(2)}, u32[]{:S(2)}) async-start(bf16[8,8,3,128]{3,1,2,0:T(8,128)(2,1)} %broadcast_in_dim.200), calls=%async_computation | async-start | bytes 98304 | tf_op jit(solution)/shard_map/all_to_all | solution.py:174
  35.2 49.7 %copy-start.4 = (s32[3,3]{1,0:T(4,128)S(1)}, s32[3,3]{1,0:T(4,128)}, u32[]{:S(2)}) copy-start(s32[3,3]{1,0:T(4,128)} %param.8) | copy-start | bytes 112
  35.4 70.2 %copy-start.2 = (bf16[256,384]{1,0:T(8,128)(2,1)S(1)}, bf16[256,384]{1,0:T(8,128)(2,1)}, u32[]{:S(2)}) copy-start(bf16[256,384]{1,0:T(8,128)(2,1)} %param.5) | copy-start | bytes 589828
  108.6 16.5 %all-to-all-start.1 = ((f32[8,8,3,129]{3,1,2,0:T(8,128)}), f32[8,8,3,129]{3,1,2,0:T(8,128)S(1)}, u32[]{:S(2)}, u32[]{:S(2)}) async-start(f32[8,8,3,129]{3,1,2,0:T(8,128)} %pad_maximum_fusion.1), calls=%async_computation.1 | async-start | bytes 393216 | tf_op jit(solution)/shard_map/all_to_all | solution.py:179
  115.4 41.2 %all-gather.4.cloned.1.call-start = ((), (), s32[]{:S(2)}) async-start(), calls=%async_computation.2 | async-start | bytes 1769472 | tf_op jit(solution)/shard_map/all_gather | solution.py:200
  129.9 4.2 %copy-start.3 = (bf16[256,3,128]{0,2,1:T(8,128)(2,1)S(1)}, bf16[256,3,128]{0,2,1:T(8,128)(2,1)}, u32[]{:S(2)}) copy-start(bf16[256,3,128]{0,2,1:T(8,128)(2,1)} %get-tuple-element.7) | copy-start | bytes 589828
  129.9 3.2 %collective-permute-start.4 = (f32[32,3,129]{2,0,1:T(8,128)S(1)}, f32[32,3,129]{2,0,1:T(8,128)S(1)}, u32[]{:S(2)}, u32[]{:S(2)}) collective-permute-start(f32[32,3,129]{2,0,1:T(8,128)S(1)} %pad_maximum_fusion.2), channel_id=1, source_target_pairs={{0,128},{8,136},{16,144},{24,152},{32,160},{40,168},{48,176},{56,1... | collective-permute-start | bytes 148616 | tf_op jit(solution)/shard_map/ppermute | solution.py:164
Sparse Core Ops, SparseCore 0:
  131.6 24.9 all-gather.3

commit v9 on v3

--- a/solution.py
+++ b/solution.py
@@ -195,10 +195,12 @@
         / jnp.sum(level_weights, axis=0)[..., None]
     )
     heads_out = mixed_heads.astype(jnp.bfloat16).reshape(row_count, head_count * head_width)
-    projected = jnp.dot(
-        lax.all_gather(heads_out, "head", axis=1, tiled=True),
-        out_weight,
-        preferred_element_type=jnp.float32,
+    head_devices = lax.axis_size("head")
+    copies = jnp.broadcast_to(heads_out[None], (head_devices,) + heads_out.shape)
+    gathered = lax.all_to_all(copies, "head", 0, 0, tiled=True)
+    weight = out_weight.reshape(head_devices, head_count * head_width, out_weight.shape[1])
+    projected = jnp.einsum(
+        "str,sro->to", gathered, weight, preferred_element_type=jnp.float32
     )
     return projected.astype(jnp.bfloat16)
 

time: 156 us -> 138 us (0.88)
  waiting for transfers between devices: 46.2 us -> 10.3 us
  blocking collectives: 42.3 us -> 76.8 us
  between operations: 14.1 us -> 0.69 us
  matrix products: 11.6 us -> 8.96 us
    all_gather x1 -> x0, waiting for transfers between devices: 36 us -> none  [local(): lax.all_gather(heads_out, 'head', axis=1, tiled=True)]
    all_to_all x0 -> x1, blocking collectives: none -> 34.6 us  [local(): gathered = lax.all_to_all(copies, 'head', 0, 0, tiled=True)]
    dot_general x1, matrix products: 4.73 us -> 2.11 us  [local(): jnp.einsum('str,sro->to', gathered, weight, preferred_element_type=jnp.fl...]
  transfers between devices with their start and end apart: 14 -> 13, of which waited for: 3 -> 2; matrix products, arithmetic and copies ran while one was open for 8% -> 9% of each run, Pallas kernels for 0% -> 0%
where the time goes in v9:
time: 138 us
  blocking collectives  76.8 us (56%)
  starting transfers between devices  28.5 us (21%)
  waiting for transfers between devices  10.3 us (7%)
  matrix products  8.96 us (6%)
  other arithmetic  6.5 us (5%)
  local copies, waits for them, and re-layouts  6.04 us (4%)
    all_gather x1, blocking collectives, local(): ring = lax.all_gather(jnp.concatenate([pair1, pair2], axis=0), ROW_AXES)  42.3 us
    all_to_all x1, blocking collectives, local(): gathered = lax.all_to_all(copies, 'head', 0, 0, tiled=True)  34.6 us
    ppermute x7, starting transfers between devices, local(): visiting.append(lax.ppermute(query2, SEQ_AXES, pairs))  9.04 us
    all_to_all x1, waiting for transfers between devices, local(): returned = lax.all_to_all(packed, 'sy', 0, 0, tiled=True)  8.51 us
    all_to_all x1, starting transfers between devices, local(): returned = lax.all_to_all(packed, 'sy', 0, 0, tiled=True)  7.54 us
    ppermute x3, starting transfers between devices, local(): arrived.append(lax.ppermute(pair0, SEQ_AXES, pairs))  6.88 us
    ppermute x1, starting transfers between devices, local(): lax.ppermute(pack(*whole_row(visiting1, row1, count1)), SEQ_AXES, down)  3.72 us
    another operation x3, local copies, waits for them, and re-layouts, pick_rows(): states.reshape(row_count // spacing, spacing, head_count, head_width)  3.03 us
  transfers between devices with their start and end apart: 13, of which 2 were waited for; matrix products, arithmetic and copies ran while one was open for 9% of the time, Pallas kernels for 0%

profile of v9, /device:TPU:1, one launch (start us, length us, event | category | flops | bytes accessed | tf_op | source)
XLA Modules:
  0.0 137.8 jit_solution(5458057774326423680)
XLA Ops:
  0.0 1.1 reshape_reshape.26
  1.1 0.8 fusion.65
  2.1 1.3 collective-permute-start.5
  3.4 1.3 collective-permute-start.6
  4.7 1.3 collective-permute-start.7
  6.0 1.3 collective-permute-start.8
  7.3 1.3 collective-permute-start.9
  8.6 1.0 reshape_reshape.25
  9.5 1.0 reshape_reshape.24
  10.6 1.1 fusion.19
  11.7 1.1 fusion.21
  13.2 42.3 %all-gather = bf16[640,2,3,128]{3,0,2,1:T(8,128)(2,1)S(1)} all-gather(bf16[40,2,3,128]{3,0,2,1:T(8,128)(2,1)S(1)} %maximum_maximum_fusion.1), channel_id=2, replica_groups=mesh['sy'=8,'sz'=16,'head'=8] {'sz'}, dimensions={0}, use_global_device_ids=true | all-gather | bytes 1044480 | tf_op jit(solution)/shard_map/all_gather | solution.py:137
  55.5 0.2 fusion.81
  55.9 0.2 convolution_bitcast_fusion.4
  56.2 0.2 fusion.23
  56.5 0.3 fusion.83
  56.9 0.2 fusion.25
  57.1 0.2 convolution_bitcast_fusion.2
  57.9 0.2 copy.54
  58.0 0.2 fusion.8
  58.3 0.8 pad_maximum_fusion
  59.4 1.3 collective-permute-start.10
  60.7 1.3 collective-permute-start.11
  62.0 1.3 collective-permute-start.3
  63.4 1.3 collective-permute-start.2
  64.7 3.5 %collective-permute-start.1 = (bf16[256,2,3,128]{3,0,2,1:T(8,128)(2,1)}, bf16[256,2,3,128]{3,0,2,1:T(8,128)(2,1)}, u32[]{:S(2)}, u32[]{:S(2)}) collective-permute-start(bf16[256,2,3,128]{3,0,2,1:T(8,128)(2,1)} %pad_maximum_fusion), channel_id=1, source_target_pairs={{0,16},{8,24},{32,48},{40,56},{64,80},{72,88},{96,112},{104,120},{... | collective-permute-start | bytes 1179656 | tf_op jit(solution)/shard_map/ppermute | solution.py:121
  68.3 1.7 %collective-permute-done.10 = bf16[8,3,128]{2,0,1:T(8,128)(2,1)S(1)} collective-permute-done((bf16[8,3,128]{2,0,1:T(8,128)(2,1)S(1)}, bf16[8,3,128]{2,0,1:T(8,128)(2,1)S(1)}, u32[]{:S(2)}, u32[]{:S(2)}) %collective-permute-start.10) | collective-permute-done | bytes 6176 | tf_op jit(solution)/shard_map/ppermute | solution.py:172
  70.0 2.0 %collective-permute-start = (bf16[256,2,3,128]{3,0,2,1:T(8,128)(2,1)}, bf16[256,2,3,128]{3,0,2,1:T(8,128)(2,1)}, u32[]{:S(2)}, u32[]{:S(2)}) collective-permute-start(bf16[256,2,3,128]{3,0,2,1:T(8,128)(2,1)} %pad_maximum_fusion), channel_id=1, source_target_pairs={{0,24},{32,56},{64,88},{96,120},{128,152},{160,184},{192,216},{224... | collective-permute-start | bytes 1179656 | tf_op jit(solution)/shard_map/ppermute | solution.py:121
  72.0 0.3 fusion.80
  72.3 0.2 fusion.33
  72.5 0.2 convolution_bitcast_fusion.1
  72.8 0.2 copy.61
  73.1 0.3 fusion.82
  73.4 0.2 fusion.26
  73.6 0.2 convolution_bitcast_fusion.3
  74.0 3.7 %collective-permute-start.4 = (f32[32,3,129]{2,0,1:T(8,128)S(1)}, f32[32,3,129]{2,0,1:T(8,128)S(1)}, u32[]{:S(2)}, u32[]{:S(2)}) collective-permute-start(f32[32,3,129]{2,0,1:T(8,128)S(1)} %pad_maximum_fusion.1), channel_id=1, source_target_pairs={{0,128},{8,136},{16,144},{24,152},{32,160},{40,168},{48,176},{56,1... | collective-permute-start | bytes 148616 | tf_op jit(solution)/shard_map/ppermute | solution.py:160
  77.7 0.7 fusion.11
  78.4 7.5 %all-to-all-start = ((f32[8,8,3,129]{3,1,2,0:T(8,128)}), f32[8,8,3,129]{3,1,2,0:T(8,128)S(1)}, u32[]{:S(2)}, u32[]{:S(2)}) async-start(f32[8,8,3,129]{3,1,2,0:T(8,128)} %fusion.11), calls=%async_computation | async-start | bytes 393216 | tf_op jit(solution)/shard_map/all_to_all | solution.py:178
  86.6 0.2 copy.66
  86.8 8.5 %all-to-all-done = f32[8,8,3,129]{3,1,2,0:T(8,128)S(1)} async-done(((f32[8,8,3,129]{3,1,2,0:T(8,128)}), f32[8,8,3,129]{3,1,2,0:T(8,128)S(1)}, u32[]{:S(2)}, u32[]{:S(2)}) %all-to-all-start) | async-done | bytes 99104 | tf_op jit(solution)/shard_map/all_to_all | solution.py:178
  95.4 0.2 copy.91
  96.5 0.2 copy.71
  96.7 1.2 maximum_maximum_fusion
  97.9 0.7 fusion.1
  98.6 0.7 fusion
  99.4 1.2 fusion.4
  101.1 34.6 %all_to_all.10 = bf16[8,256,384]{2,1,0:T(8,128)(2,1)S(1)} all-to-all(bf16[8,256,384]{2,1,0:T(8,128)(2,1)S(1)} %broadcast_in_dim.156), channel_id=1, replica_groups=mesh['sy'=8,'sz'=16,'head'=8] {'head'}, dimensions={0} | all-to-all | bytes 3145728 | tf_op jit(solution)/shard_map/all_to_all | solution.py:200
  135.6 2.1 %fusion.3 = bf16[256,640]{1,0:T(8,128)(2,1)} fusion(bf16[8,256,384]{2,1,0:T(8,128)(2,1)S(1)} %all_to_all.10, bf16[8,384,640]{2,1,0:T(8,128)(2,1)S(1)} %bitcast.200), kind=kOutput, calls=%fused_computation.8 | convolution fusion | flops 1006796800 | bytes 5832704 | tf_op jit(solution)/shard_map/str,sro->to/dot_general | solution.py:202
  (102 shorter events, 4.0 us)
Async XLA Ops:
  0.0 56.2 %copy-start.2 = (bf16[256,384]{1,0:T(8,128)(2,1)S(1)}, bf16[256,384]{1,0:T(8,128)(2,1)}, u32[]{:S(2)}) copy-start(bf16[256,384]{1,0:T(8,128)(2,1)} %param.5) | copy-start | bytes 589828
  2.1 57.3 %collective-permute-start.5 = (bf16[8,3,128]{2,0,1:T(8,128)(2,1)S(1)}, bf16[8,3,128]{2,0,1:T(8,128)(2,1)S(1)}, u32[]{:S(2)}, u32[]{:S(2)}) collective-permute-start(bf16[8,3,128]{2,0,1:T(8,128)(2,1)S(1)} %get-tuple-element.12), channel_id=1, source_target_pairs={{128,0},{136,8},{144,16},{152,24},{160,32},{168,40},{176,48},{184,... | collective-permute-start | bytes 18440 | tf_op jit(solution)/shard_map/ppermute | solution.py:172
  3.4 57.4 %collective-permute-start.6 = (bf16[8,3,128]{2,0,1:T(8,128)(2,1)S(1)}, bf16[8,3,128]{2,0,1:T(8,128)(2,1)S(1)}, u32[]{:S(2)}, u32[]{:S(2)}) collective-permute-start(bf16[8,3,128]{2,0,1:T(8,128)(2,1)S(1)} %get-tuple-element.12), channel_id=1, source_target_pairs={{256,0},{264,8},{272,16},{280,24},{288,32},{296,40},{304,48},{312,... | collective-permute-start | bytes 18440 | tf_op jit(solution)/shard_map/ppermute | solution.py:172
  4.7 57.4 %collective-permute-start.7 = (bf16[8,3,128]{2,0,1:T(8,128)(2,1)S(1)}, bf16[8,3,128]{2,0,1:T(8,128)(2,1)S(1)}, u32[]{:S(2)}, u32[]{:S(2)}) collective-permute-start(bf16[8,3,128]{2,0,1:T(8,128)(2,1)S(1)} %get-tuple-element.12), channel_id=1, source_target_pairs={{384,0},{392,8},{400,16},{408,24},{416,32},{424,40},{432,48},{440,... | collective-permute-start | bytes 18440 | tf_op jit(solution)/shard_map/ppermute | solution.py:172
  6.0 57.4 %collective-permute-start.8 = (bf16[8,3,128]{2,0,1:T(8,128)(2,1)S(1)}, bf16[8,3,128]{2,0,1:T(8,128)(2,1)S(1)}, u32[]{:S(2)}, u32[]{:S(2)}) collective-permute-start(bf16[8,3,128]{2,0,1:T(8,128)(2,1)S(1)} %get-tuple-element.12), channel_id=1, source_target_pairs={{512,0},{520,8},{528,16},{536,24},{544,32},{552,40},{560,48},{568,... | collective-permute-start | bytes 18440 | tf_op jit(solution)/shard_map/ppermute | solution.py:172
  7.3 57.5 %collective-permute-start.9 = (bf16[8,3,128]{2,0,1:T(8,128)(2,1)S(1)}, bf16[8,3,128]{2,0,1:T(8,128)(2,1)S(1)}, u32[]{:S(2)}, u32[]{:S(2)}) collective-permute-start(bf16[8,3,128]{2,0,1:T(8,128)(2,1)S(1)} %get-tuple-element.12), channel_id=1, source_target_pairs={{640,0},{648,8},{656,16},{664,24},{672,32},{680,40},{688,48},{696,... | collective-permute-start | bytes 18440 | tf_op jit(solution)/shard_map/ppermute | solution.py:172
  13.2 44.2 %copy-start = (bf16[256,384]{1,0:T(8,128)(2,1)S(1)}, bf16[256,384]{1,0:T(8,128)(2,1)}, u32[]{:S(2)}) copy-start(bf16[256,384]{1,0:T(8,128)(2,1)} %param.7) | copy-start | bytes 589828
  13.2 44.3 %copy-start.1 = (bf16[256,384]{1,0:T(8,128)(2,1)S(1)}, bf16[256,384]{1,0:T(8,128)(2,1)}, u32[]{:S(2)}) copy-start(bf16[256,384]{1,0:T(8,128)(2,1)} %param.6) | copy-start | bytes 589828
  59.4 10.6 %collective-permute-start.10 = (bf16[8,3,128]{2,0,1:T(8,128)(2,1)S(1)}, bf16[8,3,128]{2,0,1:T(8,128)(2,1)S(1)}, u32[]{:S(2)}, u32[]{:S(2)}) collective-permute-start(bf16[8,3,128]{2,0,1:T(8,128)(2,1)S(1)} %get-tuple-element.12), channel_id=1, source_target_pairs={{768,0},{776,8},{784,16},{792,24},{800,32},{808,40},{816,48},{824,... | collective-permute-start | bytes 18440 | tf_op jit(solution)/shard_map/ppermute | solution.py:172
  60.7 11.3 %collective-permute-start.11 = (bf16[8,3,128]{2,0,1:T(8,128)(2,1)S(1)}, bf16[8,3,128]{2,0,1:T(8,128)(2,1)S(1)}, u32[]{:S(2)}, u32[]{:S(2)}) collective-permute-start(bf16[8,3,128]{2,0,1:T(8,128)(2,1)S(1)} %get-tuple-element.12), channel_id=1, source_target_pairs={{896,0},{904,8},{912,16},{920,24},{928,32},{936,40},{944,48},{952,... | collective-permute-start | bytes 18440 | tf_op jit(solution)/shard_map/ppermute | solution.py:172
  62.0 11.0 %collective-permute-start.3 = (bf16[32,3,128]{2,0,1:T(8,128)(2,1)S(1)}, bf16[32,3,128]{2,0,1:T(8,128)(2,1)S(1)}, u32[]{:S(2)}, u32[]{:S(2)}) collective-permute-start(bf16[32,3,128]{2,0,1:T(8,128)(2,1)S(1)} %convert_bitcast_fusion.2), channel_id=1, source_target_pairs={{128,0},{136,8},{144,16},{152,24},{160,32},{168,40},{176,48},{184,... | collective-permute-start | bytes 73736 | tf_op jit(solution)/shard_map/ppermute | solution.py:158
  63.4 33.3 %collective-permute-start.2 = (bf16[256,2,3,128]{3,0,2,1:T(8,128)(2,1)}, bf16[256,2,3,128]{3,0,2,1:T(8,128)(2,1)S(1)}, u32[]{:S(2)}, u32[]{:S(2)}) collective-permute-start(bf16[256,2,3,128]{3,0,2,1:T(8,128)(2,1)} %pad_maximum_fusion), channel_id=1, source_target_pairs={{0,8},{8,16},{16,24},{32,40},{40,48},{48,56},{64,72},{72,80},{80,8... | collective-permute-start | bytes 1179656 | tf_op jit(solution)/shard_map/ppermute | solution.py:121
  64.7 32.0 %collective-permute-start.1 = (bf16[256,2,3,128]{3,0,2,1:T(8,128)(2,1)}, bf16[256,2,3,128]{3,0,2,1:T(8,128)(2,1)}, u32[]{:S(2)}, u32[]{:S(2)}) collective-permute-start(bf16[256,2,3,128]{3,0,2,1:T(8,128)(2,1)} %pad_maximum_fusion), channel_id=1, source_target_pairs={{0,16},{8,24},{32,48},{40,56},{64,80},{72,88},{96,112},{104,120},{... | collective-permute-start | bytes 1179656 | tf_op jit(solution)/shard_map/ppermute | solution.py:121
  70.0 26.7 %collective-permute-start = (bf16[256,2,3,128]{3,0,2,1:T(8,128)(2,1)}, bf16[256,2,3,128]{3,0,2,1:T(8,128)(2,1)}, u32[]{:S(2)}, u32[]{:S(2)}) collective-permute-start(bf16[256,2,3,128]{3,0,2,1:T(8,128)(2,1)} %pad_maximum_fusion), channel_id=1, source_target_pairs={{0,24},{32,56},{64,88},{96,120},{128,152},{160,184},{192,216},{224... | collective-permute-start | bytes 1179656 | tf_op jit(solution)/shard_map/ppermute | solution.py:121
  74.0 12.0 %collective-permute-start.4 = (f32[32,3,129]{2,0,1:T(8,128)S(1)}, f32[32,3,129]{2,0,1:T(8,128)S(1)}, u32[]{:S(2)}, u32[]{:S(2)}) collective-permute-start(f32[32,3,129]{2,0,1:T(8,128)S(1)} %pad_maximum_fusion.1), channel_id=1, source_target_pairs={{0,128},{8,136},{16,144},{24,152},{32,160},{40,168},{48,176},{56,1... | collective-permute-start | bytes 148616 | tf_op jit(solution)/shard_map/ppermute | solution.py:160
  78.4 16.9 %all-to-all-start = ((f32[8,8,3,129]{3,1,2,0:T(8,128)}), f32[8,8,3,129]{3,1,2,0:T(8,128)S(1)}, u32[]{:S(2)}, u32[]{:S(2)}) async-start(f32[8,8,3,129]{3,1,2,0:T(8,128)} %fusion.11), calls=%async_computation | async-start | bytes 393216 | tf_op jit(solution)/shard_map/all_to_all | solution.py:178
  100.9 34.7 %copy-start.3 = (bf16[3072,640]{1,0:T(8,128)(2,1)S(1)}, bf16[3072,640]{1,0:T(8,128)(2,1)}, u32[]{:S(2)}) copy-start(bf16[3072,640]{1,0:T(8,128)(2,1)} %param.9) | copy-start | bytes 11796484

commit v10 on v9

--- a/solution.py
+++ b/solution.py
@@ -113,8 +113,16 @@
     full_outs = []
     full_lses = []
 
+    chooser1, query1, pair1 = level_setup(query_all, key_all, value_all, level_offsets[1], RATE_MID)
+    chooser2, query2, pair2 = level_setup(query_all, key_all, value_all, level_offsets[2], RATE_TOP)
+    count1 = pair1.shape[0]
+    count2 = pair2.shape[0]
+    ring = lax.all_gather(jnp.concatenate([pair1, pair2], axis=0), ROW_AXES)
+    row1 = ring[:, :count1]
+
     span0 = SEG_ROWS // row_count
     chooser0, query0, pair0 = level_setup(query_all, key_all, value_all, level_offsets[0], 1)
+    pair0, ring = lax.optimization_barrier((pair0, ring))
     arrived = []
     for shift in range(span0 - 1, 0, -1):
         pairs = [(s, s + shift) for s in range(seq_count) if s % span0 + shift < span0]
@@ -130,12 +138,6 @@
     full_outs.append(full_out)
     full_lses.append(full_lse)
 
-    chooser1, query1, pair1 = level_setup(query_all, key_all, value_all, level_offsets[1], RATE_MID)
-    chooser2, query2, pair2 = level_setup(query_all, key_all, value_all, level_offsets[2], RATE_TOP)
-    count1 = pair1.shape[0]
-    count2 = pair2.shape[0]
-    ring = lax.all_gather(jnp.concatenate([pair1, pair2], axis=0), ROW_AXES)
-    row1 = ring[:, :count1]
     row2 = ring[:, count1:]
 
     def own_row(query_rows, row_blocks, count):
@@ -166,15 +168,12 @@
     full_lses.append(full_lse)
 
     own_out2, own_lse2 = own_row(query2, row2, count2)
-    visiting = [query2]
-    for gap in range(1, rows_total):
-        pairs = [(s, s - gap * row_len) for s in range(seq_count) if s // row_len >= gap]
-        visiting.append(lax.ppermute(query2, SEQ_AXES, pairs))
-    cross_out, cross_lse = whole_row(jnp.concatenate(visiting, axis=0), row2, count2)
+    copies = jnp.broadcast_to(query2[None], (rows_total,) + query2.shape)
+    column_queries = lax.all_to_all(copies, "sy", 0, 0, tiled=True)
+    cross_out, cross_lse = whole_row(
+        column_queries.reshape(rows_total * count2, head_count, head_width), row2, count2
+    )
     packed = pack(cross_out, cross_lse).reshape(rows_total, count2, head_count, head_width + 1)
-    doubled = jnp.concatenate([packed, packed], axis=0)
-    start = (rows_total - row_y) % rows_total
-    packed = lax.dynamic_slice_in_dim(doubled, start, rows_total, axis=0)
     returned = lax.all_to_all(packed, "sy", 0, 0, tiled=True)
     back_out, back_lse = unpack(returned)
     source_row = lax.broadcasted_iota(jnp.int32, back_lse.shape, 0)

time: 138 us -> 142 us (1.029)
  blocking collectives: 76.8 us -> 85.6 us
  starting transfers between devices: 28.5 us -> 23.7 us
  local copies, waits for them, and re-layouts: 6.04 us -> 9.69 us
  other arithmetic: 6.5 us -> 3.78 us
  matrix products: 8.96 us -> 7.05 us
    all_to_all x1, blocking collectives: 34.6 us -> 43.7 us  [local(): gathered = lax.all_to_all(copies, 'head', 0, 0, tiled=True)]
    ppermute x7 -> x0, starting transfers between devices: 9.04 us -> none  [local(): visiting.append(lax.ppermute(query2, SEQ_AXES, pairs))]
    all_to_all x0 -> x1, starting transfers between devices: none -> 6.83 us  [local(): column_queries = lax.all_to_all(copies, 'sy', 0, 0, tiled=True)]
    unnamed x19 -> x18, local copies, waits for them, and re-layouts: 0.84 us -> 4.81 us
    concatenate x2 -> x0, other arithmetic: 1.95 us -> none  [the longest x1 1.22 us: local(): buffer0 = jnp.concatenate(arrived + [pair0], axis=0)]
    dot_general x6, matrix products: 2.85 us -> 0.98 us  [pick_rows(): jnp.einsum('nrhd,rh->nhd', grouped, chooser, preferred_element_type=jnp.f...]
    ppermute x7 -> x0, waiting for transfers between devices: 1.74 us -> none  [local(): visiting.append(lax.ppermute(query2, SEQ_AXES, pairs))]
    ppermute x1, waiting for transfers between devices: 0.01 us -> 1.47 us  [local(): visiting1 = lax.ppermute(query1, SEQ_AXES, up)]
  transfers between devices with their start and end apart: 13 -> 7, of which waited for: 2 -> 3; matrix products, arithmetic and copies ran while one was open for 9% -> 7% of each run, Pallas kernels for 0% -> 0%
where the time goes in v10:
time: 142 us
  blocking collectives  85.6 us (60%)
  starting transfers between devices  23.7 us (17%)
  waiting for transfers between devices  11.3 us (8%)
  local copies, waits for them, and re-layouts  9.69 us (7%)
  matrix products  7.05 us (5%)
  other arithmetic  3.78 us (3%)
    all_to_all x1, blocking collectives, local(): gathered = lax.all_to_all(copies, 'head', 0, 0, tiled=True)  43.7 us
    all_gather x1, blocking collectives, local(): ring = lax.all_gather(jnp.concatenate([pair1, pair2], axis=0), ROW_AXES)  41.9 us
    all_to_all x1, waiting for transfers between devices, local(): returned = lax.all_to_all(packed, 'sy', 0, 0, tiled=True)  8.6 us
    all_to_all x1, starting transfers between devices, local(): returned = lax.all_to_all(packed, 'sy', 0, 0, tiled=True)  7.29 us
    all_to_all x1, starting transfers between devices, local(): column_queries = lax.all_to_all(copies, 'sy', 0, 0, tiled=True)  6.83 us
    ppermute x3, starting transfers between devices, local(): arrived.append(lax.ppermute(pair0, SEQ_AXES, pairs))  5.8 us
    unnamed x18, local copies, waits for them, and re-layouts  4.81 us
  transfers between devices with their start and end apart: 7, of which 3 were waited for; matrix products, arithmetic and copies ran while one was open for 7% of the time, Pallas kernels for 0%

profile of v10, /device:TPU:1, one launch (start us, length us, event | category | flops | bytes accessed | tf_op | source)
XLA Modules:
  0.0 141.8 jit_solution(15772887442885250475)
XLA Ops:
  0.0 1.1 copy.54
  1.1 1.0 reshape_reshape.24
  2.1 1.1 copy.53
  3.2 1.0 reshape_reshape.23
  4.3 0.2 fusion.18
  4.5 0.2 fusion.20
  4.7 0.2 copy.56
  4.9 0.2 copy.55
  5.2 0.1 fusion.16
  5.4 41.9 %all-gather = bf16[640,2,3,128]{3,0,2,1:T(8,128)(2,1)S(1)} all-gather(bf16[40,2,3,128]{3,0,2,1:T(8,128)(2,1)S(1)} %maximum_maximum_fusion), channel_id=2, replica_groups=mesh['sy'=8,'sz'=16,'head'=8] {'sz'}, dimensions={0}, use_global_device_ids=true | all-gather | bytes 1044480 | tf_op jit(solution)/shard_map/all_gather | solution.py:120
  47.4 2.0 %collective-permute-start = (bf16[256,2,3,128]{3,0,2,1:T(8,128)(2,1)S(1)}, bf16[256,2,3,128]{3,0,2,1:T(8,128)(2,1)}, u32[]{:S(2)}, u32[]{:S(2)}) collective-permute-start(bf16[256,2,3,128]{3,0,2,1:T(8,128)(2,1)S(1)} %pad_maximum_fusion), channel_id=1, source_target_pairs={{0,24},{32,56},{64,88},{96,120},{128,152},{160,184},{192,216},{224... | collective-permute-start | bytes 1179656 | tf_op jit(solution)/shard_map/ppermute | solution.py:129
  49.4 2.5 %collective-permute-start.1 = (bf16[256,2,3,128]{3,0,2,1:T(8,128)(2,1)S(1)}, bf16[256,2,3,128]{3,0,2,1:T(8,128)(2,1)}, u32[]{:S(2)}, u32[]{:S(2)}) collective-permute-start(bf16[256,2,3,128]{3,0,2,1:T(8,128)(2,1)S(1)} %pad_maximum_fusion), channel_id=1, source_target_pairs={{0,16},{8,24},{32,48},{40,56},{64,80},{72,88},{96,112},{104,120},{... | collective-permute-start | bytes 1179656 | tf_op jit(solution)/shard_map/ppermute | solution.py:129
  51.9 1.3 collective-permute-start.2
  53.4 0.6 broadcast_in_dim.158
  54.1 6.8 %all-to-all-start = ((bf16[8,8,3,128]{3,1,2,0:T(8,128)(2,1)}), bf16[8,8,3,128]{3,1,2,0:T(8,128)(2,1)S(1)}, u32[]{:S(2)}, u32[]{:S(2)}) async-start(bf16[8,8,3,128]{3,1,2,0:T(8,128)(2,1)} %broadcast_in_dim.158), calls=%async_computation | async-start | bytes 98304 | tf_op jit(solution)/shard_map/all_to_all | solution.py:172
  60.9 0.2 fusion.12
  61.1 1.3 collective-permute-start.3
  62.6 0.3 fusion.82
  62.9 0.2 fusion.22
  63.1 0.2 convolution_bitcast_fusion.2
  63.4 0.2 fusion.80
  63.7 0.2 fusion.43
  63.9 0.2 fusion.8
  64.1 0.2 convolution_bitcast_fusion.4
  64.3 1.5 %collective-permute-done.3 = bf16[32,3,128]{2,0,1:T(8,128)(2,1)S(1)} collective-permute-done((bf16[32,3,128]{2,0,1:T(8,128)(2,1)S(1)}, bf16[32,3,128]{2,0,1:T(8,128)(2,1)S(1)}, u32[]{:S(2)}, u32[]{:S(2)}) %collective-permute-start.3) | collective-permute-done | bytes 24608 | tf_op jit(solution)/shard_map/ppermute | solution.py:160
  65.8 0.3 fusion.81
  66.1 0.2 fusion.23
  66.3 0.2 convolution_bitcast_fusion.3
  66.7 2.5 %collective-permute-start.4 = (f32[32,3,129]{2,0,1:T(8,128)S(1)}, f32[32,3,129]{2,0,1:T(8,128)S(1)}, u32[]{:S(2)}, u32[]{:S(2)}) collective-permute-start(f32[32,3,129]{2,0,1:T(8,128)S(1)} %pad_maximum_fusion.2), channel_id=1, source_target_pairs={{0,128},{8,136},{16,144},{24,152},{32,160},{40,168},{48,176},{56,1... | collective-permute-start | bytes 148616 | tf_op jit(solution)/shard_map/ppermute | solution.py:162
  69.6 1.2 collective-permute-done.4
  71.5 0.2 copy.68
  71.7 0.3 fusion.79
  72.0 0.2 fusion.30
  72.2 0.2 convolution_bitcast_fusion.1
  72.5 0.2 copy.63
  72.7 0.7 pad_maximum_fusion.1
  73.4 7.3 %all-to-all-start.1 = ((f32[8,8,3,129]{3,1,2,0:T(8,128)}), f32[8,8,3,129]{3,1,2,0:T(8,128)S(1)}, u32[]{:S(2)}, u32[]{:S(2)}) async-start(f32[8,8,3,129]{3,1,2,0:T(8,128)} %pad_maximum_fusion.1), calls=%async_computation.1 | async-start | bytes 393216 | tf_op jit(solution)/shard_map/all_to_all | solution.py:177
  80.7 8.6 %all-to-all-done.1 = f32[8,8,3,129]{3,1,2,0:T(8,128)S(1)} async-done(((f32[8,8,3,129]{3,1,2,0:T(8,128)}), f32[8,8,3,129]{3,1,2,0:T(8,128)S(1)}, u32[]{:S(2)}, u32[]{:S(2)}) %all-to-all-start.1) | async-done | bytes 99104 | tf_op jit(solution)/shard_map/all_to_all | solution.py:177
  89.3 0.2 copy.93
  90.4 0.2 copy.73
  90.7 1.0 constant_dynamic-update-slice_fusion.3
  91.7 1.0 constant_dynamic-update-slice_fusion.2
  92.9 0.7 fusion.1
  93.6 0.7 fusion
  94.3 1.2 fusion.4
  95.7 0.2 copy.74
  96.0 43.7 %all_to_all.15 = bf16[8,256,384]{2,1,0:T(8,128)(2,1)S(1)} all-to-all(bf16[8,256,384]{2,1,0:T(8,128)(2,1)S(1)} %broadcast_in_dim.163), channel_id=1, replica_groups=mesh['sy'=8,'sz'=16,'head'=8] {'head'}, dimensions={0} | all-to-all | bytes 3145728 | tf_op jit(solution)/shard_map/all_to_all | solution.py:199
  139.7 2.1 %fusion.3 = bf16[256,640]{1,0:T(8,128)(2,1)} fusion(bf16[8,256,384]{2,1,0:T(8,128)(2,1)S(1)} %all_to_all.15, bf16[8,384,640]{2,1,0:T(8,128)(2,1)S(1)} %bitcast.203), kind=kOutput, calls=%fused_computation.7 | convolution fusion | flops 1006796800 | bytes 5832704 | tf_op jit(solution)/shard_map/str,sro->to/dot_general | solution.py:201
  (89 shorter events, 3.3 us)
Async XLA Ops:
  0.0 4.3 %copy-start = (bf16[256,384]{1,0:T(8,128)(2,1)S(1)}, bf16[256,384]{1,0:T(8,128)(2,1)}, u32[]{:S(2)}) copy-start(bf16[256,384]{1,0:T(8,128)(2,1)} %param.7) | copy-start | bytes 589828
  0.0 4.5 %copy-start.1 = (bf16[256,384]{1,0:T(8,128)(2,1)S(1)}, bf16[256,384]{1,0:T(8,128)(2,1)}, u32[]{:S(2)}) copy-start(bf16[256,384]{1,0:T(8,128)(2,1)} %param.6) | copy-start | bytes 589828
  0.0 4.2 %copy-start.3 = (s32[3,3]{1,0:T(4,128)S(1)}, s32[3,3]{1,0:T(4,128)}, u32[]{:S(2)}) copy-start(s32[3,3]{1,0:T(4,128)} %param.8) | copy-start | bytes 112
  4.8 48.4 %copy-start.2 = (bf16[256,384]{1,0:T(8,128)(2,1)S(1)}, bf16[256,384]{1,0:T(8,128)(2,1)}, u32[]{:S(2)}) copy-start(bf16[256,384]{1,0:T(8,128)(2,1)} %param.5) | copy-start | bytes 589828
  47.4 43.3 %collective-permute-start = (bf16[256,2,3,128]{3,0,2,1:T(8,128)(2,1)S(1)}, bf16[256,2,3,128]{3,0,2,1:T(8,128)(2,1)}, u32[]{:S(2)}, u32[]{:S(2)}) collective-permute-start(bf16[256,2,3,128]{3,0,2,1:T(8,128)(2,1)S(1)} %pad_maximum_fusion), channel_id=1, source_target_pairs={{0,24},{32,56},{64,88},{96,120},{128,152},{160,184},{192,216},{224... | collective-permute-start | bytes 1179656 | tf_op jit(solution)/shard_map/ppermute | solution.py:129
  49.4 42.3 %collective-permute-start.1 = (bf16[256,2,3,128]{3,0,2,1:T(8,128)(2,1)S(1)}, bf16[256,2,3,128]{3,0,2,1:T(8,128)(2,1)}, u32[]{:S(2)}, u32[]{:S(2)}) collective-permute-start(bf16[256,2,3,128]{3,0,2,1:T(8,128)(2,1)S(1)} %pad_maximum_fusion), channel_id=1, source_target_pairs={{0,16},{8,24},{32,48},{40,56},{64,80},{72,88},{96,112},{104,120},{... | collective-permute-start | bytes 1179656 | tf_op jit(solution)/shard_map/ppermute | solution.py:129
  51.9 40.9 %collective-permute-start.2 = (bf16[256,2,3,128]{3,0,2,1:T(8,128)(2,1)S(1)}, bf16[256,2,3,128]{3,0,2,1:T(8,128)(2,1)S(1)}, u32[]{:S(2)}, u32[]{:S(2)}) collective-permute-start(bf16[256,2,3,128]{3,0,2,1:T(8,128)(2,1)S(1)} %pad_maximum_fusion), channel_id=1, source_target_pairs={{0,8},{8,16},{16,24},{32,40},{40,48},{48,56},{64,72},{72,80},{80,8... | collective-permute-start | bytes 1179656 | tf_op jit(solution)/shard_map/ppermute | solution.py:129
  54.1 17.6 %all-to-all-start = ((bf16[8,8,3,128]{3,1,2,0:T(8,128)(2,1)}), bf16[8,8,3,128]{3,1,2,0:T(8,128)(2,1)S(1)}, u32[]{:S(2)}, u32[]{:S(2)}) async-start(bf16[8,8,3,128]{3,1,2,0:T(8,128)(2,1)} %broadcast_in_dim.158), calls=%async_computation | async-start | bytes 98304 | tf_op jit(solution)/shard_map/all_to_all | solution.py:172
  61.1 4.7 %collective-permute-start.3 = (bf16[32,3,128]{2,0,1:T(8,128)(2,1)S(1)}, bf16[32,3,128]{2,0,1:T(8,128)(2,1)S(1)}, u32[]{:S(2)}, u32[]{:S(2)}) collective-permute-start(bf16[32,3,128]{2,0,1:T(8,128)(2,1)S(1)} %convert_bitcast_fusion), channel_id=1, source_target_pairs={{128,0},{136,8},{144,16},{152,24},{160,32},{168,40},{176,48},{184,... | collective-permute-start | bytes 73736 | tf_op jit(solution)/shard_map/ppermute | solution.py:160
  66.7 4.2 %collective-permute-start.4 = (f32[32,3,129]{2,0,1:T(8,128)S(1)}, f32[32,3,129]{2,0,1:T(8,128)S(1)}, u32[]{:S(2)}, u32[]{:S(2)}) collective-permute-start(f32[32,3,129]{2,0,1:T(8,128)S(1)} %pad_maximum_fusion.2), channel_id=1, source_target_pairs={{0,128},{8,136},{16,144},{24,152},{32,160},{40,168},{48,176},{56,1... | collective-permute-start | bytes 148616 | tf_op jit(solution)/shard_map/ppermute | solution.py:162
  73.4 15.9 %all-to-all-start.1 = ((f32[8,8,3,129]{3,1,2,0:T(8,128)}), f32[8,8,3,129]{3,1,2,0:T(8,128)S(1)}, u32[]{:S(2)}, u32[]{:S(2)}) async-start(f32[8,8,3,129]{3,1,2,0:T(8,128)} %pad_maximum_fusion.1), calls=%async_computation.1 | async-start | bytes 393216 | tf_op jit(solution)/shard_map/all_to_all | solution.py:177
  95.9 43.8 %copy-start.4 = (bf16[3072,640]{1,0:T(8,128)(2,1)S(1)}, bf16[3072,640]{1,0:T(8,128)(2,1)}, u32[]{:S(2)}) copy-start(bf16[3072,640]{1,0:T(8,128)(2,1)} %param.9) | copy-start | bytes 11796484

commit v11 on v9

--- a/solution.py
+++ b/solution.py
@@ -80,6 +80,7 @@
 
 
 SEQ_AXES = ("sy", "sz")
+HEAD_AXES = ("hx", "hc")
 ROW_AXES = "sz"
 
 
@@ -195,12 +196,15 @@
         / jnp.sum(level_weights, axis=0)[..., None]
     )
     heads_out = mixed_heads.astype(jnp.bfloat16).reshape(row_count, head_count * head_width)
-    head_devices = lax.axis_size("head")
-    copies = jnp.broadcast_to(heads_out[None], (head_devices,) + heads_out.shape)
-    gathered = lax.all_to_all(copies, "head", 0, 0, tiled=True)
-    weight = out_weight.reshape(head_devices, head_count * head_width, out_weight.shape[1])
+    chips = lax.axis_size("hx")
+    cores = lax.axis_size("hc")
+    copies = jnp.broadcast_to(heads_out[None], (chips,) + heads_out.shape)
+    same_core = lax.all_to_all(copies, "hx", 0, 0, tiled=True)
+    copies = jnp.broadcast_to(same_core[None], (cores,) + same_core.shape)
+    gathered = lax.all_to_all(copies, "hc", 0, 0, tiled=True)
+    weight = out_weight.reshape(chips, cores, head_count * head_width, out_weight.shape[1])
     projected = jnp.einsum(
-        "str,sro->to", gathered, weight, preferred_element_type=jnp.float32
+        "cxtr,xcro->to", gathered, weight, preferred_element_type=jnp.float32
     )
     return projected.astype(jnp.bfloat16)
 
@@ -208,18 +212,18 @@
 def solution(mesh):
     seq_count, head_count = mesh.devices.shape
     split = jax.sharding.Mesh(
-        mesh.devices.reshape(seq_count // ROW, ROW, head_count), SEQ_AXES + ("head",)
+        mesh.devices.reshape(seq_count // ROW, ROW, head_count // 2, 2), SEQ_AXES + HEAD_AXES
     )
     return jax.shard_map(
         local,
         mesh=split,
         in_specs=(
-            P(SEQ_AXES, "head"),
-            P(SEQ_AXES, "head"),
-            P(SEQ_AXES, "head"),
-            P(None, "head"),
-            P(None, "head"),
+            P(SEQ_AXES, HEAD_AXES),
+            P(SEQ_AXES, HEAD_AXES),
+            P(SEQ_AXES, HEAD_AXES),
+            P(None, HEAD_AXES),
+            P(None, HEAD_AXES),
         ),
-        out_specs=P(SEQ_AXES, "head"),
+        out_specs=P(SEQ_AXES, HEAD_AXES),
         check_vma=False,
     )

time: 138 us -> 132 us (0.957)
  blocking collectives: 76.8 us -> 70.2 us
    all_to_all x1 -> x2, blocking collectives: 34.6 us -> 27.9 us  [the longest x1 15.8 us: local(): gathered = lax.all_to_all(copies, 'hc', 0, 0, tiled=True)]
  transfers between devices with their start and end apart: 13 -> 13, of which waited for: 2 -> 2; matrix products, arithmetic and copies ran while one was open for 9% -> 10% of each run, Pallas kernels for 0% -> 0%
where the time goes in v11:
time: 132 us; the launch traced here: 131 us
  blocking collectives  70.2 us (53%)
  starting transfers between devices  28.5 us (22%)
  waiting for transfers between devices  10.3 us (8%)
  matrix products  8.96 us (7%)
  other arithmetic  6.5 us (5%)
  local copies, waits for them, and re-layouts  6.11 us (5%)
    all_gather x1, blocking collectives, local(): ring = lax.all_gather(jnp.concatenate([pair1, pair2], axis=0), ROW_AXES)  42.3 us
    all_to_all x1, blocking collectives, local(): gathered = lax.all_to_all(copies, 'hc', 0, 0, tiled=True)  15.8 us
    all_to_all x1, blocking collectives, local(): same_core = lax.all_to_all(copies, 'hx', 0, 0, tiled=True)  12.1 us
    ppermute x7, starting transfers between devices, local(): visiting.append(lax.ppermute(query2, SEQ_AXES, pairs))  9.04 us
    all_to_all x1, waiting for transfers between devices, local(): returned = lax.all_to_all(packed, 'sy', 0, 0, tiled=True)  8.51 us
    all_to_all x1, starting transfers between devices, local(): returned = lax.all_to_all(packed, 'sy', 0, 0, tiled=True)  7.54 us
    ppermute x3, starting transfers between devices, local(): arrived.append(lax.ppermute(pair0, SEQ_AXES, pairs))  6.88 us
    ppermute x1, starting transfers between devices, local(): lax.ppermute(pack(*whole_row(visiting1, row1, count1)), SEQ_AXES, down)  3.72 us
  transfers between devices with their start and end apart: 13, of which 2 were waited for; matrix products, arithmetic and copies ran while one was open for 10% of the time, Pallas kernels for 0%

profile of v11, /device:TPU:1, one launch (start us, length us, event | category | flops | bytes accessed | tf_op | source)
XLA Modules:
  0.0 131.2 jit_solution(15527908277377313861)
XLA Ops:
  0.0 1.1 reshape_reshape.26
  1.1 0.8 fusion.72
  2.1 1.3 collective-permute-start.5
  3.4 1.3 collective-permute-start.6
  4.7 1.3 collective-permute-start.7
  6.0 1.3 collective-permute-start.8
  7.3 1.3 collective-permute-start.9
  8.6 1.0 reshape_reshape.25
  9.5 1.0 reshape_reshape.24
  10.6 1.1 fusion.26
  11.7 1.1 fusion.28
  13.2 42.3 %all-gather = bf16[640,2,3,128]{3,0,2,1:T(8,128)(2,1)S(1)} all-gather(bf16[40,2,3,128]{3,0,2,1:T(8,128)(2,1)S(1)} %maximum_maximum_fusion.1), channel_id=2, replica_groups=mesh['sy'=8,'sz'=16,'hx'=4,'hc'=2] {'sz'}, dimensions={0}, use_global_device_ids=true | all-gather | bytes 1044480 | tf_op jit(solution)/shard_map/all_gather | solution.py:138
  55.5 0.2 fusion.88
  55.9 0.2 convolution_bitcast_fusion.3
  56.2 0.2 fusion.30
  56.5 0.3 fusion.90
  56.9 0.2 fusion.32
  57.1 0.2 convolution_bitcast_fusion.1
  57.9 0.2 copy.57
  58.0 0.2 fusion.15
  58.3 0.8 pad_maximum_fusion
  59.4 1.3 collective-permute-start.10
  60.7 1.3 collective-permute-start.11
  62.0 1.3 collective-permute-start.3
  63.4 1.3 %collective-permute-start.2 = (bf16[256,2,3,128]{3,0,2,1:T(8,128)(2,1)}, bf16[256,2,3,128]{3,0,2,1:T(8,128)(2,1)S(1)}, u32[]{:S(2)}, u32[]{:S(2)}) collective-permute-start(bf16[256,2,3,128]{3,0,2,1:T(8,128)(2,1)} %pad_maximum_fusion), channel_id=1, source_target_pairs={{0,8},{8,16},{16,24},{32,40},{40,48},{48,56},{64,72},{72,80},{80,8... | collective-permute-start | bytes 1179656 | tf_op jit(solution)/shard_map/ppermute | solution.py:122
  64.7 3.5 %collective-permute-start.1 = (bf16[256,2,3,128]{3,0,2,1:T(8,128)(2,1)}, bf16[256,2,3,128]{3,0,2,1:T(8,128)(2,1)}, u32[]{:S(2)}, u32[]{:S(2)}) collective-permute-start(bf16[256,2,3,128]{3,0,2,1:T(8,128)(2,1)} %pad_maximum_fusion), channel_id=1, source_target_pairs={{0,16},{8,24},{32,48},{40,56},{64,80},{72,88},{96,112},{104,120},{... | collective-permute-start | bytes 1179656 | tf_op jit(solution)/shard_map/ppermute | solution.py:122
  68.3 1.7 %collective-permute-done.10 = bf16[8,3,128]{2,0,1:T(8,128)(2,1)S(1)} collective-permute-done((bf16[8,3,128]{2,0,1:T(8,128)(2,1)S(1)}, bf16[8,3,128]{2,0,1:T(8,128)(2,1)S(1)}, u32[]{:S(2)}, u32[]{:S(2)}) %collective-permute-start.10) | collective-permute-done | bytes 6176 | tf_op jit(solution)/shard_map/ppermute | solution.py:173
  70.0 2.0 %collective-permute-start = (bf16[256,2,3,128]{3,0,2,1:T(8,128)(2,1)}, bf16[256,2,3,128]{3,0,2,1:T(8,128)(2,1)}, u32[]{:S(2)}, u32[]{:S(2)}) collective-permute-start(bf16[256,2,3,128]{3,0,2,1:T(8,128)(2,1)} %pad_maximum_fusion), channel_id=1, source_target_pairs={{0,24},{32,56},{64,88},{96,120},{128,152},{160,184},{192,216},{224... | collective-permute-start | bytes 1179656 | tf_op jit(solution)/shard_map/ppermute | solution.py:122
  72.0 0.3 fusion.87
  72.3 0.2 fusion.40
  72.5 0.2 convolution_bitcast_fusion
  72.8 0.2 copy.64
  73.1 0.3 fusion.89
  73.4 0.2 fusion.33
  73.6 0.2 convolution_bitcast_fusion.2
  74.0 3.7 %collective-permute-start.4 = (f32[32,3,129]{2,0,1:T(8,128)S(1)}, f32[32,3,129]{2,0,1:T(8,128)S(1)}, u32[]{:S(2)}, u32[]{:S(2)}) collective-permute-start(f32[32,3,129]{2,0,1:T(8,128)S(1)} %pad_maximum_fusion.1), channel_id=1, source_target_pairs={{0,128},{8,136},{16,144},{24,152},{32,160},{40,168},{48,176},{56,1... | collective-permute-start | bytes 148616 | tf_op jit(solution)/shard_map/ppermute | solution.py:161
  77.7 0.7 fusion.18
  78.4 7.5 %all-to-all-start = ((f32[8,8,3,129]{3,1,2,0:T(8,128)}), f32[8,8,3,129]{3,1,2,0:T(8,128)S(1)}, u32[]{:S(2)}, u32[]{:S(2)}) async-start(f32[8,8,3,129]{3,1,2,0:T(8,128)} %fusion.18), calls=%async_computation | async-start | bytes 393216 | tf_op jit(solution)/shard_map/all_to_all | solution.py:179
  86.6 0.2 copy.69
  86.8 8.5 %all-to-all-done = f32[8,8,3,129]{3,1,2,0:T(8,128)S(1)} async-done(((f32[8,8,3,129]{3,1,2,0:T(8,128)}), f32[8,8,3,129]{3,1,2,0:T(8,128)S(1)}, u32[]{:S(2)}, u32[]{:S(2)}) %all-to-all-start) | async-done | bytes 99104 | tf_op jit(solution)/shard_map/all_to_all | solution.py:179
  95.4 0.2 copy.96
  96.7 1.2 maximum_maximum_fusion
  97.9 0.7 fusion.3
  98.6 0.7 fusion.2
  99.4 1.2 fusion.11
  101.0 12.1 %all_to_all.15 = bf16[4,256,384]{2,1,0:T(8,128)(2,1)S(1)} all-to-all(bf16[4,256,384]{2,1,0:T(8,128)(2,1)S(1)} %broadcast_in_dim.162), channel_id=1, replica_groups=mesh['sy'=8,'sz'=16,'hx'=4,'hc'=2] {'hx'}, dimensions={0} | all-to-all | bytes 1572864 | tf_op jit(solution)/shard_map/all_to_all | solution.py:202
  113.3 15.8 %all_to_all.16 = bf16[2,4,256,384]{3,2,1,0:T(8,128)(2,1)S(1)} all-to-all(bf16[2,4,256,384]{3,2,1,0:T(8,128)(2,1)S(1)} %broadcast_in_dim.163), channel_id=1, replica_groups=mesh['sy'=8,'sz'=16,'hx'=4,'hc'=2] {'hc'}, dimensions={0} | all-to-all | bytes 3145728 | tf_op jit(solution)/shard_map/all_to_all | solution.py:204
  129.1 2.1 %fusion.8 = bf16[256,640]{1,0:T(8,128)(2,1)} fusion(bf16[2,4,256,384]{3,2,1,0:T(8,128)(2,1)S(1)} %all_to_all.16, bf16[4,2,384,640]{3,2,1,0:T(8,128)(2,1)S(1)} %bitcast.201), kind=kOutput, calls=%fused_computation.10 | convolution fusion | flops 1006796800 | bytes 5832704 | tf_op jit(solution)/shard_map/cxtr,xcro->to/dot_general | solution.py:206
  (104 shorter events, 4.3 us)
Async XLA Ops:
  0.0 56.2 %copy-start.2 = (bf16[256,384]{1,0:T(8,128)(2,1)S(1)}, bf16[256,384]{1,0:T(8,128)(2,1)}, u32[]{:S(2)}) copy-start(bf16[256,384]{1,0:T(8,128)(2,1)} %param.5) | copy-start | bytes 589828
  2.1 57.3 %collective-permute-start.5 = (bf16[8,3,128]{2,0,1:T(8,128)(2,1)S(1)}, bf16[8,3,128]{2,0,1:T(8,128)(2,1)S(1)}, u32[]{:S(2)}, u32[]{:S(2)}) collective-permute-start(bf16[8,3,128]{2,0,1:T(8,128)(2,1)S(1)} %get-tuple-element.12), channel_id=1, source_target_pairs={{128,0},{136,8},{144,16},{152,24},{160,32},{168,40},{176,48},{184,... | collective-permute-start | bytes 18440 | tf_op jit(solution)/shard_map/ppermute | solution.py:173
  3.4 57.4 %collective-permute-start.6 = (bf16[8,3,128]{2,0,1:T(8,128)(2,1)S(1)}, bf16[8,3,128]{2,0,1:T(8,128)(2,1)S(1)}, u32[]{:S(2)}, u32[]{:S(2)}) collective-permute-start(bf16[8,3,128]{2,0,1:T(8,128)(2,1)S(1)} %get-tuple-element.12), channel_id=1, source_target_pairs={{256,0},{264,8},{272,16},{280,24},{288,32},{296,40},{304,48},{312,... | collective-permute-start | bytes 18440 | tf_op jit(solution)/shard_map/ppermute | solution.py:173
  4.7 57.4 %collective-permute-start.7 = (bf16[8,3,128]{2,0,1:T(8,128)(2,1)S(1)}, bf16[8,3,128]{2,0,1:T(8,128)(2,1)S(1)}, u32[]{:S(2)}, u32[]{:S(2)}) collective-permute-start(bf16[8,3,128]{2,0,1:T(8,128)(2,1)S(1)} %get-tuple-element.12), channel_id=1, source_target_pairs={{384,0},{392,8},{400,16},{408,24},{416,32},{424,40},{432,48},{440,... | collective-permute-start | bytes 18440 | tf_op jit(solution)/shard_map/ppermute | solution.py:173
  6.0 57.4 %collective-permute-start.8 = (bf16[8,3,128]{2,0,1:T(8,128)(2,1)S(1)}, bf16[8,3,128]{2,0,1:T(8,128)(2,1)S(1)}, u32[]{:S(2)}, u32[]{:S(2)}) collective-permute-start(bf16[8,3,128]{2,0,1:T(8,128)(2,1)S(1)} %get-tuple-element.12), channel_id=1, source_target_pairs={{512,0},{520,8},{528,16},{536,24},{544,32},{552,40},{560,48},{568,... | collective-permute-start | bytes 18440 | tf_op jit(solution)/shard_map/ppermute | solution.py:173
  7.3 57.5 %collective-permute-start.9 = (bf16[8,3,128]{2,0,1:T(8,128)(2,1)S(1)}, bf16[8,3,128]{2,0,1:T(8,128)(2,1)S(1)}, u32[]{:S(2)}, u32[]{:S(2)}) collective-permute-start(bf16[8,3,128]{2,0,1:T(8,128)(2,1)S(1)} %get-tuple-element.12), channel_id=1, source_target_pairs={{640,0},{648,8},{656,16},{664,24},{672,32},{680,40},{688,48},{696,... | collective-permute-start | bytes 18440 | tf_op jit(solution)/shard_map/ppermute | solution.py:173
  13.2 44.2 %copy-start = (bf16[256,384]{1,0:T(8,128)(2,1)S(1)}, bf16[256,384]{1,0:T(8,128)(2,1)}, u32[]{:S(2)}) copy-start(bf16[256,384]{1,0:T(8,128)(2,1)} %param.7) | copy-start | bytes 589828
  13.2 44.3 %copy-start.1 = (bf16[256,384]{1,0:T(8,128)(2,1)S(1)}, bf16[256,384]{1,0:T(8,128)(2,1)}, u32[]{:S(2)}) copy-start(bf16[256,384]{1,0:T(8,128)(2,1)} %param.6) | copy-start | bytes 589828
  59.4 10.6 %collective-permute-start.10 = (bf16[8,3,128]{2,0,1:T(8,128)(2,1)S(1)}, bf16[8,3,128]{2,0,1:T(8,128)(2,1)S(1)}, u32[]{:S(2)}, u32[]{:S(2)}) collective-permute-start(bf16[8,3,128]{2,0,1:T(8,128)(2,1)S(1)} %get-tuple-element.12), channel_id=1, source_target_pairs={{768,0},{776,8},{784,16},{792,24},{800,32},{808,40},{816,48},{824,... | collective-permute-start | bytes 18440 | tf_op jit(solution)/shard_map/ppermute | solution.py:173
  60.7 11.3 %collective-permute-start.11 = (bf16[8,3,128]{2,0,1:T(8,128)(2,1)S(1)}, bf16[8,3,128]{2,0,1:T(8,128)(2,1)S(1)}, u32[]{:S(2)}, u32[]{:S(2)}) collective-permute-start(bf16[8,3,128]{2,0,1:T(8,128)(2,1)S(1)} %get-tuple-element.12), channel_id=1, source_target_pairs={{896,0},{904,8},{912,16},{920,24},{928,32},{936,40},{944,48},{952,... | collective-permute-start | bytes 18440 | tf_op jit(solution)/shard_map/ppermute | solution.py:173
  62.0 11.0 %collective-permute-start.3 = (bf16[32,3,128]{2,0,1:T(8,128)(2,1)S(1)}, bf16[32,3,128]{2,0,1:T(8,128)(2,1)S(1)}, u32[]{:S(2)}, u32[]{:S(2)}) collective-permute-start(bf16[32,3,128]{2,0,1:T(8,128)(2,1)S(1)} %convert_bitcast_fusion.2), channel_id=1, source_target_pairs={{128,0},{136,8},{144,16},{152,24},{160,32},{168,40},{176,48},{184,... | collective-permute-start | bytes 73736 | tf_op jit(solution)/shard_map/ppermute | solution.py:159
  63.4 33.3 %collective-permute-start.2 = (bf16[256,2,3,128]{3,0,2,1:T(8,128)(2,1)}, bf16[256,2,3,128]{3,0,2,1:T(8,128)(2,1)S(1)}, u32[]{:S(2)}, u32[]{:S(2)}) collective-permute-start(bf16[256,2,3,128]{3,0,2,1:T(8,128)(2,1)} %pad_maximum_fusion), channel_id=1, source_target_pairs={{0,8},{8,16},{16,24},{32,40},{40,48},{48,56},{64,72},{72,80},{80,8... | collective-permute-start | bytes 1179656 | tf_op jit(solution)/shard_map/ppermute | solution.py:122
  64.7 32.0 %collective-permute-start.1 = (bf16[256,2,3,128]{3,0,2,1:T(8,128)(2,1)}, bf16[256,2,3,128]{3,0,2,1:T(8,128)(2,1)}, u32[]{:S(2)}, u32[]{:S(2)}) collective-permute-start(bf16[256,2,3,128]{3,0,2,1:T(8,128)(2,1)} %pad_maximum_fusion), channel_id=1, source_target_pairs={{0,16},{8,24},{32,48},{40,56},{64,80},{72,88},{96,112},{104,120},{... | collective-permute-start | bytes 1179656 | tf_op jit(solution)/shard_map/ppermute | solution.py:122
  70.0 26.7 %collective-permute-start = (bf16[256,2,3,128]{3,0,2,1:T(8,128)(2,1)}, bf16[256,2,3,128]{3,0,2,1:T(8,128)(2,1)}, u32[]{:S(2)}, u32[]{:S(2)}) collective-permute-start(bf16[256,2,3,128]{3,0,2,1:T(8,128)(2,1)} %pad_maximum_fusion), channel_id=1, source_target_pairs={{0,24},{32,56},{64,88},{96,120},{128,152},{160,184},{192,216},{224... | collective-permute-start | bytes 1179656 | tf_op jit(solution)/shard_map/ppermute | solution.py:122
  74.0 12.0 %collective-permute-start.4 = (f32[32,3,129]{2,0,1:T(8,128)S(1)}, f32[32,3,129]{2,0,1:T(8,128)S(1)}, u32[]{:S(2)}, u32[]{:S(2)}) collective-permute-start(f32[32,3,129]{2,0,1:T(8,128)S(1)} %pad_maximum_fusion.1), channel_id=1, source_target_pairs={{0,128},{8,136},{16,144},{24,152},{32,160},{40,168},{48,176},{56,1... | collective-permute-start | bytes 148616 | tf_op jit(solution)/shard_map/ppermute | solution.py:161
  78.4 16.9 %all-to-all-start = ((f32[8,8,3,129]{3,1,2,0:T(8,128)}), f32[8,8,3,129]{3,1,2,0:T(8,128)S(1)}, u32[]{:S(2)}, u32[]{:S(2)}) async-start(f32[8,8,3,129]{3,1,2,0:T(8,128)} %fusion.18), calls=%async_computation | async-start | bytes 393216 | tf_op jit(solution)/shard_map/all_to_all | solution.py:179
  113.1 15.9 %copy-start.3 = (bf16[3072,640]{1,0:T(8,128)(2,1)S(1)}, bf16[3072,640]{1,0:T(8,128)(2,1)}, u32[]{:S(2)}) copy-start(bf16[3072,640]{1,0:T(8,128)(2,1)} %param.9) | copy-start | bytes 11796484

commit v12 on v11

--- a/solution.py
+++ b/solution.py
@@ -200,12 +200,14 @@
     cores = lax.axis_size("hc")
     copies = jnp.broadcast_to(heads_out[None], (chips,) + heads_out.shape)
     same_core = lax.all_to_all(copies, "hx", 0, 0, tiled=True)
-    copies = jnp.broadcast_to(same_core[None], (cores,) + same_core.shape)
-    gathered = lax.all_to_all(copies, "hc", 0, 0, tiled=True)
+    other_core = lax.ppermute(same_core, "hc", [(0, 1), (1, 0)])
     weight = out_weight.reshape(chips, cores, head_count * head_width, out_weight.shape[1])
+    core = lax.axis_index("hc")
+    mine = lax.dynamic_index_in_dim(weight, core, 1, keepdims=False)
+    theirs = lax.dynamic_index_in_dim(weight, 1 - core, 1, keepdims=False)
     projected = jnp.einsum(
-        "cxtr,xcro->to", gathered, weight, preferred_element_type=jnp.float32
-    )
+        "xtr,xro->to", same_core, mine, preferred_element_type=jnp.float32
+    ) + jnp.einsum("xtr,xro->to", other_core, theirs, preferred_element_type=jnp.float32)
     return projected.astype(jnp.bfloat16)
 
 

time: 132 us -> 131 us (level)
  blocking collectives: 70.2 us -> 54.4 us
  starting transfers between devices: 28.5 us -> 39.8 us
  matrix products: 8.96 us -> 12.2 us
    all_to_all x1 -> x0, blocking collectives: 15.8 us -> none  [local(): gathered = lax.all_to_all(copies, 'hc', 0, 0, tiled=True)]
    ppermute x0 -> x1, starting transfers between devices: none -> 12.8 us  [local(): other_core = lax.ppermute(same_core, 'hc', [(0, 1), (1, 0)])]
    dot_general x1 -> x2, matrix products: 2.11 us -> 5.4 us  [the longest x1 3.07 us: local(): jnp.einsum('xtr,xro->to', other_core, theirs, preferred_element_type=jnp....]
  transfers between devices with their start and end apart: 13 -> 14, of which waited for: 2 -> 2; matrix products, arithmetic and copies ran while one was open for 10% -> 12% of each run, Pallas kernels for 0% -> 0%
where the time goes in v12:
time: 131 us
  blocking collectives  54.4 us (42%)
  starting transfers between devices  39.8 us (30%)
  matrix products  12.2 us (9%)
  waiting for transfers between devices  11 us (8%)
  other arithmetic  6.38 us (5%)
  local copies, waits for them, and re-layouts  5.96 us (5%)
    all_gather x1, blocking collectives, local(): ring = lax.all_gather(jnp.concatenate([pair1, pair2], axis=0), ROW_AXES)  42.3 us
    ppermute x1, starting transfers between devices, local(): other_core = lax.ppermute(same_core, 'hc', [(0, 1), (1, 0)])  12.8 us
    all_to_all x1, blocking collectives, local(): same_core = lax.all_to_all(copies, 'hx', 0, 0, tiled=True)  12.1 us
    ppermute x7, starting transfers between devices, local(): visiting.append(lax.ppermute(query2, SEQ_AXES, pairs))  9.04 us
    all_to_all x1, waiting for transfers between devices, local(): returned = lax.all_to_all(packed, 'sy', 0, 0, tiled=True)  8.51 us
    all_to_all x1, starting transfers between devices, local(): returned = lax.all_to_all(packed, 'sy', 0, 0, tiled=True)  6.84 us
    ppermute x3, starting transfers between devices, local(): arrived.append(lax.ppermute(pair0, SEQ_AXES, pairs))  6.15 us
    ppermute x1, starting transfers between devices, local(): lax.ppermute(pack(*whole_row(visiting1, row1, count1)), SEQ_AXES, down)  3.72 us
  transfers between devices with their start and end apart: 14, of which 2 were waited for; matrix products, arithmetic and copies ran while one was open for 12% of the time, Pallas kernels for 0%

profile of v12, /device:TPU:1, one launch (start us, length us, event | category | flops | bytes accessed | tf_op | source)
XLA Modules:
  0.0 130.5 jit_solution(10550828814923105557)
XLA Ops:
  0.0 1.1 reshape_reshape.26
  1.1 0.8 fusion.84
  2.1 1.3 collective-permute-start.5
  3.4 1.3 collective-permute-start.6
  4.7 1.3 collective-permute-start.7
  6.0 1.3 collective-permute-start.8
  7.3 1.3 collective-permute-start.9
  8.6 1.0 reshape_reshape.25
  9.5 1.0 reshape_reshape.24
  10.6 1.1 fusion.36
  11.7 1.1 fusion.38
  13.2 42.3 %all-gather = bf16[640,2,3,128]{3,0,2,1:T(8,128)(2,1)S(1)} all-gather(bf16[40,2,3,128]{3,0,2,1:T(8,128)(2,1)S(1)} %maximum_maximum_fusion.1), channel_id=2, replica_groups=mesh['sy'=8,'sz'=16,'hx'=4,'hc'=2] {'sz'}, dimensions={0}, use_global_device_ids=true | all-gather | bytes 1044480 | tf_op jit(solution)/shard_map/all_gather | solution.py:138
  55.5 0.2 fusion.100
  55.9 0.2 convolution_bitcast_fusion.3
  56.2 0.2 fusion.40
  56.5 0.3 fusion.102
  56.9 0.2 fusion.42
  57.1 0.2 convolution_bitcast_fusion.1
  57.9 0.2 copy.60
  58.0 0.2 fusion.25
  58.3 0.8 pad_maximum_fusion
  59.4 1.3 collective-permute-start.10
  60.7 1.3 collective-permute-start.11
  62.0 1.3 collective-permute-start.3
  63.4 1.3 %collective-permute-start.2 = (bf16[256,2,3,128]{3,0,2,1:T(8,128)(2,1)}, bf16[256,2,3,128]{3,0,2,1:T(8,128)(2,1)S(1)}, u32[]{:S(2)}, u32[]{:S(2)}) collective-permute-start(bf16[256,2,3,128]{3,0,2,1:T(8,128)(2,1)} %pad_maximum_fusion), channel_id=1, source_target_pairs={{0,8},{8,16},{16,24},{32,40},{40,48},{48,56},{64,72},{72,80},{80,8... | collective-permute-start | bytes 1179656 | tf_op jit(solution)/shard_map/ppermute | solution.py:122
  64.7 2.8 %collective-permute-start.1 = (bf16[256,2,3,128]{3,0,2,1:T(8,128)(2,1)}, bf16[256,2,3,128]{3,0,2,1:T(8,128)(2,1)S(1)}, u32[]{:S(2)}, u32[]{:S(2)}) collective-permute-start(bf16[256,2,3,128]{3,0,2,1:T(8,128)(2,1)} %pad_maximum_fusion), channel_id=1, source_target_pairs={{0,16},{8,24},{32,48},{40,56},{64,80},{72,88},{96,112},{104,120},{... | collective-permute-start | bytes 1179656 | tf_op jit(solution)/shard_map/ppermute | solution.py:122
  67.5 2.4 %collective-permute-done.10 = bf16[8,3,128]{2,0,1:T(8,128)(2,1)S(1)} collective-permute-done((bf16[8,3,128]{2,0,1:T(8,128)(2,1)S(1)}, bf16[8,3,128]{2,0,1:T(8,128)(2,1)S(1)}, u32[]{:S(2)}, u32[]{:S(2)}) %collective-permute-start.10) | collective-permute-done | bytes 6176 | tf_op jit(solution)/shard_map/ppermute | solution.py:173
  70.0 2.0 %collective-permute-start = (bf16[256,2,3,128]{3,0,2,1:T(8,128)(2,1)}, bf16[256,2,3,128]{3,0,2,1:T(8,128)(2,1)}, u32[]{:S(2)}, u32[]{:S(2)}) collective-permute-start(bf16[256,2,3,128]{3,0,2,1:T(8,128)(2,1)} %pad_maximum_fusion), channel_id=1, source_target_pairs={{0,24},{32,56},{64,88},{96,120},{128,152},{160,184},{192,216},{224... | collective-permute-start | bytes 1179656 | tf_op jit(solution)/shard_map/ppermute | solution.py:122
  72.0 0.3 fusion.99
  72.3 0.2 fusion.50
  72.5 0.2 convolution_bitcast_fusion
  72.8 0.2 copy.67
  73.1 0.3 fusion.101
  73.4 0.2 fusion.43
  73.6 0.2 convolution_bitcast_fusion.2
  74.0 3.7 %collective-permute-start.4 = (f32[32,3,129]{2,0,1:T(8,128)S(1)}, f32[32,3,129]{2,0,1:T(8,128)S(1)}, u32[]{:S(2)}, u32[]{:S(2)}) collective-permute-start(f32[32,3,129]{2,0,1:T(8,128)S(1)} %pad_maximum_fusion.1), channel_id=1, source_target_pairs={{0,128},{8,136},{16,144},{24,152},{32,160},{40,168},{48,176},{56,1... | collective-permute-start | bytes 148616 | tf_op jit(solution)/shard_map/ppermute | solution.py:161
  77.7 0.7 fusion.28
  78.4 6.8 %all-to-all-start = ((f32[8,8,3,129]{3,1,2,0:T(8,128)}), f32[8,8,3,129]{3,1,2,0:T(8,128)S(1)}, u32[]{:S(2)}, u32[]{:S(2)}) async-start(f32[8,8,3,129]{3,1,2,0:T(8,128)} %fusion.28), calls=%async_computation | async-start | bytes 393216 | tf_op jit(solution)/shard_map/all_to_all | solution.py:179
  86.1 8.5 %all-to-all-done = f32[8,8,3,129]{3,1,2,0:T(8,128)S(1)} async-done(((f32[8,8,3,129]{3,1,2,0:T(8,128)}), f32[8,8,3,129]{3,1,2,0:T(8,128)S(1)}, u32[]{:S(2)}, u32[]{:S(2)}) %all-to-all-start) | async-done | bytes 99104 | tf_op jit(solution)/shard_map/all_to_all | solution.py:179
  94.6 0.2 copy.99
  96.0 1.1 maximum_maximum_fusion
  97.1 0.7 fusion.1
  97.8 0.7 fusion
  98.5 1.2 fusion.21
  100.2 12.1 %all_to_all.10 = bf16[4,256,384]{2,1,0:T(8,128)(2,1)S(1)} all-to-all(bf16[4,256,384]{2,1,0:T(8,128)(2,1)S(1)} %broadcast_in_dim.156), channel_id=1, replica_groups=mesh['sy'=8,'sz'=16,'hx'=4,'hc'=2] {'hx'}, dimensions={0} | all-to-all | bytes 1572864 | tf_op jit(solution)/shard_map/all_to_all | solution.py:202
  112.3 12.8 %collective-permute-start.12 = (bf16[4,256,384]{2,1,0:T(8,128)(2,1)S(1)}, bf16[4,256,384]{2,1,0:T(8,128)(2,1)S(1)}, u32[]{:S(2)}, u32[]{:S(2)}) collective-permute-start(bf16[4,256,384]{2,1,0:T(8,128)(2,1)S(1)} %all_to_all.10), channel_id=1, source_target_pairs={{0,1},{1,0},{2,3},{3,2},{4,5},{5,4},{6,7},{7,6},{8,9},{9,8},{10,11... | collective-permute-start | bytes 2359304 | tf_op jit(solution)/shard_map/ppermute | solution.py:203
  125.1 2.3 %fusion.9 = f32[256,640]{1,0:T(8,128)S(1)} fusion(bf16[4,256,384]{2,1,0:T(8,128)(2,1)S(1)} %all_to_all.10, bf16[4,2,384,640]{3,2,1,0:T(8,128)(2,1)} %bitcast.211, s32[]{:T(128)S(6)} %select_n.222), kind=kOutput, calls=%fused_computation.13 | convolution fusion | flops 503316480 | bytes 3407876 | tf_op jit(solution)/shard_map/xtr,xro->to/dot_general | solution.py:208
  127.5 3.1 %fusion.18 = bf16[256,640]{1,0:T(8,128)(2,1)} fusion(f32[256,640]{1,0:T(8,128)S(1)} %fusion.9, bf16[4,256,384]{2,1,0:T(8,128)(2,1)S(1)} %collective-permute-done.12, bf16[4,2,384,640]{3,2,1,0:T(8,128)(2,1)} %bitcast.212, s32[]{:T(128)S(6)} %select_n.223), kind=kOutput, calls=%fused_computation.16 | convolution fusion | flops 503644160 | bytes 3735556 | tf_op jit(solution)/shard_map/xtr,xro->to/dot_general | solution.py:210
  (103 shorter events, 4.3 us)
Async XLA Ops:
  0.0 56.2 %copy-start.2 = (bf16[256,384]{1,0:T(8,128)(2,1)S(1)}, bf16[256,384]{1,0:T(8,128)(2,1)}, u32[]{:S(2)}) copy-start(bf16[256,384]{1,0:T(8,128)(2,1)} %param.5) | copy-start | bytes 589828
  2.1 57.3 %collective-permute-start.5 = (bf16[8,3,128]{2,0,1:T(8,128)(2,1)S(1)}, bf16[8,3,128]{2,0,1:T(8,128)(2,1)S(1)}, u32[]{:S(2)}, u32[]{:S(2)}) collective-permute-start(bf16[8,3,128]{2,0,1:T(8,128)(2,1)S(1)} %get-tuple-element.12), channel_id=1, source_target_pairs={{128,0},{136,8},{144,16},{152,24},{160,32},{168,40},{176,48},{184,... | collective-permute-start | bytes 18440 | tf_op jit(solution)/shard_map/ppermute | solution.py:173
  3.4 57.4 %collective-permute-start.6 = (bf16[8,3,128]{2,0,1:T(8,128)(2,1)S(1)}, bf16[8,3,128]{2,0,1:T(8,128)(2,1)S(1)}, u32[]{:S(2)}, u32[]{:S(2)}) collective-permute-start(bf16[8,3,128]{2,0,1:T(8,128)(2,1)S(1)} %get-tuple-element.12), channel_id=1, source_target_pairs={{256,0},{264,8},{272,16},{280,24},{288,32},{296,40},{304,48},{312,... | collective-permute-start | bytes 18440 | tf_op jit(solution)/shard_map/ppermute | solution.py:173
  4.7 57.4 %collective-permute-start.7 = (bf16[8,3,128]{2,0,1:T(8,128)(2,1)S(1)}, bf16[8,3,128]{2,0,1:T(8,128)(2,1)S(1)}, u32[]{:S(2)}, u32[]{:S(2)}) collective-permute-start(bf16[8,3,128]{2,0,1:T(8,128)(2,1)S(1)} %get-tuple-element.12), channel_id=1, source_target_pairs={{384,0},{392,8},{400,16},{408,24},{416,32},{424,40},{432,48},{440,... | collective-permute-start | bytes 18440 | tf_op jit(solution)/shard_map/ppermute | solution.py:173
  6.0 57.4 %collective-permute-start.8 = (bf16[8,3,128]{2,0,1:T(8,128)(2,1)S(1)}, bf16[8,3,128]{2,0,1:T(8,128)(2,1)S(1)}, u32[]{:S(2)}, u32[]{:S(2)}) collective-permute-start(bf16[8,3,128]{2,0,1:T(8,128)(2,1)S(1)} %get-tuple-element.12), channel_id=1, source_target_pairs={{512,0},{520,8},{528,16},{536,24},{544,32},{552,40},{560,48},{568,... | collective-permute-start | bytes 18440 | tf_op jit(solution)/shard_map/ppermute | solution.py:173
  7.3 57.5 %collective-permute-start.9 = (bf16[8,3,128]{2,0,1:T(8,128)(2,1)S(1)}, bf16[8,3,128]{2,0,1:T(8,128)(2,1)S(1)}, u32[]{:S(2)}, u32[]{:S(2)}) collective-permute-start(bf16[8,3,128]{2,0,1:T(8,128)(2,1)S(1)} %get-tuple-element.12), channel_id=1, source_target_pairs={{640,0},{648,8},{656,16},{664,24},{672,32},{680,40},{688,48},{696,... | collective-permute-start | bytes 18440 | tf_op jit(solution)/shard_map/ppermute | solution.py:173
  13.2 44.2 %copy-start = (bf16[256,384]{1,0:T(8,128)(2,1)S(1)}, bf16[256,384]{1,0:T(8,128)(2,1)}, u32[]{:S(2)}) copy-start(bf16[256,384]{1,0:T(8,128)(2,1)} %param.7) | copy-start | bytes 589828
  13.2 44.3 %copy-start.1 = (bf16[256,384]{1,0:T(8,128)(2,1)S(1)}, bf16[256,384]{1,0:T(8,128)(2,1)}, u32[]{:S(2)}) copy-start(bf16[256,384]{1,0:T(8,128)(2,1)} %param.6) | copy-start | bytes 589828
  59.4 10.6 %collective-permute-start.10 = (bf16[8,3,128]{2,0,1:T(8,128)(2,1)S(1)}, bf16[8,3,128]{2,0,1:T(8,128)(2,1)S(1)}, u32[]{:S(2)}, u32[]{:S(2)}) collective-permute-start(bf16[8,3,128]{2,0,1:T(8,128)(2,1)S(1)} %get-tuple-element.12), channel_id=1, source_target_pairs={{768,0},{776,8},{784,16},{792,24},{800,32},{808,40},{816,48},{824,... | collective-permute-start | bytes 18440 | tf_op jit(solution)/shard_map/ppermute | solution.py:173
  60.7 11.3 %collective-permute-start.11 = (bf16[8,3,128]{2,0,1:T(8,128)(2,1)S(1)}, bf16[8,3,128]{2,0,1:T(8,128)(2,1)S(1)}, u32[]{:S(2)}, u32[]{:S(2)}) collective-permute-start(bf16[8,3,128]{2,0,1:T(8,128)(2,1)S(1)} %get-tuple-element.12), channel_id=1, source_target_pairs={{896,0},{904,8},{912,16},{920,24},{928,32},{936,40},{944,48},{952,... | collective-permute-start | bytes 18440 | tf_op jit(solution)/shard_map/ppermute | solution.py:173
  62.0 11.0 %collective-permute-start.3 = (bf16[32,3,128]{2,0,1:T(8,128)(2,1)S(1)}, bf16[32,3,128]{2,0,1:T(8,128)(2,1)S(1)}, u32[]{:S(2)}, u32[]{:S(2)}) collective-permute-start(bf16[32,3,128]{2,0,1:T(8,128)(2,1)S(1)} %convert_bitcast_fusion.2), channel_id=1, source_target_pairs={{128,0},{136,8},{144,16},{152,24},{160,32},{168,40},{176,48},{184,... | collective-permute-start | bytes 73736 | tf_op jit(solution)/shard_map/ppermute | solution.py:159
  63.4 32.6 %collective-permute-start.2 = (bf16[256,2,3,128]{3,0,2,1:T(8,128)(2,1)}, bf16[256,2,3,128]{3,0,2,1:T(8,128)(2,1)S(1)}, u32[]{:S(2)}, u32[]{:S(2)}) collective-permute-start(bf16[256,2,3,128]{3,0,2,1:T(8,128)(2,1)} %pad_maximum_fusion), channel_id=1, source_target_pairs={{0,8},{8,16},{16,24},{32,40},{40,48},{48,56},{64,72},{72,80},{80,8... | collective-permute-start | bytes 1179656 | tf_op jit(solution)/shard_map/ppermute | solution.py:122
  64.7 31.3 %collective-permute-start.1 = (bf16[256,2,3,128]{3,0,2,1:T(8,128)(2,1)}, bf16[256,2,3,128]{3,0,2,1:T(8,128)(2,1)S(1)}, u32[]{:S(2)}, u32[]{:S(2)}) collective-permute-start(bf16[256,2,3,128]{3,0,2,1:T(8,128)(2,1)} %pad_maximum_fusion), channel_id=1, source_target_pairs={{0,16},{8,24},{32,48},{40,56},{64,80},{72,88},{96,112},{104,120},{... | collective-permute-start | bytes 1179656 | tf_op jit(solution)/shard_map/ppermute | solution.py:122
  70.0 26.0 %collective-permute-start = (bf16[256,2,3,128]{3,0,2,1:T(8,128)(2,1)}, bf16[256,2,3,128]{3,0,2,1:T(8,128)(2,1)}, u32[]{:S(2)}, u32[]{:S(2)}) collective-permute-start(bf16[256,2,3,128]{3,0,2,1:T(8,128)(2,1)} %pad_maximum_fusion), channel_id=1, source_target_pairs={{0,24},{32,56},{64,88},{96,120},{128,152},{160,184},{192,216},{224... | collective-permute-start | bytes 1179656 | tf_op jit(solution)/shard_map/ppermute | solution.py:122
  74.0 11.3 %collective-permute-start.4 = (f32[32,3,129]{2,0,1:T(8,128)S(1)}, f32[32,3,129]{2,0,1:T(8,128)S(1)}, u32[]{:S(2)}, u32[]{:S(2)}) collective-permute-start(f32[32,3,129]{2,0,1:T(8,128)S(1)} %pad_maximum_fusion.1), channel_id=1, source_target_pairs={{0,128},{8,136},{16,144},{24,152},{32,160},{40,168},{48,176},{56,1... | collective-permute-start | bytes 148616 | tf_op jit(solution)/shard_map/ppermute | solution.py:161
  78.4 16.2 %all-to-all-start = ((f32[8,8,3,129]{3,1,2,0:T(8,128)}), f32[8,8,3,129]{3,1,2,0:T(8,128)S(1)}, u32[]{:S(2)}, u32[]{:S(2)}) async-start(f32[8,8,3,129]{3,1,2,0:T(8,128)} %fusion.28), calls=%async_computation | async-start | bytes 393216 | tf_op jit(solution)/shard_map/all_to_all | solution.py:179
  112.3 15.1 %collective-permute-start.12 = (bf16[4,256,384]{2,1,0:T(8,128)(2,1)S(1)}, bf16[4,256,384]{2,1,0:T(8,128)(2,1)S(1)}, u32[]{:S(2)}, u32[]{:S(2)}) collective-permute-start(bf16[4,256,384]{2,1,0:T(8,128)(2,1)S(1)} %all_to_all.10), channel_id=1, source_target_pairs={{0,1},{1,0},{2,3},{3,2},{4,5},{5,4},{6,7},{7,6},{8,9},{9,8},{10,11... | collective-permute-start | bytes 2359304 | tf_op jit(solution)/shard_map/ppermute | solution.py:203

commit v13 on v12

--- a/solution.py
+++ b/solution.py
@@ -114,8 +114,20 @@
     full_outs = []
     full_lses = []
 
+    chooser1, query1, pair1 = level_setup(query_all, key_all, value_all, level_offsets[1], RATE_MID)
+    chooser2, query2, pair2 = level_setup(query_all, key_all, value_all, level_offsets[2], RATE_TOP)
+    count1 = pair1.shape[0]
+    count2 = pair2.shape[0]
+    copies = jnp.broadcast_to(query2[None], (rows_total,) + query2.shape)
+    column_queries = lax.all_to_all(copies, "sy", 0, 0, tiled=True)
+    payload, column_queries = lax.optimization_barrier(
+        (jnp.concatenate([pair1, pair2], axis=0), column_queries)
+    )
+    ring = lax.all_gather(payload, ROW_AXES)
+
     span0 = SEG_ROWS // row_count
     chooser0, query0, pair0 = level_setup(query_all, key_all, value_all, level_offsets[0], 1)
+    pair0, ring = lax.optimization_barrier((pair0, ring))
     arrived = []
     for shift in range(span0 - 1, 0, -1):
         pairs = [(s, s + shift) for s in range(seq_count) if s % span0 + shift < span0]
@@ -131,11 +143,6 @@
     full_outs.append(full_out)
     full_lses.append(full_lse)
 
-    chooser1, query1, pair1 = level_setup(query_all, key_all, value_all, level_offsets[1], RATE_MID)
-    chooser2, query2, pair2 = level_setup(query_all, key_all, value_all, level_offsets[2], RATE_TOP)
-    count1 = pair1.shape[0]
-    count2 = pair2.shape[0]
-    ring = lax.all_gather(jnp.concatenate([pair1, pair2], axis=0), ROW_AXES)
     row1 = ring[:, :count1]
     row2 = ring[:, count1:]
 
@@ -167,15 +174,10 @@
     full_lses.append(full_lse)
 
     own_out2, own_lse2 = own_row(query2, row2, count2)
-    visiting = [query2]
-    for gap in range(1, rows_total):
-        pairs = [(s, s - gap * row_len) for s in range(seq_count) if s // row_len >= gap]
-        visiting.append(lax.ppermute(query2, SEQ_AXES, pairs))
-    cross_out, cross_lse = whole_row(jnp.concatenate(visiting, axis=0), row2, count2)
+    cross_out, cross_lse = whole_row(
+        column_queries.reshape(rows_total * count2, head_count, head_width), row2, count2
+    )
     packed = pack(cross_out, cross_lse).reshape(rows_total, count2, head_count, head_width + 1)
-    doubled = jnp.concatenate([packed, packed], axis=0)
-    start = (rows_total - row_y) % rows_total
-    packed = lax.dynamic_slice_in_dim(doubled, start, rows_total, axis=0)
     returned = lax.all_to_all(packed, "sy", 0, 0, tiled=True)
     back_out, back_lse = unpack(returned)
     source_row = lax.broadcasted_iota(jnp.int32, back_lse.shape, 0)

time: 131 us -> 128 us (0.977)
  the two profiles are of different devices: /device:TPU:1 before, /device:TPU:169 now
where the time goes in v13:
time: 128 us
  blocking collectives  53 us (41%)
  starting transfers between devices  26.2 us (20%)
  waiting for transfers between devices  22.4 us (18%)
  matrix products  12.2 us (10%)
  local copies, waits for them, and re-layouts  8.5 us (7%)
  other arithmetic  4.55 us (4%)
    all_gather x1, blocking collectives, local(): ring = lax.all_gather(payload, ROW_AXES)  37.9 us
    ppermute x3, waiting for transfers between devices, local(): arrived.append(lax.ppermute(pair0, SEQ_AXES, pairs))  18.9 us
    all_to_all x1, blocking collectives, local(): same_core = lax.all_to_all(copies, 'hx', 0, 0, tiled=True)  15.2 us
    all_to_all x1, starting transfers between devices, local(): returned = lax.all_to_all(packed, 'sy', 0, 0, tiled=True)  7.55 us
    all_to_all x1, starting transfers between devices, local(): column_queries = lax.all_to_all(copies, 'sy', 0, 0, tiled=True)  6.53 us
    ppermute x3, starting transfers between devices, local(): arrived.append(lax.ppermute(pair0, SEQ_AXES, pairs))  3.9 us
    ppermute x1, starting transfers between devices, local(): other_core = lax.ppermute(same_core, 'hc', [(0, 1), (1, 0)])  3.83 us
    all_to_all x1, waiting for transfers between devices, local(): returned = lax.all_to_all(packed, 'sy', 0, 0, tiled=True)  3.49 us
  transfers between devices with their start and end apart: 8, of which 2 were waited for; matrix products, arithmetic and copies ran while one was open for 12% of the time, Pallas kernels for 0%

profile of v13, /device:TPU:169, one launch (start us, length us, event | category | flops | bytes accessed | tf_op | source)
XLA Modules:
  0.0 127.5 jit_solution(16574829162293281123)
XLA Ops:
  0.0 0.8 fusion.81
  0.8 1.0 reshape_reshape.25
  2.0 0.6 broadcast_in_dim.94
  2.6 6.5 %all-to-all-start = ((bf16[8,8,3,128]{3,1,2,0:T(8,128)(2,1)}), bf16[8,8,3,128]{3,1,2,0:T(8,128)(2,1)S(1)}, u32[]{:S(2)}, u32[]{:S(2)}) async-start(bf16[8,8,3,128]{3,1,2,0:T(8,128)(2,1)} %broadcast_in_dim.94), calls=%async_computation | async-start | bytes 98304 | tf_op jit(solution)/shard_map/all_to_all | solution.py:122
  9.2 1.1 fusion.27
  10.4 3.1 %collective-permute-start.3 = (bf16[32,3,128]{2,0,1:T(8,128)(2,1)S(1)}, bf16[32,3,128]{2,0,1:T(8,128)(2,1)S(1)}, u32[]{:S(2)}, u32[]{:S(2)}) collective-permute-start(bf16[32,3,128]{2,0,1:T(8,128)(2,1)S(1)} %convert_bitcast_fusion), channel_id=1, source_target_pairs={{128,0},{136,8},{144,16},{152,24},{160,32},{168,40},{176,48},{184,... | collective-permute-start | bytes 73736 | tf_op jit(solution)/shard_map/ppermute | solution.py:166
  13.5 1.1 copy.59
  14.5 1.0 reshape_reshape.24
  15.5 1.1 copy.58
  16.6 1.0 reshape_reshape.23
  17.6 1.1 fusion.35
  18.7 0.2 fusion.37
  19.2 0.2 copy.61
  19.3 0.2 copy.60
  20.1 0.2 fusion.25
  20.4 37.9 %all-gather = bf16[640,2,3,128]{3,0,2,1:T(8,128)(2,1)S(1)} all-gather(bf16[40,2,3,128]{3,0,2,1:T(8,128)(2,1)S(1)} %maximum_maximum_fusion), channel_id=2, replica_groups=mesh['sy'=8,'sz'=16,'hx'=4,'hc'=2] {'sz'}, dimensions={0}, use_global_device_ids=true | all-gather | bytes 1044480 | tf_op jit(solution)/shard_map/all_gather | solution.py:126
  58.3 0.3 fusion.98
  58.6 0.2 fusion.47
  58.8 0.2 convolution_bitcast_fusion
  59.0 0.2 fusion.99
  59.3 0.2 fusion.60
  59.5 0.2 convolution_bitcast_fusion.3
  59.8 0.3 fusion.100
  60.1 0.2 fusion.40
  60.3 0.2 convolution_bitcast_fusion.2
  60.5 0.3 fusion.101
  60.9 0.2 fusion.39
  61.1 0.2 convolution_bitcast_fusion.1
  61.3 0.7 collective-permute-start
  62.0 1.3 %collective-permute-start.1 = (bf16[256,2,3,128]{3,0,2,1:T(8,128)(2,1)S(1)}, bf16[256,2,3,128]{3,0,2,1:T(8,128)(2,1)S(1)}, u32[]{:S(2)}, u32[]{:S(2)}) collective-permute-start(bf16[256,2,3,128]{3,0,2,1:T(8,128)(2,1)S(1)} %pad_maximum_fusion), channel_id=1, source_target_pairs={{0,16},{8,24},{32,48},{40,56},{64,80},{72,88},{96,112},{104,120},{... | collective-permute-start | bytes 1179656 | tf_op jit(solution)/shard_map/ppermute | solution.py:134
  63.3 1.9 %collective-permute-start.2 = (bf16[256,2,3,128]{3,0,2,1:T(8,128)(2,1)S(1)}, bf16[256,2,3,128]{3,0,2,1:T(8,128)(2,1)S(1)}, u32[]{:S(2)}, u32[]{:S(2)}) collective-permute-start(bf16[256,2,3,128]{3,0,2,1:T(8,128)(2,1)S(1)} %pad_maximum_fusion), channel_id=1, source_target_pairs={{0,8},{8,16},{16,24},{32,40},{40,48},{48,56},{64,72},{72,80},{80,8... | collective-permute-start | bytes 1179656 | tf_op jit(solution)/shard_map/ppermute | solution.py:134
  65.3 0.2 copy.68
  65.7 1.3 %collective-permute-start.4 = (f32[32,3,129]{2,0,1:T(8,128)S(1)}, f32[32,3,129]{2,0,1:T(8,128)S(1)}, u32[]{:S(2)}, u32[]{:S(2)}) collective-permute-start(f32[32,3,129]{2,0,1:T(8,128)S(1)} %pad_maximum_fusion.2), channel_id=1, source_target_pairs={{0,128},{8,136},{16,144},{24,152},{32,160},{40,168},{48,176},{56,1... | collective-permute-start | bytes 148616 | tf_op jit(solution)/shard_map/ppermute | solution.py:168
  67.0 0.7 pad_maximum_fusion.1
  67.7 7.5 %all-to-all-start.1 = ((f32[8,8,3,129]{3,1,2,0:T(8,128)}), f32[8,8,3,129]{3,1,2,0:T(8,128)S(1)}, u32[]{:S(2)}, u32[]{:S(2)}) async-start(f32[8,8,3,129]{3,1,2,0:T(8,128)} %pad_maximum_fusion.1), calls=%async_computation.1 | async-start | bytes 393216 | tf_op jit(solution)/shard_map/all_to_all | solution.py:181
  75.9 0.2 copy.73
  76.1 3.5 %all-to-all-done.1 = f32[8,8,3,129]{3,1,2,0:T(8,128)S(1)} async-done(((f32[8,8,3,129]{3,1,2,0:T(8,128)}), f32[8,8,3,129]{3,1,2,0:T(8,128)S(1)}, u32[]{:S(2)}, u32[]{:S(2)}) %all-to-all-start.1) | async-done | bytes 99104 | tf_op jit(solution)/shard_map/all_to_all | solution.py:181
  79.6 0.2 copy.100
  80.7 0.2 copy.78
  81.0 18.9 %collective-permute-done.2 = bf16[256,2,3,128]{3,0,2,1:T(8,128)(2,1)S(1)} collective-permute-done((bf16[256,2,3,128]{3,0,2,1:T(8,128)(2,1)S(1)}, bf16[256,2,3,128]{3,0,2,1:T(8,128)(2,1)S(1)}, u32[]{:S(2)}, u32[]{:S(2)}) %collective-permute-start.2) | collective-permute-done | bytes 393248 | tf_op jit(solution)/shard_map/ppermute | solution.py:134
  100.0 0.7 fusion.1
  100.7 0.7 fusion
  101.4 1.2 fusion.21
  102.8 0.2 copy.79
  103.1 15.2 %all_to_all.15 = bf16[4,256,384]{2,1,0:T(8,128)(2,1)S(1)} all-to-all(bf16[4,256,384]{2,1,0:T(8,128)(2,1)S(1)} %broadcast_in_dim.163), channel_id=1, replica_groups=mesh['sy'=8,'sz'=16,'hx'=4,'hc'=2] {'hx'}, dimensions={0} | all-to-all | bytes 1572864 | tf_op jit(solution)/shard_map/all_to_all | solution.py:204
  118.2 3.8 %collective-permute-start.5 = (bf16[4,256,384]{2,1,0:T(8,128)(2,1)S(1)}, bf16[4,256,384]{2,1,0:T(8,128)(2,1)S(1)}, u32[]{:S(2)}, u32[]{:S(2)}) collective-permute-start(bf16[4,256,384]{2,1,0:T(8,128)(2,1)S(1)} %all_to_all.15), channel_id=1, source_target_pairs={{0,1},{1,0},{2,3},{3,2},{4,5},{5,4},{6,7},{7,6},{8,9},{9,8},{10,11... | collective-permute-start | bytes 2359304 | tf_op jit(solution)/shard_map/ppermute | solution.py:205
  122.1 2.3 %fusion.9 = f32[256,640]{1,0:T(8,128)S(1)} fusion(bf16[4,256,384]{2,1,0:T(8,128)(2,1)S(1)} %all_to_all.15, bf16[4,2,384,640]{3,2,1,0:T(8,128)(2,1)} %bitcast.214, s32[]{:T(128)S(6)} %select_n.210), kind=kOutput, calls=%fused_computation.12 | convolution fusion | flops 503316480 | bytes 3407876 | tf_op jit(solution)/shard_map/xtr,xro->to/dot_general | solution.py:210
  124.4 3.1 %fusion.18 = bf16[256,640]{1,0:T(8,128)(2,1)} fusion(f32[256,640]{1,0:T(8,128)S(1)} %fusion.9, bf16[4,256,384]{2,1,0:T(8,128)(2,1)S(1)} %collective-permute-done.5, bf16[4,2,384,640]{3,2,1,0:T(8,128)(2,1)} %bitcast.215, s32[]{:T(128)S(6)} %select_n.211), kind=kOutput, calls=%fused_computation.15 | convolution fusion | flops 503644160 | bytes 3735556 | tf_op jit(solution)/shard_map/xtr,xro->to/dot_general | solution.py:212
  (86 shorter events, 3.4 us)
Async XLA Ops:
  0.0 19.0 %copy-start.1 = (bf16[256,384]{1,0:T(8,128)(2,1)S(1)}, bf16[256,384]{1,0:T(8,128)(2,1)}, u32[]{:S(2)}) copy-start(bf16[256,384]{1,0:T(8,128)(2,1)} %param.5) | copy-start | bytes 589828
  0.0 18.7 %copy-start = (bf16[256,384]{1,0:T(8,128)(2,1)S(1)}, bf16[256,384]{1,0:T(8,128)(2,1)}, u32[]{:S(2)}) copy-start(bf16[256,384]{1,0:T(8,128)(2,1)} %param.6) | copy-start | bytes 589828
  2.6 17.8 %all-to-all-start = ((bf16[8,8,3,128]{3,1,2,0:T(8,128)(2,1)}), bf16[8,8,3,128]{3,1,2,0:T(8,128)(2,1)S(1)}, u32[]{:S(2)}, u32[]{:S(2)}) async-start(bf16[8,8,3,128]{3,1,2,0:T(8,128)(2,1)} %broadcast_in_dim.94), calls=%async_computation | async-start | bytes 98304 | tf_op jit(solution)/shard_map/all_to_all | solution.py:122
  10.4 49.4 %collective-permute-start.3 = (bf16[32,3,128]{2,0,1:T(8,128)(2,1)S(1)}, bf16[32,3,128]{2,0,1:T(8,128)(2,1)S(1)}, u32[]{:S(2)}, u32[]{:S(2)}) collective-permute-start(bf16[32,3,128]{2,0,1:T(8,128)(2,1)S(1)} %convert_bitcast_fusion), channel_id=1, source_target_pairs={{128,0},{136,8},{144,16},{152,24},{160,32},{168,40},{176,48},{184,... | collective-permute-start | bytes 73736 | tf_op jit(solution)/shard_map/ppermute | solution.py:166
  61.3 19.6 %collective-permute-start = (bf16[256,2,3,128]{3,0,2,1:T(8,128)(2,1)S(1)}, bf16[256,2,3,128]{3,0,2,1:T(8,128)(2,1)S(1)}, u32[]{:S(2)}, u32[]{:S(2)}) collective-permute-start(bf16[256,2,3,128]{3,0,2,1:T(8,128)(2,1)S(1)} %pad_maximum_fusion), channel_id=1, source_target_pairs={{0,24},{32,56},{64,88},{96,120},{128,152},{160,184},{192,216},{224... | collective-permute-start | bytes 1179656 | tf_op jit(solution)/shard_map/ppermute | solution.py:134
  62.0 18.9 %collective-permute-start.1 = (bf16[256,2,3,128]{3,0,2,1:T(8,128)(2,1)S(1)}, bf16[256,2,3,128]{3,0,2,1:T(8,128)(2,1)S(1)}, u32[]{:S(2)}, u32[]{:S(2)}) collective-permute-start(bf16[256,2,3,128]{3,0,2,1:T(8,128)(2,1)S(1)} %pad_maximum_fusion), channel_id=1, source_target_pairs={{0,16},{8,24},{32,48},{40,56},{64,80},{72,88},{96,112},{104,120},{... | collective-permute-start | bytes 1179656 | tf_op jit(solution)/shard_map/ppermute | solution.py:134
  63.3 36.6 %collective-permute-start.2 = (bf16[256,2,3,128]{3,0,2,1:T(8,128)(2,1)S(1)}, bf16[256,2,3,128]{3,0,2,1:T(8,128)(2,1)S(1)}, u32[]{:S(2)}, u32[]{:S(2)}) collective-permute-start(bf16[256,2,3,128]{3,0,2,1:T(8,128)(2,1)S(1)} %pad_maximum_fusion), channel_id=1, source_target_pairs={{0,8},{8,16},{16,24},{32,40},{40,48},{48,56},{64,72},{72,80},{80,8... | collective-permute-start | bytes 1179656 | tf_op jit(solution)/shard_map/ppermute | solution.py:134
  65.7 9.5 %collective-permute-start.4 = (f32[32,3,129]{2,0,1:T(8,128)S(1)}, f32[32,3,129]{2,0,1:T(8,128)S(1)}, u32[]{:S(2)}, u32[]{:S(2)}) collective-permute-start(f32[32,3,129]{2,0,1:T(8,128)S(1)} %pad_maximum_fusion.2), channel_id=1, source_target_pairs={{0,128},{8,136},{16,144},{24,152},{32,160},{40,168},{48,176},{56,1... | collective-permute-start | bytes 148616 | tf_op jit(solution)/shard_map/ppermute | solution.py:168
  67.7 11.9 %all-to-all-start.1 = ((f32[8,8,3,129]{3,1,2,0:T(8,128)}), f32[8,8,3,129]{3,1,2,0:T(8,128)S(1)}, u32[]{:S(2)}, u32[]{:S(2)}) async-start(f32[8,8,3,129]{3,1,2,0:T(8,128)} %pad_maximum_fusion.1), calls=%async_computation.1 | async-start | bytes 393216 | tf_op jit(solution)/shard_map/all_to_all | solution.py:181
  118.2 6.2 %collective-permute-start.5 = (bf16[4,256,384]{2,1,0:T(8,128)(2,1)S(1)}, bf16[4,256,384]{2,1,0:T(8,128)(2,1)S(1)}, u32[]{:S(2)}, u32[]{:S(2)}) collective-permute-start(bf16[4,256,384]{2,1,0:T(8,128)(2,1)S(1)} %all_to_all.15), channel_id=1, source_target_pairs={{0,1},{1,0},{2,3},{3,2},{4,5},{5,4},{6,7},{7,6},{8,9},{9,8},{10,11... | collective-permute-start | bytes 2359304 | tf_op jit(solution)/shard_map/ppermute | solution.py:205

commit v14 on v13

--- a/solution.py
+++ b/solution.py
@@ -126,8 +126,10 @@
     ring = lax.all_gather(payload, ROW_AXES)
 
     span0 = SEG_ROWS // row_count
-    chooser0, query0, pair0 = level_setup(query_all, key_all, value_all, level_offsets[0], 1)
-    pair0, ring = lax.optimization_barrier((pair0, ring))
+    query_late, key_late, value_late, ring = lax.optimization_barrier(
+        (query_all, key_all, value_all, ring)
+    )
+    chooser0, query0, pair0 = level_setup(query_late, key_late, value_late, level_offsets[0], 1)
     arrived = []
     for shift in range(span0 - 1, 0, -1):
         pairs = [(s, s + shift) for s in range(seq_count) if s % span0 + shift < span0]

time: 128 us -> 128 us (level)
  the two profiles are of different devices: /device:TPU:169 before, /device:TPU:1 now
where the time goes in v14:
time: 128 us; the launch traced here: 127 us
  blocking collectives  53.7 us (42%)
  starting transfers between devices  38.2 us (30%)
  matrix products  11.6 us (9%)
  local copies, waits for them, and re-layouts  9.24 us (7%)
  waiting for transfers between devices  7.98 us (6%)
  other arithmetic  5.6 us (4%)
    all_gather x1, blocking collectives, local(): ring = lax.all_gather(payload, ROW_AXES)  41.6 us
    ppermute x1, starting transfers between devices, local(): other_core = lax.ppermute(same_core, 'hc', [(0, 1), (1, 0)])  13.3 us
    all_to_all x1, blocking collectives, local(): same_core = lax.all_to_all(copies, 'hx', 0, 0, tiled=True)  12.1 us
    all_to_all x1, waiting for transfers between devices, local(): returned = lax.all_to_all(packed, 'sy', 0, 0, tiled=True)  7.97 us
    all_to_all x1, starting transfers between devices, local(): column_queries = lax.all_to_all(copies, 'sy', 0, 0, tiled=True)  7.65 us
    all_to_all x1, starting transfers between devices, local(): returned = lax.all_to_all(packed, 'sy', 0, 0, tiled=True)  6.82 us
    ppermute x3, starting transfers between devices, local(): arrived.append(lax.ppermute(pair0, SEQ_AXES, pairs))  5.31 us
    ppermute x1, starting transfers between devices, local(): lax.ppermute(pack(*whole_row(visiting1, row1, count1)), SEQ_AXES, down)  3.83 us
  transfers between devices with their start and end apart: 8, of which 1 were waited for; matrix products, arithmetic and copies ran while one was open for 11% of the time, Pallas kernels for 0%

profile of v14, /device:TPU:1, one launch (start us, length us, event | category | flops | bytes accessed | tf_op | source)
XLA Modules:
  0.0 127.0 jit_solution(17701290021546593989)
XLA Ops:
  0.0 0.8 fusion.81
  0.8 1.0 reshape_reshape.22
  2.0 0.6 broadcast_in_dim.94
  2.6 7.7 %all-to-all-start = ((bf16[8,8,3,128]{3,1,2,0:T(8,128)(2,1)}), bf16[8,8,3,128]{3,1,2,0:T(8,128)(2,1)S(1)}, u32[]{:S(2)}, u32[]{:S(2)}) async-start(bf16[8,8,3,128]{3,1,2,0:T(8,128)(2,1)} %broadcast_in_dim.94), calls=%async_computation | async-start | bytes 98304 | tf_op jit(solution)/shard_map/all_to_all | solution.py:122
  10.3 1.1 fusion.27
  11.5 1.3 %collective-permute-start.3 = (bf16[32,3,128]{2,0,1:T(8,128)(2,1)S(1)}, bf16[32,3,128]{2,0,1:T(8,128)(2,1)S(1)}, u32[]{:S(2)}, u32[]{:S(2)}) collective-permute-start(bf16[32,3,128]{2,0,1:T(8,128)(2,1)S(1)} %convert_bitcast_fusion), channel_id=1, source_target_pairs={{128,0},{136,8},{144,16},{152,24},{160,32},{168,40},{176,48},{184,... | collective-permute-start | bytes 73736 | tf_op jit(solution)/shard_map/ppermute | solution.py:168
  12.8 1.1 copy.55
  13.8 1.1 copy.57
  14.9 1.0 reshape_reshape.21
  15.9 1.1 copy.56
  17.0 1.0 reshape_reshape.20
  18.0 0.2 fusion.35
  18.2 0.2 fusion.37
  19.0 0.2 fusion.25
  19.3 41.6 %all-gather = bf16[640,2,3,128]{3,0,2,1:T(8,128)(2,1)S(1)} all-gather(bf16[40,2,3,128]{3,0,2,1:T(8,128)(2,1)S(1)} %maximum_maximum_fusion.1), channel_id=2, replica_groups=mesh['sy'=8,'sz'=16,'hx'=4,'hc'=2] {'sz'}, dimensions={0}, use_global_device_ids=true | all-gather | bytes 1044480 | tf_op jit(solution)/shard_map/all_gather | solution.py:126
  61.0 0.3 fusion.98
  61.3 0.2 fusion.47
  61.5 0.2 convolution_bitcast_fusion
  61.7 0.2 fusion.99
  61.9 0.2 fusion.60
  62.1 0.2 convolution_bitcast_fusion.3
  62.4 0.3 fusion.100
  62.8 0.2 fusion.40
  63.0 0.2 convolution_bitcast_fusion.2
  63.2 0.3 fusion.101
  63.5 0.2 fusion.39
  63.7 0.2 convolution_bitcast_fusion.1
  64.0 0.2 copy.59
  64.2 0.2 copy.58
  64.3 0.8 pad_maximum_fusion
  65.1 1.3 %collective-permute-start.2 = (bf16[256,2,3,128]{3,0,2,1:T(8,128)(2,1)}, bf16[256,2,3,128]{3,0,2,1:T(8,128)(2,1)S(1)}, u32[]{:S(2)}, u32[]{:S(2)}) collective-permute-start(bf16[256,2,3,128]{3,0,2,1:T(8,128)(2,1)} %pad_maximum_fusion), channel_id=1, source_target_pairs={{0,8},{8,16},{16,24},{32,40},{40,48},{48,56},{64,72},{72,80},{80,8... | collective-permute-start | bytes 1179656 | tf_op jit(solution)/shard_map/ppermute | solution.py:136
  66.4 2.7 %collective-permute-start.1 = (bf16[256,2,3,128]{3,0,2,1:T(8,128)(2,1)}, bf16[256,2,3,128]{3,0,2,1:T(8,128)(2,1)S(1)}, u32[]{:S(2)}, u32[]{:S(2)}) collective-permute-start(bf16[256,2,3,128]{3,0,2,1:T(8,128)(2,1)} %pad_maximum_fusion), channel_id=1, source_target_pairs={{0,16},{8,24},{32,48},{40,56},{64,80},{72,88},{96,112},{104,120},{... | collective-permute-start | bytes 1179656 | tf_op jit(solution)/shard_map/ppermute | solution.py:136
  69.1 1.3 %collective-permute-start = (bf16[256,2,3,128]{3,0,2,1:T(8,128)(2,1)}, bf16[256,2,3,128]{3,0,2,1:T(8,128)(2,1)S(1)}, u32[]{:S(2)}, u32[]{:S(2)}) collective-permute-start(bf16[256,2,3,128]{3,0,2,1:T(8,128)(2,1)} %pad_maximum_fusion), channel_id=1, source_target_pairs={{0,24},{32,56},{64,88},{96,120},{128,152},{160,184},{192,216},{224... | collective-permute-start | bytes 1179656 | tf_op jit(solution)/shard_map/ppermute | solution.py:136
  70.5 0.2 copy.65
  70.9 3.8 %collective-permute-start.4 = (f32[32,3,129]{2,0,1:T(8,128)S(1)}, f32[32,3,129]{2,0,1:T(8,128)S(1)}, u32[]{:S(2)}, u32[]{:S(2)}) collective-permute-start(f32[32,3,129]{2,0,1:T(8,128)S(1)} %pad_maximum_fusion.2), channel_id=1, source_target_pairs={{0,128},{8,136},{16,144},{24,152},{32,160},{40,168},{48,176},{56,1... | collective-permute-start | bytes 148616 | tf_op jit(solution)/shard_map/ppermute | solution.py:170
  74.7 0.7 pad_maximum_fusion.1
  75.4 6.8 %all-to-all-start.1 = ((f32[8,8,3,129]{3,1,2,0:T(8,128)}), f32[8,8,3,129]{3,1,2,0:T(8,128)S(1)}, u32[]{:S(2)}, u32[]{:S(2)}) async-start(f32[8,8,3,129]{3,1,2,0:T(8,128)} %pad_maximum_fusion.1), calls=%async_computation.1 | async-start | bytes 393216 | tf_op jit(solution)/shard_map/all_to_all | solution.py:183
  82.9 0.2 copy.69
  83.1 8.0 %all-to-all-done.1 = f32[8,8,3,129]{3,1,2,0:T(8,128)S(1)} async-done(((f32[8,8,3,129]{3,1,2,0:T(8,128)}), f32[8,8,3,129]{3,1,2,0:T(8,128)S(1)}, u32[]{:S(2)}, u32[]{:S(2)}) %all-to-all-start.1) | async-done | bytes 99104 | tf_op jit(solution)/shard_map/all_to_all | solution.py:183
  91.1 0.2 copy.95
  92.2 0.2 copy.74
  92.5 0.9 fusion
  93.4 0.9 fusion.1
  94.3 1.3 %fusion.21 = f32[1,256,3,128]{1,3,2,0:T(8,128)S(1)} fusion(f32[3,256,1024]{2,1,0:T(8,128)S(1)} %get-tuple-element.42, f32[3,256]{1,0:T(4,128)S(1)} %fusion.1, f32[3,256]{1,0:T(4,128)S(1)} %get-tuple-element.41, pred[256,1024]{1,0:T(8,128)(4,1)S(1)} %fusion.25, bf16[1024,2,3,128]{3,0,2,1:T(8,128)(2,1)S(1)} %maximum_maximum_fusion), kind=kOutput, calls=%fused_computation.17 | convolution fusion | flops 205258752 | bytes 4595712 | tf_op jit(solution)/shard_map/hqk,khd->qhd/dot_general | solution.py:35
  96.1 12.1 %all_to_all.15 = bf16[4,256,384]{2,1,0:T(8,128)(2,1)S(1)} all-to-all(bf16[4,256,384]{2,1,0:T(8,128)(2,1)S(1)} %broadcast_in_dim.163), channel_id=1, replica_groups=mesh['sy'=8,'sz'=16,'hx'=4,'hc'=2] {'hx'}, dimensions={0} | all-to-all | bytes 1572864 | tf_op jit(solution)/shard_map/all_to_all | solution.py:206
  108.2 13.3 %collective-permute-start.5 = (bf16[4,256,384]{2,1,0:T(8,128)(2,1)S(1)}, bf16[4,256,384]{2,1,0:T(8,128)(2,1)S(1)}, u32[]{:S(2)}, u32[]{:S(2)}) collective-permute-start(bf16[4,256,384]{2,1,0:T(8,128)(2,1)S(1)} %all_to_all.15), channel_id=1, source_target_pairs={{0,1},{1,0},{2,3},{3,2},{4,5},{5,4},{6,7},{7,6},{8,9},{9,8},{10,11... | collective-permute-start | bytes 2359304 | tf_op jit(solution)/shard_map/ppermute | solution.py:207
  121.6 2.3 %fusion.9 = f32[256,640]{1,0:T(8,128)S(1)} fusion(bf16[4,256,384]{2,1,0:T(8,128)(2,1)S(1)} %all_to_all.15, bf16[4,2,384,640]{3,2,1,0:T(8,128)(2,1)} %bitcast.209, s32[]{:T(128)S(6)} %select_n.210), kind=kOutput, calls=%fused_computation.13 | convolution fusion | flops 503316480 | bytes 3407876 | tf_op jit(solution)/shard_map/xtr,xro->to/dot_general | solution.py:212
  123.9 3.1 %fusion.18 = bf16[256,640]{1,0:T(8,128)(2,1)} fusion(f32[256,640]{1,0:T(8,128)S(1)} %fusion.9, bf16[4,256,384]{2,1,0:T(8,128)(2,1)S(1)} %collective-permute-done.5, bf16[4,2,384,640]{3,2,1,0:T(8,128)(2,1)} %bitcast.210, s32[]{:T(128)S(6)} %select_n.211), kind=kOutput, calls=%fused_computation.16 | convolution fusion | flops 503644160 | bytes 3735556 | tf_op jit(solution)/shard_map/xtr,xro->to/dot_general | solution.py:214
  (83 shorter events, 3.3 us)
Async XLA Ops:
  0.0 18.0 %copy-start = (bf16[256,384]{1,0:T(8,128)(2,1)S(1)}, bf16[256,384]{1,0:T(8,128)(2,1)}, u32[]{:S(2)}) copy-start(bf16[256,384]{1,0:T(8,128)(2,1)} %param.7) | copy-start | bytes 589828
  0.0 18.2 %copy-start.1 = (bf16[256,384]{1,0:T(8,128)(2,1)S(1)}, bf16[256,384]{1,0:T(8,128)(2,1)}, u32[]{:S(2)}) copy-start(bf16[256,384]{1,0:T(8,128)(2,1)} %param.6) | copy-start | bytes 589828
  2.6 16.7 %all-to-all-start = ((bf16[8,8,3,128]{3,1,2,0:T(8,128)(2,1)}), bf16[8,8,3,128]{3,1,2,0:T(8,128)(2,1)S(1)}, u32[]{:S(2)}, u32[]{:S(2)}) async-start(bf16[8,8,3,128]{3,1,2,0:T(8,128)(2,1)} %broadcast_in_dim.94), calls=%async_computation | async-start | bytes 98304 | tf_op jit(solution)/shard_map/all_to_all | solution.py:122
  11.5 50.9 %collective-permute-start.3 = (bf16[32,3,128]{2,0,1:T(8,128)(2,1)S(1)}, bf16[32,3,128]{2,0,1:T(8,128)(2,1)S(1)}, u32[]{:S(2)}, u32[]{:S(2)}) collective-permute-start(bf16[32,3,128]{2,0,1:T(8,128)(2,1)S(1)} %convert_bitcast_fusion), channel_id=1, source_target_pairs={{128,0},{136,8},{144,16},{152,24},{160,32},{168,40},{176,48},{184,... | collective-permute-start | bytes 73736 | tf_op jit(solution)/shard_map/ppermute | solution.py:168
  65.1 27.3 %collective-permute-start.2 = (bf16[256,2,3,128]{3,0,2,1:T(8,128)(2,1)}, bf16[256,2,3,128]{3,0,2,1:T(8,128)(2,1)S(1)}, u32[]{:S(2)}, u32[]{:S(2)}) collective-permute-start(bf16[256,2,3,128]{3,0,2,1:T(8,128)(2,1)} %pad_maximum_fusion), channel_id=1, source_target_pairs={{0,8},{8,16},{16,24},{32,40},{40,48},{48,56},{64,72},{72,80},{80,8... | collective-permute-start | bytes 1179656 | tf_op jit(solution)/shard_map/ppermute | solution.py:136
  66.4 26.0 %collective-permute-start.1 = (bf16[256,2,3,128]{3,0,2,1:T(8,128)(2,1)}, bf16[256,2,3,128]{3,0,2,1:T(8,128)(2,1)S(1)}, u32[]{:S(2)}, u32[]{:S(2)}) collective-permute-start(bf16[256,2,3,128]{3,0,2,1:T(8,128)(2,1)} %pad_maximum_fusion), channel_id=1, source_target_pairs={{0,16},{8,24},{32,48},{40,56},{64,80},{72,88},{96,112},{104,120},{... | collective-permute-start | bytes 1179656 | tf_op jit(solution)/shard_map/ppermute | solution.py:136
  69.1 23.3 %collective-permute-start = (bf16[256,2,3,128]{3,0,2,1:T(8,128)(2,1)}, bf16[256,2,3,128]{3,0,2,1:T(8,128)(2,1)S(1)}, u32[]{:S(2)}, u32[]{:S(2)}) collective-permute-start(bf16[256,2,3,128]{3,0,2,1:T(8,128)(2,1)} %pad_maximum_fusion), channel_id=1, source_target_pairs={{0,24},{32,56},{64,88},{96,120},{128,152},{160,184},{192,216},{224... | collective-permute-start | bytes 1179656 | tf_op jit(solution)/shard_map/ppermute | solution.py:136
  70.9 11.4 %collective-permute-start.4 = (f32[32,3,129]{2,0,1:T(8,128)S(1)}, f32[32,3,129]{2,0,1:T(8,128)S(1)}, u32[]{:S(2)}, u32[]{:S(2)}) collective-permute-start(f32[32,3,129]{2,0,1:T(8,128)S(1)} %pad_maximum_fusion.2), channel_id=1, source_target_pairs={{0,128},{8,136},{16,144},{24,152},{32,160},{40,168},{48,176},{56,1... | collective-permute-start | bytes 148616 | tf_op jit(solution)/shard_map/ppermute | solution.py:170
  75.4 15.7 %all-to-all-start.1 = ((f32[8,8,3,129]{3,1,2,0:T(8,128)}), f32[8,8,3,129]{3,1,2,0:T(8,128)S(1)}, u32[]{:S(2)}, u32[]{:S(2)}) async-start(f32[8,8,3,129]{3,1,2,0:T(8,128)} %pad_maximum_fusion.1), calls=%async_computation.1 | async-start | bytes 393216 | tf_op jit(solution)/shard_map/all_to_all | solution.py:183
  108.2 15.7 %collective-permute-start.5 = (bf16[4,256,384]{2,1,0:T(8,128)(2,1)S(1)}, bf16[4,256,384]{2,1,0:T(8,128)(2,1)S(1)}, u32[]{:S(2)}, u32[]{:S(2)}) collective-permute-start(bf16[4,256,384]{2,1,0:T(8,128)(2,1)S(1)} %all_to_all.15), channel_id=1, source_target_pairs={{0,1},{1,0},{2,3},{3,2},{4,5},{5,4},{6,7},{7,6},{8,9},{9,8},{10,11... | collective-permute-start | bytes 2359304 | tf_op jit(solution)/shard_map/ppermute | solution.py:207
